TPU v7x, 128 devices: a whole 4x4x4 slice. The times are simulated.
128 devices in a mesh: sens: 8 (over y, core), tm: 16 (over z, x).
Axes of the slice: x: 4, y: 4, z: 4, core: 2. Of those that a mesh axis runs over, the one named last changes fastest.
Arguments:
- observations: bfloat16 [131072, 4096], P('sens', 'tm'), may hold values from -6 to 6
- loadings: float32 [131072, 128], P('sens'), may hold values from -6 to 6
- noise_var: float32 [131072], P('sens'), may hold values from 0.25 to 4
- decay: float32 [4096, 128], P('tm'), may hold values from 0.4 to 1
- tiles: int32 [12288, 2], replicated, may hold values from 0 to 1023, as said below
Outputs:
- new_loadings: float32 [131072, 128], P(('sens', 'tm'))
- new_noise: float32 [131072], P(('sens', 'tm'))
Inputs may be any that keep to these rules, and one draw needn't show every extreme that they name: `tiles`: every pair is a distinct tile; every sensor block appears in at least one pair; the second entry is below 16.
All inputs are finite; a program needn't handle non-finite values.
Results may differ from a plain program's by a relative error of at most 0.0059.
Values may be sent and summed in bfloat16 or wider, within the bound.
No kernel may reach another device: no remote copies, remote signals or barrier semaphores. Data moves between devices by JAX's collectives and lax.ppermute only.
A program may use at most 128 MiB of HBM per device.

v0:
```python
import jax
import jax.numpy as jnp
from jax import lax
from jax.sharding import PartitionSpec as P

BLOCK = 128


HIGH = lax.Precision.HIGHEST


def carried_in(part, axis, combine, identity, reverse):
    count = lax.axis_size(axis)
    place = lax.axis_index(axis)
    ahead = count - 1 - place if reverse else place
    gathered = jax.tree.map(lambda a: lax.all_gather(a, axis), part)
    state = jax.tree.map(lambda a, e: jnp.zeros_like(a) + jnp.asarray(e, a.dtype), part, identity)

    def one(step, state):
        source = count - 1 - step if reverse else step
        return combine(
            state, jax.tree.map(lambda a: lax.dynamic_index_in_dim(a, source, 0, False), gathered)
        )

    return lax.fori_loop(0, ahead, one, state)


def compose(before_seg, after_seg):
    return (before_seg[0] * after_seg[0], after_seg[0] * before_seg[1] + after_seg[1])


def prefix_rows(gains, values, position):
    inclusive = lax.associative_scan(compose, (gains, values), axis=0)
    shifted_gain = jnp.concatenate([jnp.ones_like(gains[:1]), inclusive[0][:-1]], 0)
    shifted_value = jnp.concatenate([jnp.zeros_like(values[:1]), inclusive[1][:-1]], 0)
    before_gain = lax.dynamic_index_in_dim(shifted_gain, position, 0, keepdims=True)
    before_value = lax.dynamic_index_in_dim(shifted_value, position, 0, keepdims=True)
    return ((before_gain, before_value), (inclusive[0][-1:], inclusive[1][-1:]))


def per_device(observations, loadings, noise_var, decay, tiles):
    sens_count = lax.axis_size("sens")
    time_count = lax.axis_size("tm")
    sens_index = lax.axis_index("sens")
    time_index = lax.axis_index("tm")
    sens_dev, window_len = observations.shape
    factors = loadings.shape[1]
    blocks_dev = sens_dev // BLOCK
    blocks_share = blocks_dev // time_count
    segment_len = window_len // sens_count
    block_ids = sens_index * blocks_dev + jnp.arange(blocks_dev)
    block_hit = (tiles[:, 0][:, None] == block_ids[None, :]).astype(jnp.float32)
    window_hit = (tiles[:, 1][:, None] == jnp.arange(time_count)[None, :]).astype(jnp.float32)
    tile_mask = jnp.dot(block_hit.T, window_hit, precision=HIGH)
    present = lax.dynamic_index_in_dim(tile_mask, time_index, 1, keepdims=False)
    sensor_mask = jnp.repeat(present, BLOCK)
    weighted = loadings / noise_var[:, None] * sensor_mask[:, None]
    scaled = weighted.astype(jnp.bfloat16)
    info_part = lax.dot_general(
        observations, scaled, (((0,), (0,)), ((), ())), preferred_element_type=jnp.float32
    )
    gram_part = jnp.dot(weighted.T, loadings, precision=HIGH)
    info_vec = lax.psum_scatter(info_part, "sens", scatter_dimension=0, tiled=True)
    information = lax.psum(gram_part, "sens")
    identity = jnp.eye(factors, dtype=jnp.float32)
    lower = jnp.linalg.cholesky(identity + information)
    covariance = jax.scipy.linalg.cho_solve((lower, True), identity)
    local_est = jnp.dot(info_vec, covariance, precision=HIGH)
    decays = lax.dynamic_slice_in_dim(decay, sens_index * segment_len, segment_len, 0)
    fwd_gain, fwd_local = lax.associative_scan(compose, (decays, local_est), axis=0)
    back_gain, back_local = lax.associative_scan(
        compose, (jnp.flip(decays, 0), jnp.flip(local_est, 0)), axis=0
    )
    members = (
        lax.all_gather(fwd_gain[-1:], "sens", axis=0, tiled=True),
        lax.all_gather(fwd_local[-1:], "sens", axis=0, tiled=True),
        lax.all_gather(back_gain[-1:], "sens", axis=0, tiled=True),
        lax.all_gather(back_local[-1:], "sens", axis=0, tiled=True),
    )
    back_gain = jnp.flip(back_gain, 0)
    back_local = jnp.flip(back_local, 0)
    sens_fwd, group_fwd = prefix_rows(members[0], members[1], sens_index)
    sens_back, group_back = prefix_rows(
        jnp.flip(members[2], 0), jnp.flip(members[3], 0), sens_count - 1 - sens_index
    )
    time_fwd = carried_in(
        (group_fwd[0], group_fwd[1]),
        "tm",
        compose,
        (jnp.ones_like(group_fwd[0]), jnp.zeros_like(group_fwd[1])),
        False,
    )
    time_back = carried_in(
        (group_back[0], group_back[1]),
        "tm",
        compose,
        (jnp.ones_like(group_back[0]), jnp.zeros_like(group_back[1])),
        True,
    )
    enter_fwd = compose(time_fwd, sens_fwd)[1]
    enter_back = compose(time_back, sens_back)[1]
    forward = fwd_local + fwd_gain * enter_fwd
    backward = back_local + back_gain * enter_back
    smoothed = ((1.0 - decays) / (1.0 + decays) * (forward + backward - local_est)).astype(
        jnp.bfloat16
    )
    mask_mine = lax.dynamic_slice_in_dim(tile_mask, time_index * blocks_share, blocks_share, 0)
    observed = observations * sensor_mask.astype(jnp.bfloat16)[:, None]
    sums_sq = jnp.sum(jnp.square(observed.astype(jnp.float32)), axis=1)
    shard_rows = lax.all_gather(smoothed, "sens", axis=0, tiled=True)
    cross_terms = jnp.dot(observed, shard_rows, preferred_element_type=jnp.float32)
    squares = lax.dot_general(
        shard_rows, shard_rows, (((0,), (0,)), ((), ())), preferred_element_type=jnp.float32
    )
    cross_terms, squares = (cross_terms, squares)
    moment = squares + window_len * covariance
    cross_mine, sq_mine = (
        lax.psum_scatter(cross_terms, "tm", scatter_dimension=0, tiled=True),
        lax.psum_scatter(sums_sq, "tm", scatter_dimension=0, tiled=True),
    )
    all_moments = lax.all_gather(moment[None], "tm", axis=0, tiled=True)
    moment_mine = jnp.einsum("bw,wij->bij", mask_mine, all_moments, precision=HIGH)
    counts_mine = jnp.sum(mask_mine, axis=1)
    cross_blocks = cross_mine.reshape(blocks_share, BLOCK, factors)

    def solve_block(moment_block, cross_block):
        lower_block = jnp.linalg.cholesky(moment_block)
        return jax.scipy.linalg.cho_solve((lower_block, True), cross_block.T).T

    new_loadings = jax.vmap(solve_block)(moment_mine, cross_blocks).reshape(
        blocks_share * BLOCK, factors
    )
    explained = jnp.sum(new_loadings * cross_mine, axis=1)
    new_noise = (sq_mine - explained) / (window_len * jnp.repeat(counts_mine, BLOCK))
    return (new_loadings, new_noise)


def solution(mesh):
    return jax.shard_map(
        per_device,
        mesh=mesh,
        in_specs=(P("sens", "tm"), P("sens", None), P("sens"), P("tm", None), P()),
        out_specs=(P(("sens", "tm"), None), P(("sens", "tm"))),
        check_vma=False,
    )
```

profile of v0, /device:TPU:0, one launch (start us, length us, event | category | flops | bytes accessed | tf_op | source)
XLA Modules:
  0.0 492.3 jit_solution(8631777493236364026)
XLA Ops:
  7.2 1.1 fusion.43
  8.3 1.8 fusion.4
  10.2 25.4 %fusion.2 = f32[128,128]{1,0:T(8,128)} fusion(f32[16384,128]{1,0:T(8,128)} %param.10, f32[16384]{0:T(1024)S(1)} %broadcast_bitcast_fusion, f32[16384]{0:T(1024)} %param.11), kind=kOutput, calls=%fused_computation.8 | convolution fusion | flops 3225419776 | bytes 8585216 | tf_op jit(solution)/shard_map/dot_general | solution.py:62
  35.7 13.2 %fusion.13 = f32[256,128]{0,1:T(8,128)S(1)} fusion(bf16[16384,256]{1,0:T(8,128)(2,1)} %param.9, f32[16384,128]{1,0:T(8,128)} %param.10, f32[16384]{0:T(1024)S(1)} %broadcast_bitcast_fusion, f32[16384]{0:T(1024)S(1)} %copy-done.1), kind=kOutput, calls=%fused_computation.18 | convolution fusion | flops 1080033280 | bytes 17039360 | tf_op jit(solution)/shard_map/dot_general | solution.py:59
  48.9 0.8 copy.34
  49.7 0.2 all-gather.15.cloned.1.call-start
  49.9 0.7 constant_dynamic-slice_fusion.3
  50.7 0.7 constant_dynamic-slice_fusion.1
  51.4 46.6 %all-reduce.72.cloned.1.call-done = f32[128,128]{1,0:T(8,128)} async-done(((f32[128,128]{1,0:T(8,128)}), f32[128,128]{1,0:T(8,128)}) %all-reduce.72.cloned.1.call-update) | async-done | bytes 65552 | tf_op jit(solution)/shard_map/psum | solution.py:64
  98.0 0.9 convert_add_fusion
  99.0 0.9 fusion.29
  99.8 11.7 %cholesky.32 = f32[128,128]{1,0:T(8,128)S(1)} custom-call(f32[128,128]{1,0:T(8,128)S(1)} %fusion.29), custom_call_target="Cholesky" | custom-call | tf_op jit(solution)/shard_map/jit(cholesky)/cholesky | solution.py:66
  111.6 0.6 compare_reduce_fusion.1
  112.2 0.6 fusion.24
  112.8 9.8 %custom-call.21 = f32[1,128,128]{1,2,0:T(8,128)S(1)} custom-call(f32[1,128,128]{2,1,0:T(8,128)S(1)} %fusion.24), custom_call_target="InvertDiagBlocksLowerTriangular" | custom-call | tf_op jit(solution)/shard_map/jit(_cho_solve)/triangular_solve | solution.py:67
  122.6 0.2 fusion.27
  122.9 0.2 fusion.25
  123.1 7.7 %reduce-scatter.7.cloned.1.call-done = f32[32,128]{1,0:T(8,128)} async-done(((f32[256,128]{1,0:T(8,128)}), f32[32,128]{1,0:T(8,128)}) %reduce-scatter.7.cloned.1.call-update) | async-done | bytes 16400
  130.8 0.9 fusion.57
  133.0 7.8 %all-gather.9 = f32[8,1,128]{2,1,0:T(1,128)S(1)} all-gather(f32[1,1,128]{2,1,0:T(1,128)S(1)} %add_bitcast_fusion.1), channel_id=1, replica_groups=mesh['sens'=8,'tm'=16] {'sens'}, dimensions={0}, use_global_device_ids=true | all-gather | bytes 4608 | tf_op jit(solution)/shard_map/all_gather | solution.py:77
  140.9 9.8 %all-gather.11 = f32[8,1,128]{2,1,0:T(1,128)S(1)} all-gather(f32[1,1,128]{2,1,0:T(1,128)S(1)} %add_bitcast_fusion), channel_id=1, replica_groups=mesh['sens'=8,'tm'=16] {'sens'}, dimensions={0}, use_global_device_ids=true | all-gather | bytes 4608 | tf_op jit(solution)/shard_map/all_gather | solution.py:78
  151.4 8.1 %all-gather.5 = f32[8,1,128]{2,1,0:T(1,128)S(1)} all-gather(f32[1,1,128]{2,1,0:T(1,128)S(1)} %add_bitcast_fusion.3), channel_id=1, replica_groups=mesh['sens'=8,'tm'=16] {'sens'}, dimensions={0}, use_global_device_ids=true | all-gather | bytes 4608 | tf_op jit(solution)/shard_map/all_gather | solution.py:75
  159.7 9.5 %all-gather.7 = f32[8,1,128]{2,1,0:T(1,128)S(1)} all-gather(f32[1,1,128]{2,1,0:T(1,128)S(1)} %add_bitcast_fusion.2), channel_id=1, replica_groups=mesh['sens'=8,'tm'=16] {'sens'}, dimensions={0}, use_global_device_ids=true | all-gather | bytes 4608 | tf_op jit(solution)/shard_map/all_gather | solution.py:76
  169.7 20.8 %all-gather.10 = f32[16,1,128]{2,1,0:T(1,128)S(1)} all-gather(f32[1,1,128]{2,1,0:T(1,128)S(1)} %slice_bitcast_fusion.5), channel_id=4, replica_groups=mesh['sens'=8,'tm'=16] {'tm'}, dimensions={0}, use_global_device_ids=true | all-gather | bytes 8704 | tf_op jit(solution)/shard_map/all_gather | solution.py:16
  190.6 19.4 %all-gather.12 = f32[16,1,128]{2,1,0:T(1,128)S(1)} all-gather(f32[1,1,128]{2,1,0:T(1,128)S(1)} %slice_bitcast_fusion.4), channel_id=5, replica_groups=mesh['sens'=8,'tm'=16] {'tm'}, dimensions={0}, use_global_device_ids=true | all-gather | bytes 8704 | tf_op jit(solution)/shard_map/all_gather | solution.py:16
  210.0 0.5 while.27
  210.8 19.2 %all-gather.6 = f32[16,1,128]{2,1,0:T(1,128)S(1)} all-gather(f32[1,1,128]{2,1,0:T(1,128)S(1)} %slice_bitcast_fusion.7), channel_id=2, replica_groups=mesh['sens'=8,'tm'=16] {'tm'}, dimensions={0}, use_global_device_ids=true | all-gather | bytes 8704 | tf_op jit(solution)/shard_map/all_gather | solution.py:16
  230.0 19.4 %all-gather.8 = f32[16,1,128]{2,1,0:T(1,128)S(1)} all-gather(f32[1,1,128]{2,1,0:T(1,128)S(1)} %slice_bitcast_fusion.6), channel_id=3, replica_groups=mesh['sens'=8,'tm'=16] {'tm'}, dimensions={0}, use_global_device_ids=true | all-gather | bytes 8704 | tf_op jit(solution)/shard_map/all_gather | solution.py:16
  249.5 0.7 multiply_convert_fusion
  250.3 12.8 %all_gather.54 = bf16[256,128]{1,0:T(8,128)(2,1)S(1)} all-gather(bf16[32,128]{1,0:T(8,128)(2,1)S(1)} %multiply_convert_fusion), channel_id=1, replica_groups=mesh['sens'=8,'tm'=16] {'sens'}, dimensions={0}, use_global_device_ids=true | all-gather | bytes 73728 | tf_op jit(solution)/shard_map/all_gather | solution.py:110
  263.0 0.8 convolution_add_fusion
  264.0 6.8 %fusion = f32[16384,128]{1,0:T(8,128)} fusion(bf16[256,128]{1,0:T(8,128)(2,1)S(1)} %all_gather.54, bf16[16384,256]{1,0:T(8,128)(2,1)} %param.9, bf16[16384]{0:T(1024)(128)(2,1)S(1)} %bitcast_convert_fusion), kind=kOutput, calls=%fused_computation.6 | convolution fusion | flops 1077936128 | bytes 16875520 | tf_op jit(solution)/shard_map/dot_general | solution.py:111
  270.9 0.3 all-reduce.74.cloned.1.call-start
  271.1 7.5 %multiply_reduce_fusion = f32[16384]{0:T(1024)} fusion(bf16[16384,256]{1,0:T(8,128)(2,1)} %param.9, bf16[16384]{0:T(1024)(128)(2,1)S(1)} %bitcast_convert_fusion), kind=kLoop, calls=%fused_computation.4 | loop fusion | flops 16760832 | bytes 8486912 | tf_op jit(solution)/shard_map/reduce_sum | solution.py:109
  278.7 0.1 dynamic-slice_reduce_fusion
  278.9 0.6 dynamic-slice
  280.1 24.2 %all-gather.15.cloned.1.call-done = f32[2048,128]{1,0:T(8,128)} async-done(((f32[128,128]{1,0:T(8,128)}), f32[2048,128]{1,0:T(8,128)}) %all-gather.15.cloned.1.call-update) | async-done | bytes 1048592 | tf_op jit(solution)/shard_map/all_gather | solution.py:121
  304.2 2.4 fusion.16
  306.7 0.2 copy.24
  306.9 0.1 fusion.22
  307.1 93.8 %custom-call.22 = f32[8,128,128]{2,1,0:T(8,128)S(1)} custom-call(f32[8,128,128]{2,1,0:T(8,128)S(1)} %fusion.22), custom_call_target="Cholesky" | custom-call | tf_op jit(solution)/shard_map/vmap(jit(cholesky))/cholesky | solution.py:127
  400.9 0.1 compare_reduce_fusion
  401.0 0.1 select_bitcast_fusion
  401.2 78.6 %custom-call.23 = f32[8,1,128,128]{2,3,1,0:T(8,128)S(1)} custom-call(f32[8,1,128,128]{3,2,1,0:T(8,128)S(1)} %select_bitcast_fusion), custom_call_target="InvertDiagBlocksLowerTriangular" | custom-call | tf_op jit(solution)/shard_map/vmap(jit(_cho_solve))/triangular_solve | solution.py:128
  479.8 1.6 fusion.20
  481.5 1.2 fusion.18
  482.7 1.4 multiply_reduce_fusion.1
  484.2 1.3 fusion.34
  (269 shorter events, 3.3 us)
Async XLA Ops:
  7.2 90.9 %all-reduce.72.cloned.1.call-start = ((), (), s32[]{:S(2)}) async-start(), calls=%async_computation.2 | async-start | bytes 131072 | tf_op jit(solution)/shard_map/psum | solution.py:64
  10.2 25.5 %copy-start.1 = (f32[16384]{0:T(1024)S(1)}, f32[16384]{0:T(1024)}, u32[]{:S(2)}) copy-start(f32[16384]{0:T(1024)} %param.11) | copy-start | bytes 196612
  35.6 95.2 %reduce-scatter.7.cloned.1.call-start = ((), (), s32[]{:S(2)}) async-start(), calls=%async_computation.5 | async-start | bytes 147456
  49.7 254.6 %all-gather.15.cloned.1.call-start = ((), (), s32[]{:S(2)}) async-start(), calls=%async_computation.4 | async-start | bytes 1114112 | tf_op jit(solution)/shard_map/all_gather | solution.py:121
  263.9 215.9 %reduce-scatter.5.cloned.1.call-start = ((), (), s32[]{:S(2)}) async-start(), calls=%async_computation.3 | async-start | bytes 8912896 | tf_op jit(solution)/shard_map/reduce_scatter | solution.py:118
  270.9 8.0 %copy-start.2 = (u32[128]{0:T(128)S(1)}, u32[128]{0:T(128)}, u32[]{:S(2)}) copy-start(u32[128]{0:T(128)} %constant.324) | copy-start | bytes 1540
  270.9 213.3 %all-reduce.74.cloned.1.call-start = ((), (), s32[]{:S(2)}) async-start(), calls=%async_computation.6 | async-start | bytes 131072
  482.7 2.8 copy-start
Sparse Core Ops, SparseCore 0:
  35.7 62.2 all-reduce.71
  100.9 29.7 reduce-scatter.6
  264.0 40.1 all-gather.14
  307.5 85.3 reduce-scatter.4
  395.9 82.6 all-reduce.73
where the time goes:
time: 502 us; the launch traced here: 492 us
  other arithmetic  209 us (42%)
  blocking collectives  127 us (25%)
  waiting for transfers between devices  78.6 us (16%)
  matrix products  54.7 us (11%)
  between operations  15.7 us (3%)
  local copies, waits for them, and re-layouts  6.16 us (1%)
    another operation x4, other arithmetic, solve_block(): lower_block = jnp.linalg.cholesky(moment_block)  94 us
    all_gather x4, blocking collectives, carried_in(): gathered = jax.tree.map(lambda a: lax.all_gather(a, axis), part)  78.9 us
    another operation x3, other arithmetic, solve_block(): return jax.scipy.linalg.cho_solve((lower_block, True), cross_block.T).T  78.7 us
    psum x1, waiting for transfers between devices, per_device(): information = lax.psum(gram_part, 'sens')  46.6 us
    dot_general x1, matrix products, per_device(): gram_part = jnp.dot(weighted.T, loadings, precision=HIGH)  25.4 us
    all_gather x1, waiting for transfers between devices, per_device(): all_moments = lax.all_gather(moment[None], 'tm', axis=0, tiled=True)  24.2 us
    dot_general x1, matrix products, per_device(): lax.dot_general(observations, scaled, (((0,), (0,)), ((), ())), preferred...  13.2 us
    all_gather x1, blocking collectives, per_device(): shard_rows = lax.all_gather(smoothed, 'sens', axis=0, tiled=True)  12.8 us
  transfers between devices with their start and end apart: 5, of which 3 were waited for; matrix products, arithmetic and copies ran while one was open for 48% of the time, Pallas kernels for 0%

commit v1 on v0

v1 whole, which is shorter than its diff:
```python
import jax
import jax.numpy as jnp
from jax import lax
from jax.sharding import PartitionSpec as P

BLOCK = 128


HIGH = lax.Precision.HIGHEST


def compose(before_seg, after_seg):
    return (before_seg[0] * after_seg[0], after_seg[0] * before_seg[1] + after_seg[1])


def entering(gains, values, position):
    inclusive = lax.associative_scan(compose, (gains, values), axis=0)
    shifted_value = jnp.concatenate([jnp.zeros_like(values[:1]), inclusive[1][:-1]], 0)
    return lax.dynamic_index_in_dim(shifted_value, position, 0, keepdims=True)


def per_device(observations, loadings, noise_var, decay, tiles):
    sens_count = lax.axis_size("sens")
    time_count = lax.axis_size("tm")
    sens_index = lax.axis_index("sens")
    time_index = lax.axis_index("tm")
    sens_dev, window_len = observations.shape
    factors = loadings.shape[1]
    blocks_dev = sens_dev // BLOCK
    blocks_share = blocks_dev // time_count
    block_ids = sens_index * blocks_dev + jnp.arange(blocks_dev)
    block_hit = (tiles[:, 0][:, None] == block_ids[None, :]).astype(jnp.float32)
    window_hit = (tiles[:, 1][:, None] == jnp.arange(time_count)[None, :]).astype(jnp.float32)
    tile_mask = jnp.dot(block_hit.T, window_hit, precision=HIGH)
    present = lax.dynamic_index_in_dim(tile_mask, time_index, 1, keepdims=False)
    sensor_mask = jnp.repeat(present, BLOCK)
    weighted = loadings / noise_var[:, None] * sensor_mask[:, None]
    scaled = weighted.astype(jnp.bfloat16)
    info_part = lax.dot_general(
        observations, scaled, (((0,), (0,)), ((), ())), preferred_element_type=jnp.float32
    )
    gram_part = lax.dot_general(
        weighted, loadings, (((0,), (0,)), ((), ())), precision=lax.Precision.HIGH,
        preferred_element_type=jnp.float32,
    )
    summed = lax.psum(jnp.concatenate([info_part, gram_part], 0), "sens")
    info_vec = summed[:window_len]
    information = summed[window_len:]
    identity = jnp.eye(factors, dtype=jnp.float32)
    lower = jnp.linalg.cholesky(identity + information)
    covariance = jax.scipy.linalg.cho_solve((lower, True), identity)
    local_est = jnp.dot(info_vec, covariance, precision=HIGH)
    fwd_gain, fwd_local = lax.associative_scan(compose, (decay, local_est), axis=0)
    back_gain, back_local = lax.associative_scan(
        compose, (jnp.flip(decay, 0), jnp.flip(local_est, 0)), axis=0
    )
    summary = jnp.concatenate(
        [fwd_gain[-1:], fwd_local[-1:], back_gain[-1:], back_local[-1:]], 0
    )
    windows = lax.all_gather(summary, "tm", axis=0, tiled=False)
    enter_fwd = entering(windows[:, 0], windows[:, 1], time_index)
    enter_back = entering(
        jnp.flip(windows[:, 2], 0), jnp.flip(windows[:, 3], 0), time_count - 1 - time_index
    )
    back_gain = jnp.flip(back_gain, 0)
    back_local = jnp.flip(back_local, 0)
    forward = fwd_local + fwd_gain * enter_fwd
    backward = back_local + back_gain * enter_back
    smoothed = ((1.0 - decay) / (1.0 + decay) * (forward + backward - local_est)).astype(
        jnp.bfloat16
    )
    mask_mine = lax.dynamic_slice_in_dim(tile_mask, time_index * blocks_share, blocks_share, 0)
    observed = observations * sensor_mask.astype(jnp.bfloat16)[:, None]
    sums_sq = jnp.sum(jnp.square(observed.astype(jnp.float32)), axis=1)
    cross_terms = jnp.dot(observed, smoothed, preferred_element_type=jnp.float32)
    squares = lax.dot_general(
        smoothed, smoothed, (((0,), (0,)), ((), ())), preferred_element_type=jnp.float32
    )
    moment = squares + window_len * covariance
    share = sens_dev // time_count
    cross_mine = lax.psum_scatter(cross_terms, "tm", scatter_dimension=0, tiled=True)
    sq_mine = lax.psum_scatter(
        sums_sq.reshape(-1, factors), "tm", scatter_dimension=0, tiled=True
    ).reshape(share)
    all_moments = lax.all_gather(moment, "tm", axis=0, tiled=False)
    moment_mine = jnp.einsum("bw,wij->bij", mask_mine, all_moments, precision=HIGH)
    counts_mine = jnp.sum(mask_mine, axis=1)
    cross_blocks = cross_mine.reshape(blocks_share, BLOCK, factors)

    def solve_block(moment_block, cross_block):
        lower_block = jnp.linalg.cholesky(moment_block)
        return jax.scipy.linalg.cho_solve((lower_block, True), cross_block.T).T

    new_loadings = jax.vmap(solve_block)(moment_mine, cross_blocks).reshape(
        blocks_share * BLOCK, factors
    )
    explained = jnp.sum(new_loadings * cross_mine, axis=1)
    new_noise = (sq_mine - explained) / (window_len * jnp.repeat(counts_mine, BLOCK))
    return (new_loadings, new_noise)


def solution(mesh):
    return jax.shard_map(
        per_device,
        mesh=mesh,
        in_specs=(P("sens", "tm"), P("sens", None), P("sens"), P("tm", None), P()),
        out_specs=(P(("sens", "tm"), None), P(("sens", "tm"))),
        check_vma=False,
    )
```

time: 502 us -> 387 us (0.77); the launches traced: 492 us -> 387 us
  blocking collectives: 127 us -> 23.6 us
  matrix products: 54.7 us -> 46 us
  waiting for transfers between devices: 78.6 us -> 85.9 us
    all_gather x9 -> x1, blocking collectives: 127 us -> 23.6 us  [per_device(): windows = lax.all_gather(summary, 'tm', axis=0, tiled=False)]
    psum x1, waiting for transfers between devices: 46.6 us -> 62.4 us  [per_device(): summed = lax.psum(jnp.concatenate([info_part, gram_part], 0), 'sens')]
    unnamed x7 -> x5, waiting for transfers between devices: 7.8 us -> 0.09 us
    dot_general x1, matrix products: 13.2 us -> 6.84 us  [per_device(): lax.dot_general(observations, scaled, (((0,), (0,)), ((), ())), preferred...]
  transfers between devices with their start and end apart: 5 -> 4, of which waited for: 3 -> 2; matrix products, arithmetic and copies ran while one was open for 48% -> 50% of each run, Pallas kernels for 0% -> 0%
where the time goes in v1:
time: 387 us
  other arithmetic  210 us (54%)
  waiting for transfers between devices  85.9 us (22%)
  matrix products  46 us (12%)
  blocking collectives  23.6 us (6%)
  between operations  16.3 us (4%)
  local copies, waits for them, and re-layouts  4.97 us (1%)
    another operation x4, other arithmetic, solve_block(): lower_block = jnp.linalg.cholesky(moment_block)  94 us
    another operation x3, other arithmetic, solve_block(): return jax.scipy.linalg.cho_solve((lower_block, True), cross_block.T).T  78.7 us
    psum x1, waiting for transfers between devices, per_device(): summed = lax.psum(jnp.concatenate([info_part, gram_part], 0), 'sens')  62.4 us
    all_gather x1, blocking collectives, per_device(): windows = lax.all_gather(summary, 'tm', axis=0, tiled=False)  23.6 us
    all_gather x1, waiting for transfers between devices, per_device(): all_moments = lax.all_gather(moment, 'tm', axis=0, tiled=False)  23.3 us
    dot_general x1, matrix products, per_device(): lax.dot_general(weighted, loadings, (((0,), (0,)), ((), ())), precision=l...  22.7 us
    another operation x3, other arithmetic, per_device(): lower = jnp.linalg.cholesky(identity + information)  12.4 us
    another operation x2, other arithmetic, per_device(): covariance = jax.scipy.linalg.cho_solve((lower, True), identity)  10.5 us
  transfers between devices with their start and end apart: 4, of which 2 were waited for; matrix products, arithmetic and copies ran while one was open for 50% of the time, Pallas kernels for 0%

profile of v1, /device:TPU:0, one launch (start us, length us, event | category | flops | bytes accessed | tf_op | source)
XLA Modules:
  0.0 387.0 jit_solution(15816338091799716416)
XLA Ops:
  7.2 0.0 all-reduce.86.cloned.1.call-start
  7.2 1.1 fusion.50
  8.3 1.8 fusion.4
  10.1 0.1 broadcast_bitcast_fusion
  10.2 22.7 %fusion.2 = f32[128,128]{1,0:T(8,128)S(1)} fusion(f32[16384,128]{1,0:T(8,128)} %param.6, f32[16384]{0:T(1024)S(1)} %broadcast_bitcast_fusion, f32[16384]{0:T(1024)} %param.7), kind=kOutput, calls=%fused_computation.4 | convolution fusion | flops 1614807040 | bytes 8585216 | tf_op jit(solution)/shard_map/dot_general | solution.py:42
  33.1 6.8 %fusion.13 = f32[256,128]{1,0:T(8,128)S(1)} fusion(bf16[16384,256]{1,0:T(8,128)(2,1)S(1)} %bitcast.76, f32[16384,128]{1,0:T(8,128)S(1)} %bitcast.96, f32[16384]{0:T(1024)S(1)} %broadcast_bitcast_fusion, f32[16384]{0:T(1024)S(1)} %copy-done.2), kind=kOutput, calls=%fused_computation.14 | convolution fusion | flops 1080033280 | bytes 17039360 | tf_op jit(solution)/shard_map/dot_general | solution.py:39
  39.9 0.7 pad_maximum_fusion
  40.6 0.0 all-reduce.86.cloned.1.call-update
  40.6 0.2 all-gather.5.cloned.1.call-start
  41.1 62.4 %all-reduce.86.cloned.1.call-done = f32[384,128]{1,0:T(8,128)} async-done(((f32[384,128]{1,0:T(8,128)}), f32[384,128]{1,0:T(8,128)}) %all-reduce.86.cloned.1.call-update) | async-done | bytes 196624 | tf_op jit(solution)/shard_map/psum | solution.py:46
  103.5 0.9 slice_add_fusion
  104.3 0.1 copy.26
  104.4 0.9 fusion.33
  105.3 11.7 %cholesky.32 = f32[128,128]{1,0:T(8,128)S(1)} custom-call(f32[128,128]{1,0:T(8,128)S(1)} %fusion.33), custom_call_target="Cholesky" | custom-call | tf_op jit(solution)/shard_map/jit(cholesky)/cholesky | solution.py:50
  117.0 0.6 compare_reduce_fusion.1
  117.7 0.7 fusion.26
  118.4 9.8 %custom-call.21 = f32[1,128,128]{1,2,0:T(8,128)S(1)} custom-call(f32[1,128,128]{2,1,0:T(8,128)S(1)} %fusion.26), custom_call_target="InvertDiagBlocksLowerTriangular" | custom-call | tf_op jit(solution)/shard_map/jit(_cho_solve)/triangular_solve | solution.py:51
  128.2 0.2 fusion.31
  128.4 0.2 fusion.29
  128.6 1.2 fusion.24
  133.6 23.6 %all-gather.2 = f32[16,4,128]{2,1,0:T(4,128)S(1)} all-gather(f32[1,4,128]{2,1,0:T(4,128)S(1)} %maximum_bitcast_fusion), channel_id=2, replica_groups=mesh['sens'=8,'tm'=16] {'tm'}, dimensions={0}, use_global_device_ids=true | all-gather | bytes 34816 | tf_op jit(solution)/shard_map/all_gather | solution.py:60
  158.0 0.1 rev.12
  158.1 0.1 rev.13
  158.6 0.1 multiply_convert_fusion
  158.7 0.8 convolution_add_fusion
  159.5 0.0 all-gather.5.cloned.1.call-update
  159.6 0.0 reduce-scatter.2.cloned.1.call-start
  159.6 0.1 bitcast_convert_fusion
  159.7 6.9 %fusion = f32[16384,128]{1,0:T(8,128)} fusion(bf16[256,128]{1,0:T(8,128)(2,1)S(1)} %multiply_convert_fusion, bf16[16384,256]{1,0:T(8,128)(2,1)} %param.5, bf16[16384]{0:T(1024)(128)(2,1)S(1)} %bitcast_convert_fusion), kind=kOutput, calls=%fused_computation.2 | convolution fusion | flops 1077936128 | bytes 16875520 | tf_op jit(solution)/shard_map/dot_general | solution.py:75
  166.6 0.3 all-reduce.88.cloned.1.call-start
  166.9 7.5 %multiply_reduce_fusion = f32[16384]{0:T(1024)} fusion(bf16[16384,256]{1,0:T(8,128)(2,1)} %param.5, bf16[16384]{0:T(1024)(128)(2,1)S(1)} %bitcast_convert_fusion), kind=kLoop, calls=%fused_computation | loop fusion | flops 16760832 | bytes 8486912 | tf_op jit(solution)/shard_map/reduce_sum | solution.py:74
  174.5 0.1 dynamic-slice_reduce_fusion
  174.6 0.6 dynamic-slice
  175.8 23.3 %all-gather.5.cloned.1.call-done = f32[2048,128]{1,0:T(8,128)} async-done(((f32[128,128]{1,0:T(8,128)}), f32[2048,128]{1,0:T(8,128)}) %all-gather.5.cloned.1.call-update) | async-done | bytes 1048592 | tf_op jit(solution)/shard_map/all_gather | solution.py:85
  199.2 2.4 fusion.16
  201.6 0.2 copy.31
  201.9 0.1 fusion.22
  202.0 93.8 %custom-call.22 = f32[8,128,128]{2,1,0:T(8,128)S(1)} custom-call(f32[8,128,128]{2,1,0:T(8,128)S(1)} %fusion.22), custom_call_target="Cholesky" | custom-call | tf_op jit(solution)/shard_map/vmap(jit(cholesky))/cholesky | solution.py:91
  295.8 0.1 select_reduce_fusion
  295.8 0.1 compare_reduce_fusion
  296.0 0.1 select_bitcast_fusion
  296.1 78.6 %custom-call.23 = f32[8,1,128,128]{2,3,1,0:T(8,128)S(1)} custom-call(f32[8,1,128,128]{3,2,1,0:T(8,128)S(1)} %select_bitcast_fusion), custom_call_target="InvertDiagBlocksLowerTriangular" | custom-call | tf_op jit(solution)/shard_map/vmap(jit(_cho_solve))/triangular_solve | solution.py:92
  374.7 0.0 reduce-scatter.2.cloned.1.call-done
  374.7 1.6 fusion.20
  376.4 1.2 fusion.18
  377.6 1.4 multiply_reduce_fusion.1
  379.1 0.0 all-reduce.88.cloned.1.call-done
  379.1 1.4 fusion.43
  (361 shorter events, 3.9 us)
Async XLA Ops:
  7.2 96.3 %all-reduce.86.cloned.1.call-start = ((), (), s32[]{:S(2)}) async-start(), calls=%async_computation.1 | async-start | bytes 393216 | tf_op jit(solution)/shard_map/psum | solution.py:46
  8.3 24.7 %slice-start = ((s8[8388608]{0:T(1024)(128)(4,1)}), s8[4194304]{0:T(1024)(128)(4,1)S(1)}, s32[]{:S(2)}) async-start(s8[8388608]{0:T(1024)(128)(4,1)} %bitcast.75), calls=%async_computation.5 | async-start | bytes 8388608
  8.3 24.7 %slice-start.2 = ((s8[8388608]{0:T(1024)(128)(4,1)}), s8[4194304]{0:T(1024)(128)(4,1)S(1)}, s32[]{:S(2)}) async-start(s8[8388608]{0:T(1024)(128)(4,1)} %bitcast.95), calls=%async_computation.7 | async-start | bytes 8388608
  10.2 22.8 %slice-start.1 = ((s8[8388608]{0:T(1024)(128)(4,1)}), s8[4194304]{0:T(1024)(128)(4,1)S(1)}, s32[]{:S(2)}) async-start(s8[8388608]{0:T(1024)(128)(4,1)} %bitcast.75), calls=%async_computation.6 | async-start | bytes 8388608
  10.2 22.8 %slice-start.3 = ((s8[8388608]{0:T(1024)(128)(4,1)}), s8[4194304]{0:T(1024)(128)(4,1)S(1)}, s32[]{:S(2)}) async-start(s8[8388608]{0:T(1024)(128)(4,1)} %bitcast.95), calls=%async_computation.8 | async-start | bytes 8388608
  10.2 22.8 %copy-start.2 = (f32[16384]{0:T(1024)S(1)}, f32[16384]{0:T(1024)}, u32[]{:S(2)}) copy-start(f32[16384]{0:T(1024)} %param.7) | copy-start | bytes 196612
  33.1 7.8 %copy-start.1 = (f32[256,128]{1,0:T(8,128)S(1)}, f32[256,128]{1,0:T(8,128)}, u32[]{:S(2)}) copy-start(f32[256,128]{1,0:T(8,128)} %param.8) | copy-start | bytes 393220
  40.6 158.5 %all-gather.5.cloned.1.call-start = ((), (), s32[]{:S(2)}) async-start(), calls=%async_computation.3 | async-start | bytes 1114112 | tf_op jit(solution)/shard_map/all_gather | solution.py:85
  159.6 215.2 %reduce-scatter.2.cloned.1.call-start = ((), (), s32[]{:S(2)}) async-start(), calls=%async_computation.2 | async-start | bytes 8912896 | tf_op jit(solution)/shard_map/reduce_scatter | solution.py:81
  166.6 8.0 %copy-start.3 = (u32[128]{0:T(128)S(1)}, u32[128]{0:T(128)}, u32[]{:S(2)}) copy-start(u32[128]{0:T(128)} %constant.299) | copy-start | bytes 1540
  166.6 212.4 %all-reduce.88.cloned.1.call-start = ((), (), s32[]{:S(2)}) async-start(), calls=%async_computation.4 | async-start | bytes 131072
  377.6 2.8 copy-start
Sparse Core Ops, SparseCore 0:
  40.8 62.6 all-reduce.85
  159.7 39.4 all-gather.4
  202.6 85.3 reduce-scatter.1
  291.1 82.1 all-reduce.87

commit v2 on v1

--- a/solution.py
+++ b/solution.py
@@ -1,6 +1,8 @@
 import jax
 import jax.numpy as jnp
 from jax import lax
+from jax.experimental import pallas as pl
+from jax.experimental.pallas import tpu as pltpu
 from jax.sharding import PartitionSpec as P
 
 BLOCK = 128
@@ -11,6 +13,37 @@
 
 def compose(before_seg, after_seg):
     return (before_seg[0] * after_seg[0], after_seg[0] * before_seg[1] + after_seg[1])
+
+
+def _gauss_jordan(a_ref, o_ref):
+    n = a_ref.shape[-1]
+    o_ref[...] = a_ref[...]
+    lane = lax.broadcasted_iota(jnp.int32, (1, 1, n), 2)
+    sub = lax.broadcasted_iota(jnp.int32, (1, n, 1), 1)
+
+    def step(k, carry):
+        a = o_ref[...]
+        colmask = lane == k
+        rowmask = sub == k
+        c = jnp.sum(jnp.where(colmask, a, 0.0), axis=2, keepdims=True)
+        r = jnp.sum(jnp.where(rowmask, a, 0.0), axis=1, keepdims=True)
+        p = jnp.sum(jnp.where(colmask, r, 0.0), axis=2, keepdims=True)
+        inv_p = 1.0 / p
+        rs = jnp.where(colmask, inv_p, r * inv_p)
+        out = jnp.where(colmask, -c * inv_p, a - c * rs)
+        o_ref[...] = jnp.where(rowmask, rs, out)
+        return carry
+
+    lax.fori_loop(0, n, step, 0)
+
+
+def spd_inverse(a):
+    return pl.pallas_call(
+        _gauss_jordan,
+        out_shape=jax.ShapeDtypeStruct(a.shape, jnp.float32),
+        in_specs=[pl.BlockSpec(memory_space=pltpu.VMEM)],
+        out_specs=pl.BlockSpec(memory_space=pltpu.VMEM),
+    )(a)
 
 
 def entering(gains, values, position):
@@ -39,16 +72,23 @@
     info_part = lax.dot_general(
         observations, scaled, (((0,), (0,)), ((), ())), preferred_element_type=jnp.float32
     )
-    gram_part = lax.dot_general(
-        weighted, loadings, (((0,), (0,)), ((), ())), precision=lax.Precision.HIGH,
+    weighted_lo = (weighted - scaled.astype(jnp.float32)).astype(jnp.bfloat16)
+    loadings_hi = loadings.astype(jnp.bfloat16)
+    loadings_lo = (loadings - loadings_hi.astype(jnp.float32)).astype(jnp.bfloat16)
+    split = lax.dot_general(
+        jnp.concatenate([scaled, weighted_lo], 1),
+        jnp.concatenate([loadings_hi, loadings_lo], 1),
+        (((0,), (0,)), ((), ())),
         preferred_element_type=jnp.float32,
+    )
+    gram_part = (
+        split[:factors, :factors] + split[:factors, factors:] + split[factors:, :factors]
     )
     summed = lax.psum(jnp.concatenate([info_part, gram_part], 0), "sens")
     info_vec = summed[:window_len]
     information = summed[window_len:]
     identity = jnp.eye(factors, dtype=jnp.float32)
-    lower = jnp.linalg.cholesky(identity + information)
-    covariance = jax.scipy.linalg.cho_solve((lower, True), identity)
+    covariance = spd_inverse((identity + information)[None])[0]
     local_est = jnp.dot(info_vec, covariance, precision=HIGH)
     fwd_gain, fwd_local = lax.associative_scan(compose, (decay, local_est), axis=0)
     back_gain, back_local = lax.associative_scan(
@@ -86,14 +126,10 @@
     moment_mine = jnp.einsum("bw,wij->bij", mask_mine, all_moments, precision=HIGH)
     counts_mine = jnp.sum(mask_mine, axis=1)
     cross_blocks = cross_mine.reshape(blocks_share, BLOCK, factors)
-
-    def solve_block(moment_block, cross_block):
-        lower_block = jnp.linalg.cholesky(moment_block)
-        return jax.scipy.linalg.cho_solve((lower_block, True), cross_block.T).T
-
-    new_loadings = jax.vmap(solve_block)(moment_mine, cross_blocks).reshape(
-        blocks_share * BLOCK, factors
-    )
+    inverse_mine = spd_inverse(moment_mine)
+    new_loadings = jnp.einsum(
+        "bsk,bjk->bsj", cross_blocks, inverse_mine, precision=HIGH
+    ).reshape(blocks_share * BLOCK, factors)
     explained = jnp.sum(new_loadings * cross_mine, axis=1)
     new_noise = (sq_mine - explained) / (window_len * jnp.repeat(counts_mine, BLOCK))
     return (new_loadings, new_noise)

time: 387 us -> 365 us (0.943)
  other arithmetic: 210 us -> 28.8 us
  waiting for transfers between devices: 85.9 us -> 214 us
  Pallas kernels: 0 us -> 54.7 us
  matrix products: 46 us -> 21.3 us
    another operation x12 -> x0, other arithmetic: 196 us -> none  [the longest x4 94 us: solve_block(): lower_block = jnp.linalg.cholesky(moment_block)]
    unnamed x5, waiting for transfers between devices: 0.09 us -> 80.5 us
    pallas_call x0 -> x2, Pallas kernels: none -> 54.7 us  [spd_inverse(): pl.pallas_call(_gauss_jordan, out_shape=jax.ShapeDtypeStruct(a.shape, jnp...]
    reduce_scatter x1, waiting for transfers between devices: 0.02 us -> 47.4 us  [per_device(): lax.psum_scatter(cross_terms, 'tm', scatter_dimension=0, tiled=True)]
    dot_general x1 -> x2, matrix products: 22.7 us -> 4.83 us  [the longest x1 2.43 us: per_device(): lax.dot_general(jnp.concatenate([scaled, weighted_lo], 1), jnp.concatenat...]
    convert_element_type x0 -> x1, other arithmetic: none -> 15.1 us  [per_device(): (loadings - loadings_hi.astype(jnp.float32)).astype(jnp.bfloat16)]
  transfers between devices with their start and end apart: 4 -> 4, of which waited for: 2 -> 4; matrix products, arithmetic and copies ran while one was open for 50% -> 6% of each run, Pallas kernels for 0% -> 10%
where the time goes in v2:
time: 365 us
  waiting for transfers between devices  214 us (59%)
  Pallas kernels  54.7 us (15%)
  other arithmetic  28.8 us (8%)
  blocking collectives  23.8 us (7%)
  matrix products  21.3 us (6%)
  between operations  16.2 us (4%)
  local copies, waits for them, and re-layouts  5.53 us (2%)
    unnamed x5, waiting for transfers between devices  80.5 us
    psum x1, waiting for transfers between devices, per_device(): summed = lax.psum(jnp.concatenate([info_part, gram_part], 0), 'sens')  62.6 us
    pallas_call x2, Pallas kernels, spd_inverse(): pl.pallas_call(_gauss_jordan, out_shape=jax.ShapeDtypeStruct(a.shape, jnp...  54.7 us
    reduce_scatter x1, waiting for transfers between devices, per_device(): lax.psum_scatter(cross_terms, 'tm', scatter_dimension=0, tiled=True)  47.4 us
    all_gather x1, blocking collectives, per_device(): windows = lax.all_gather(summary, 'tm', axis=0, tiled=False)  23.8 us
    all_gather x1, waiting for transfers between devices, per_device(): all_moments = lax.all_gather(moment, 'tm', axis=0, tiled=False)  23.6 us
    convert_element_type x1, other arithmetic, per_device(): (loadings - loadings_hi.astype(jnp.float32)).astype(jnp.bfloat16)  15.1 us
    reduce_sum x1, other arithmetic, per_device(): sums_sq = jnp.sum(jnp.square(observed.astype(jnp.float32)), axis=1)  7.52 us
  transfers between devices with their start and end apart: 4, of which 4 were waited for; matrix products, arithmetic and copies ran while one was open for 6% of the time, Pallas kernels for 10%

profile of v2, /device:TPU:0, one launch (start us, length us, event | category | flops | bytes accessed | tf_op | source)
XLA Modules:
  0.0 364.6 jit_solution(8953959380704981224)
XLA Ops:
  7.2 0.0 all-reduce.86.cloned.1.call-start
  7.2 1.1 fusion.42
  8.3 1.8 fusion.9
  10.1 0.1 broadcast_bitcast_fusion
  10.2 0.0 slice-start
  10.2 15.1 %subtract_convert_fusion = (bf16[16384,128]{1,0:T(8,128)(2,1)S(1)}, bf16[16384,128]{1,0:T(8,128)(2,1)S(1)}, bf16[16384,128]{1,0:T(8,128)(2,1)S(1)}, bf16[16384,128]{1,0:T(8,128)(2,1)S(1)}) fusion(f32[16384,128]{1,0:T(8,128)} %param.6, f32[16384]{0:T(1024)S(1)} %broadcast_bitcast_fusion, f32[16384]{0:T(1024)} %param.7), kind=kLoop, calls=%fused_computation.8 | loop fusion | flops 20971520 | bytes 25296896 | tf_op jit(solution)/shard_map/convert_element_type | solution.py:77
  25.3 0.0 slice-start.1
  25.3 2.4 fusion
  27.7 0.0 copy-start.1
  27.8 0.0 slice-done
  27.8 0.0 slice-done.1
  27.8 3.4 convolution_bitcast_fusion
  31.2 0.7 pad_maximum_fusion
  31.9 0.0 all-reduce.86.cloned.1.call-update
  31.9 0.0 all-gather.5.cloned.1.call-start
  31.9 0.0 copy-done.1
  32.1 62.6 %all-reduce.86.cloned.1.call-done = f32[384,128]{1,0:T(8,128)} async-done(((f32[384,128]{1,0:T(8,128)}), f32[384,128]{1,0:T(8,128)}) %all-reduce.86.cloned.1.call-update) | async-done | bytes 196624 | tf_op jit(solution)/shard_map/psum | solution.py:87
  94.7 1.5 fusion.21.a_ref
  96.2 16.7 %shard_map.68 = f32[1,128,128]{2,1,0:T(8,128)} custom-call(f32[1,128,128]{2,1,0:T(8,128)} %fusion.21.a_ref), custom_call_target="tpu_custom_call" | custom-call | tf_op jit(solution)/shard_map/pallas_call | solution.py:41
  112.9 1.2 fusion.17
  117.8 23.8 %all-gather.2 = f32[16,4,128]{2,1,0:T(4,128)S(1)} all-gather(f32[1,4,128]{2,1,0:T(4,128)S(1)} %maximum_bitcast_fusion), channel_id=2, replica_groups=mesh['sens'=8,'tm'=16] {'tm'}, dimensions={0}, use_global_device_ids=true | all-gather | bytes 34816 | tf_op jit(solution)/shard_map/all_gather | solution.py:100
  142.8 0.1 rev.13
  142.9 0.1 rev.12
  143.1 0.1 multiply_convert_fusion
  143.1 0.0 copy-done.2
  143.1 0.8 convolution_add_fusion
  144.0 0.0 all-gather.5.cloned.1.call-update
  144.0 0.0 reduce-scatter.2.cloned.1.call-start
  144.1 0.1 bitcast_convert_fusion
  144.1 6.9 %fusion.7 = f32[16384,128]{1,0:T(8,128)} fusion(bf16[256,128]{1,0:T(8,128)(2,1)S(1)} %multiply_convert_fusion, bf16[16384,256]{1,0:T(8,128)(2,1)} %param.5, bf16[16384]{0:T(1024)(128)(2,1)S(1)} %bitcast_convert_fusion), kind=kOutput, calls=%fused_computation.11 | convolution fusion | flops 1077936128 | bytes 16875520 | tf_op jit(solution)/shard_map/dot_general | solution.py:115
  151.0 0.0 reduce-scatter.2.cloned.1.call-update
  151.0 0.0 all-reduce.88.cloned.1.call-start
  151.1 7.5 %multiply_reduce_fusion = f32[16384]{0:T(1024)} fusion(bf16[16384,256]{1,0:T(8,128)(2,1)} %param.5, bf16[16384]{0:T(1024)(128)(2,1)S(1)} %bitcast_convert_fusion), kind=kLoop, calls=%fused_computation | loop fusion | flops 16760832 | bytes 8486912 | tf_op jit(solution)/shard_map/reduce_sum | solution.py:114
  158.6 0.0 all-reduce.88.cloned.1.call-update
  158.6 0.1 dynamic-slice_reduce_fusion
  158.7 0.0 copy-done.3
  158.8 0.6 dynamic-slice
  160.0 23.6 %all-gather.5.cloned.1.call-done = f32[2048,128]{1,0:T(8,128)} async-done(((f32[128,128]{1,0:T(8,128)}), f32[2048,128]{1,0:T(8,128)}) %all-gather.5.cloned.1.call-update) | async-done | bytes 1048592 | tf_op jit(solution)/shard_map/all_gather | solution.py:125
  183.6 2.4 fusion.14
  186.0 0.9 copy.18.a_ref
  186.9 38.0 %shard_map.69 = f32[8,128,128]{2,1,0:T(8,128)} custom-call(f32[8,128,128]{2,1,0:T(8,128)} %copy.18.a_ref), custom_call_target="tpu_custom_call" | custom-call | tf_op jit(solution)/shard_map/pallas_call | solution.py:41
  224.9 47.4 %reduce-scatter.2.cloned.1.call-done = f32[1024,128]{1,0:T(8,128)} async-done(((f32[16384,128]{1,0:T(8,128)}), f32[1024,128]{1,0:T(8,128)}) %reduce-scatter.2.cloned.1.call-update) | async-done | bytes 524304 | tf_op jit(solution)/shard_map/reduce_scatter | solution.py:121
  272.4 2.4 fusion.61
  274.8 0.0 copy-start
  274.8 1.4 multiply_reduce_fusion.1
  276.2 80.4 %all-reduce.88.cloned.1.call-done = f32[128,128]{1,0:T(8,128)} async-done(((f32[128,128]{1,0:T(8,128)}), f32[128,128]{1,0:T(8,128)}) %all-reduce.88.cloned.1.call-update) | async-done | bytes 65552
  356.7 1.4 fusion.32
  358.0 0.0 copy-done
  (342 shorter events, 3.7 us)
Async XLA Ops:
  7.2 87.6 %all-reduce.86.cloned.1.call-start = ((), (), s32[]{:S(2)}) async-start(), calls=%async_computation.1 | async-start | bytes 393216 | tf_op jit(solution)/shard_map/psum | solution.py:87
  10.2 17.6 %slice-start = ((s8[8388608]{0:T(1024)(128)(4,1)}), s8[4194304]{0:T(1024)(128)(4,1)S(1)}, s32[]{:S(2)}) async-start(s8[8388608]{0:T(1024)(128)(4,1)} %bitcast.59), calls=%async_computation.5 | async-start | bytes 8388608
  25.3 2.5 slice-start.1
  27.7 4.2 %copy-start.1 = (f32[256,128]{1,0:T(8,128)S(1)}, f32[256,128]{1,0:T(8,128)}, u32[]{:S(2)}) copy-start(f32[256,128]{1,0:T(8,128)} %param.8) | copy-start | bytes 393220
  31.9 151.7 %all-gather.5.cloned.1.call-start = ((), (), s32[]{:S(2)}) async-start(), calls=%async_computation.3 | async-start | bytes 1114112 | tf_op jit(solution)/shard_map/all_gather | solution.py:125
  112.9 30.2 %copy-start.2 = (f32[1,128,128]{2,1,0:T(8,128)S(1)}, f32[1,128,128]{2,1,0:T(8,128)}, u32[]{:S(2)}) copy-start(f32[1,128,128]{2,1,0:T(8,128)} %shard_map.68) | copy-start | bytes 196612
  144.0 128.4 %reduce-scatter.2.cloned.1.call-start = ((), (), s32[]{:S(2)}) async-start(), calls=%async_computation.2 | async-start | bytes 8912896 | tf_op jit(solution)/shard_map/reduce_scatter | solution.py:121
  151.0 7.7 %copy-start.3 = (u32[128]{0:T(128)S(1)}, u32[128]{0:T(128)}, u32[]{:S(2)}) copy-start(u32[128]{0:T(128)} %constant.204) | copy-start | bytes 1540
  151.0 205.6 %all-reduce.88.cloned.1.call-start = ((), (), s32[]{:S(2)}) async-start(), calls=%async_computation.4 | async-start | bytes 131072
  274.8 83.3 %copy-start = (f32[8,128,128]{2,1,0:T(8,128)}, f32[8,128,128]{2,1,0:T(8,128)S(1)}, u32[]{:S(2)}) copy-start(f32[8,128,128]{2,1,0:T(8,128)S(1)} %fusion.61) | copy-start | bytes 1572868
Sparse Core Ops, SparseCore 0:
  32.0 62.6 all-reduce.85
  144.1 39.4 all-gather.4
  187.0 85.3 reduce-scatter.1
  275.4 81.2 all-reduce.87

commit v3 on v2

--- a/solution.py
+++ b/solution.py
@@ -67,6 +67,7 @@
     tile_mask = jnp.dot(block_hit.T, window_hit, precision=HIGH)
     present = lax.dynamic_index_in_dim(tile_mask, time_index, 1, keepdims=False)
     sensor_mask = jnp.repeat(present, BLOCK)
+    obs_mine = lax.all_to_all(observations, "tm", 0, 1, tiled=True)
     weighted = loadings / noise_var[:, None] * sensor_mask[:, None]
     scaled = weighted.astype(jnp.bfloat16)
     info_part = lax.dot_general(
@@ -110,19 +111,23 @@
         jnp.bfloat16
     )
     mask_mine = lax.dynamic_slice_in_dim(tile_mask, time_index * blocks_share, blocks_share, 0)
-    observed = observations * sensor_mask.astype(jnp.bfloat16)[:, None]
-    sums_sq = jnp.sum(jnp.square(observed.astype(jnp.float32)), axis=1)
-    cross_terms = jnp.dot(observed, smoothed, preferred_element_type=jnp.float32)
     squares = lax.dot_general(
         smoothed, smoothed, (((0,), (0,)), ((), ())), preferred_element_type=jnp.float32
     )
     moment = squares + window_len * covariance
-    share = sens_dev // time_count
-    cross_mine = lax.psum_scatter(cross_terms, "tm", scatter_dimension=0, tiled=True)
-    sq_mine = lax.psum_scatter(
-        sums_sq.reshape(-1, factors), "tm", scatter_dimension=0, tiled=True
-    ).reshape(share)
-    all_moments = lax.all_gather(moment, "tm", axis=0, tiled=False)
+    gathered = lax.all_gather(
+        jnp.concatenate([smoothed.astype(jnp.float32), moment], 0), "tm", axis=0, tiled=False
+    )
+    smooth_all = gathered[:, :window_len].reshape(time_count * window_len, factors)
+    all_moments = gathered[:, window_len:]
+    mask_full = jnp.broadcast_to(
+        mask_mine[:, None, :, None], (blocks_share, BLOCK, time_count, window_len)
+    ).reshape(blocks_share * BLOCK, time_count * window_len)
+    observed = obs_mine * mask_full.astype(jnp.bfloat16)
+    sq_mine = jnp.sum(jnp.square(observed.astype(jnp.float32)), axis=1)
+    cross_mine = jnp.dot(
+        observed, smooth_all.astype(jnp.bfloat16), preferred_element_type=jnp.float32
+    )
     moment_mine = jnp.einsum("bw,wij->bij", mask_mine, all_moments, precision=HIGH)
     counts_mine = jnp.sum(mask_mine, axis=1)
     cross_blocks = cross_mine.reshape(blocks_share, BLOCK, factors)

time: 365 us -> 293 us (0.80)
  waiting for transfers between devices: 214 us -> 105 us
  blocking collectives: 23.8 us -> 58.9 us
  starting transfers between devices: 0.16 us -> 8.26 us
    unnamed x5 -> x2, waiting for transfers between devices: 80.5 us -> 0.03 us
    reduce_scatter x1 -> x0, waiting for transfers between devices: 47.4 us -> none  [per_device(): lax.psum_scatter(cross_terms, 'tm', scatter_dimension=0, tiled=True)]
    all_gather x1, blocking collectives: 23.8 us -> 58.9 us  [per_device(): windows = lax.all_gather(summary, 'tm', axis=0, tiled=False)]
    all_gather x1, waiting for transfers between devices: 23.6 us -> 48.2 us  [per_device(): lax.all_gather(jnp.concatenate([smoothed.astype(jnp.float32), moment], 0)...]
    all_to_all x0 -> x1, starting transfers between devices: none -> 8.18 us  [per_device(): obs_mine = lax.all_to_all(observations, 'tm', 0, 1, tiled=True)]
    psum x1, waiting for transfers between devices: 62.6 us -> 56.3 us  [per_device(): summed = lax.psum(jnp.concatenate([info_part, gram_part], 0), 'sens')]
  transfers between devices with their start and end apart: 4 -> 3, of which waited for: 4 -> 2; matrix products, arithmetic and copies ran while one was open for 6% -> 4% of each run, Pallas kernels for 10% -> 19%
where the time goes in v3:
time: 293 us; the launch traced here: 292 us
  waiting for transfers between devices  105 us (36%)
  blocking collectives  58.9 us (20%)
  Pallas kernels  54.7 us (19%)
  other arithmetic  25.8 us (9%)
  matrix products  17.9 us (6%)
  between operations  15.8 us (5%)
  starting transfers between devices  8.26 us (3%)
  local copies, waits for them, and re-layouts  6.35 us (2%)
    all_gather x1, blocking collectives, per_device(): windows = lax.all_gather(summary, 'tm', axis=0, tiled=False)  58.9 us
    psum x1, waiting for transfers between devices, per_device(): summed = lax.psum(jnp.concatenate([info_part, gram_part], 0), 'sens')  56.3 us
    pallas_call x2, Pallas kernels, spd_inverse(): pl.pallas_call(_gauss_jordan, out_shape=jax.ShapeDtypeStruct(a.shape, jnp...  54.7 us
    all_gather x1, waiting for transfers between devices, per_device(): lax.all_gather(jnp.concatenate([smoothed.astype(jnp.float32), moment], 0)...  48.2 us
    convert_element_type x1, other arithmetic, per_device(): (loadings - loadings_hi.astype(jnp.float32)).astype(jnp.bfloat16)  15.1 us
    all_to_all x1, starting transfers between devices, per_device(): obs_mine = lax.all_to_all(observations, 'tm', 0, 1, tiled=True)  8.18 us
    dot_general x1, matrix products, per_device(): jnp.dot(observed, smooth_all.astype(jnp.bfloat16), preferred_element_type...  6.44 us
  transfers between devices with their start and end apart: 3, of which 2 were waited for; matrix products, arithmetic and copies ran while one was open for 4% of the time, Pallas kernels for 19%

profile of v3, /device:TPU:0, one launch (start us, length us, event | category | flops | bytes accessed | tf_op | source)
XLA Modules:
  0.0 292.3 jit_solution(11459546721898591477)
XLA Ops:
  7.2 0.0 all-reduce.84.cloned.1.call-start
  7.2 1.1 fusion.41
  8.3 1.8 fusion.8
  10.1 0.1 broadcast_bitcast_fusion
  10.2 0.0 slice-start
  10.2 15.1 %subtract_convert_fusion = (bf16[16384,128]{1,0:T(8,128)(2,1)S(1)}, bf16[16384,128]{1,0:T(8,128)(2,1)S(1)}, bf16[16384,128]{1,0:T(8,128)(2,1)S(1)}, bf16[16384,128]{1,0:T(8,128)(2,1)S(1)}) fusion(f32[16384,128]{1,0:T(8,128)} %param.6, f32[16384]{0:T(1024)S(1)} %broadcast_bitcast_fusion, f32[16384]{0:T(1024)} %param.7), kind=kLoop, calls=%fused_computation.9 | loop fusion | flops 20971520 | bytes 25296896 | tf_op jit(solution)/shard_map/convert_element_type | solution.py:78
  25.3 0.0 slice-start.1
  25.3 2.4 fusion
  27.8 0.0 slice-done
  27.8 0.0 slice-done.1
  27.8 3.4 %convolution_bitcast_fusion = f32[256,128]{1,0:T(8,128)S(1)} fusion(bf16[16384,128]{1,0:T(8,128)(2,1)S(1)} %get-tuple-element.9, bf16[16384,256]{1,0:T(8,128)(2,1)S(1)} %bitcast.68), kind=kOutput, calls=%fused_computation.19 | convolution fusion | flops 1073741824 | bytes 12713984 | tf_op jit(solution)/shard_map/dot_general | solution.py:73
  31.2 0.7 pad_maximum_fusion
  31.9 0.0 all-reduce.84.cloned.1.call-update
  31.9 0.0 copy-start.2
  31.9 8.2 %all-to-all-start = ((bf16[16,1024,256]{2,1,0:T(8,128)(2,1)}), bf16[16,1024,256]{2,1,0:T(8,128)(2,1)}, u32[]{:S(2)}, u32[]{:S(2)}) async-start(bf16[16,1024,256]{2,1,0:T(8,128)(2,1)} %bitcast.66), calls=%async_computation | async-start | bytes 16777216 | tf_op jit(solution)/shard_map/all_to_all | solution.py:70
  40.1 0.0 all-gather.5.cloned.1.call-start
  40.2 0.0 copy-done.2
  40.3 56.3 %all-reduce.84.cloned.1.call-done = f32[384,128]{1,0:T(8,128)} async-done(((f32[384,128]{1,0:T(8,128)}), f32[384,128]{1,0:T(8,128)}) %all-reduce.84.cloned.1.call-update) | async-done | bytes 196624 | tf_op jit(solution)/shard_map/psum | solution.py:88
  96.7 1.5 fusion.21.a_ref
  98.1 16.7 %shard_map.68 = f32[1,128,128]{2,1,0:T(8,128)} custom-call(f32[1,128,128]{2,1,0:T(8,128)} %fusion.21.a_ref), custom_call_target="tpu_custom_call" | custom-call | tf_op jit(solution)/shard_map/pallas_call | solution.py:41
  114.8 0.0 copy-start.3
  114.8 1.2 fusion.17
  119.8 58.9 %all-gather.2 = f32[16,4,128]{2,1,0:T(4,128)S(1)} all-gather(f32[1,4,128]{2,1,0:T(4,128)S(1)} %maximum_bitcast_fusion), channel_id=2, replica_groups=mesh['sens'=8,'tm'=16] {'tm'}, dimensions={0}, use_global_device_ids=true | all-gather | bytes 34816 | tf_op jit(solution)/shard_map/all_gather | solution.py:101
  179.9 0.1 rev.13
  180.0 0.1 rev.12
  180.2 0.1 fusion.37
  180.2 0.0 copy-done.3
  180.3 0.2 convolution_add_fusion
  180.5 0.7 pad_maximum_fusion.1
  181.1 0.0 all-gather.5.cloned.1.call-update
  181.2 0.1 dynamic-slice_convert_fusion
  181.2 0.1 broadcast_in_dim.20
  181.4 0.1 dynamic-slice_reduce_fusion
  181.5 48.2 %all-gather.5.cloned.1.call-done = f32[6144,128]{1,0:T(8,128)} async-done(((f32[384,128]{1,0:T(8,128)}), f32[6144,128]{1,0:T(8,128)}) %all-gather.5.cloned.1.call-update) | async-done | bytes 3145744 | tf_op jit(solution)/shard_map/all_gather | solution.py:118
  229.7 1.3 slice.1032
  231.0 1.2 fusion.13
  232.3 0.9 copy.18.a_ref
  233.2 38.0 %shard_map.69 = f32[8,128,128]{2,1,0:T(8,128)} custom-call(f32[8,128,128]{2,1,0:T(8,128)} %copy.18.a_ref), custom_call_target="tpu_custom_call" | custom-call | tf_op jit(solution)/shard_map/pallas_call | solution.py:41
  271.1 0.0 all-to-all-done
  271.2 0.0 copy-start.1
  271.2 6.4 %fusion.7 = f32[1024,128,1]{1,0,2:T(8,128)S(1)} fusion(bf16[16,1024,256]{2,1,0:T(8,128)(2,1)} %all-to-all-done, bf16[1024,16]{0,1:T(8,128)(2,1)S(1)} %bitcast.73, f32[16,384,128]{2,1,0:T(8,128)} %bitcast.72), kind=kOutput, calls=%fused_computation.12 | convolution fusion | flops 1077936128 | bytes 9994240 | tf_op jit(solution)/shard_map/dot_general | solution.py:128
  277.6 0.0 copy-done.1
  277.6 1.2 fusion.67
  278.8 0.0 copy-start
  278.8 0.2 fusion.15
  279.1 5.7 %multiply_reduce_fusion = f32[1024]{0:T(1024)S(1)} fusion(bf16[16,1024,256]{2,1,0:T(8,128)(2,1)} %all-to-all-done, bf16[1024,16]{0,1:T(8,128)(2,1)S(1)} %bitcast.74), kind=kLoop, calls=%fused_computation | loop fusion | flops 16776192 | bytes 8425472 | tf_op jit(solution)/shard_map/reduce_sum | solution.py:127
  284.7 0.7 bitcast_divide_fusion
  285.4 0.0 copy-done
  (341 shorter events, 3.7 us)
Async XLA Ops:
  7.2 89.5 %all-reduce.84.cloned.1.call-start = ((), (), s32[]{:S(2)}) async-start(), calls=%async_computation.1 | async-start | bytes 393216 | tf_op jit(solution)/shard_map/psum | solution.py:88
  10.2 17.6 %slice-start = ((s8[8388608]{0:T(1024)(128)(4,1)}), s8[4194304]{0:T(1024)(128)(4,1)S(1)}, s32[]{:S(2)}) async-start(s8[8388608]{0:T(1024)(128)(4,1)} %bitcast.67), calls=%async_computation.3 | async-start | bytes 8388608
  25.3 2.5 slice-start.1
  31.9 8.3 %copy-start.2 = (f32[256,128]{1,0:T(8,128)S(1)}, f32[256,128]{1,0:T(8,128)}, u32[]{:S(2)}) copy-start(f32[256,128]{1,0:T(8,128)} %param.8) | copy-start | bytes 393220
  31.9 239.2 %all-to-all-start = ((bf16[16,1024,256]{2,1,0:T(8,128)(2,1)}), bf16[16,1024,256]{2,1,0:T(8,128)(2,1)}, u32[]{:S(2)}, u32[]{:S(2)}) async-start(bf16[16,1024,256]{2,1,0:T(8,128)(2,1)} %bitcast.66), calls=%async_computation | async-start | bytes 16777216 | tf_op jit(solution)/shard_map/all_to_all | solution.py:70
  40.1 189.6 %all-gather.5.cloned.1.call-start = ((), (), s32[]{:S(2)}) async-start(), calls=%async_computation.2 | async-start | bytes 3342336 | tf_op jit(solution)/shard_map/all_gather | solution.py:118
  114.8 65.4 %copy-start.3 = (f32[1,128,128]{2,1,0:T(8,128)S(1)}, f32[1,128,128]{2,1,0:T(8,128)}, u32[]{:S(2)}) copy-start(f32[1,128,128]{2,1,0:T(8,128)} %shard_map.68) | copy-start | bytes 196612
  271.2 6.4 %copy-start.1 = (f32[8,128,128]{2,1,0:T(8,128)S(1)}, f32[8,128,128]{2,1,0:T(8,128)}, u32[]{:S(2)}) copy-start(f32[8,128,128]{2,1,0:T(8,128)} %shard_map.69) | copy-start | bytes 1572868
  278.8 6.6 %copy-start = (f32[8,128,128]{2,1,0:T(8,128)}, f32[8,128,128]{2,1,0:T(8,128)S(1)}, u32[]{:S(2)}) copy-start(f32[8,128,128]{2,1,0:T(8,128)S(1)} %fusion.67) | copy-start | bytes 1572868
Sparse Core Ops, SparseCore 0:
  32.0 64.5 all-reduce.83
  181.3 48.3 all-gather.4

commit v4 on v3

--- a/solution.py
+++ b/solution.py
@@ -46,10 +46,13 @@
     )(a)
 
 
-def entering(gains, values, position):
-    inclusive = lax.associative_scan(compose, (gains, values), axis=0)
-    shifted_value = jnp.concatenate([jnp.zeros_like(values[:1]), inclusive[1][:-1]], 0)
-    return lax.dynamic_index_in_dim(shifted_value, position, 0, keepdims=True)
+def butterfly_sum(part, axis, count):
+    distance = 1
+    while distance < count:
+        pairs = [(i, i ^ distance) for i in range(count)]
+        part = part + lax.ppermute(part, axis, pairs)
+        distance *= 2
+    return part
 
 
 def per_device(observations, loadings, noise_var, decay, tiles):
@@ -85,49 +88,39 @@
     gram_part = (
         split[:factors, :factors] + split[:factors, factors:] + split[factors:, :factors]
     )
-    summed = lax.psum(jnp.concatenate([info_part, gram_part], 0), "sens")
+    summed = butterfly_sum(jnp.concatenate([info_part, gram_part], 0), "sens", sens_count)
     info_vec = summed[:window_len]
     information = summed[window_len:]
     identity = jnp.eye(factors, dtype=jnp.float32)
     covariance = spd_inverse((identity + information)[None])[0]
     local_est = jnp.dot(info_vec, covariance, precision=HIGH)
-    fwd_gain, fwd_local = lax.associative_scan(compose, (decay, local_est), axis=0)
-    back_gain, back_local = lax.associative_scan(
-        compose, (jnp.flip(decay, 0), jnp.flip(local_est, 0)), axis=0
+    gathered = lax.all_gather(
+        jnp.concatenate([local_est, decay, covariance], 0), "tm", axis=0, tiled=False
     )
-    summary = jnp.concatenate(
-        [fwd_gain[-1:], fwd_local[-1:], back_gain[-1:], back_local[-1:]], 0
+    steps = time_count * window_len
+    est_all = gathered[:, :window_len].reshape(steps, factors)
+    decay_all = gathered[:, window_len : 2 * window_len].reshape(steps, factors)
+    cov_all = gathered[:, 2 * window_len :]
+    forward = lax.associative_scan(compose, (decay_all, est_all), axis=0)[1]
+    backward = jnp.flip(
+        lax.associative_scan(compose, (jnp.flip(decay_all, 0), jnp.flip(est_all, 0)), axis=0)[1],
+        0,
     )
-    windows = lax.all_gather(summary, "tm", axis=0, tiled=False)
-    enter_fwd = entering(windows[:, 0], windows[:, 1], time_index)
-    enter_back = entering(
-        jnp.flip(windows[:, 2], 0), jnp.flip(windows[:, 3], 0), time_count - 1 - time_index
-    )
-    back_gain = jnp.flip(back_gain, 0)
-    back_local = jnp.flip(back_local, 0)
-    forward = fwd_local + fwd_gain * enter_fwd
-    backward = back_local + back_gain * enter_back
-    smoothed = ((1.0 - decay) / (1.0 + decay) * (forward + backward - local_est)).astype(
-        jnp.bfloat16
+    smooth_all = (
+        (1.0 - decay_all) / (1.0 + decay_all) * (forward + backward - est_all)
+    ).astype(jnp.bfloat16)
+    smooth_win = smooth_all.reshape(time_count, window_len, factors)
+    all_moments = (
+        jnp.einsum("wtk,wtj->wkj", smooth_win, smooth_win, preferred_element_type=jnp.float32)
+        + window_len * cov_all
     )
     mask_mine = lax.dynamic_slice_in_dim(tile_mask, time_index * blocks_share, blocks_share, 0)
-    squares = lax.dot_general(
-        smoothed, smoothed, (((0,), (0,)), ((), ())), preferred_element_type=jnp.float32
-    )
-    moment = squares + window_len * covariance
-    gathered = lax.all_gather(
-        jnp.concatenate([smoothed.astype(jnp.float32), moment], 0), "tm", axis=0, tiled=False
-    )
-    smooth_all = gathered[:, :window_len].reshape(time_count * window_len, factors)
-    all_moments = gathered[:, window_len:]
     mask_full = jnp.broadcast_to(
         mask_mine[:, None, :, None], (blocks_share, BLOCK, time_count, window_len)
     ).reshape(blocks_share * BLOCK, time_count * window_len)
     observed = obs_mine * mask_full.astype(jnp.bfloat16)
     sq_mine = jnp.sum(jnp.square(observed.astype(jnp.float32)), axis=1)
-    cross_mine = jnp.dot(
-        observed, smooth_all.astype(jnp.bfloat16), preferred_element_type=jnp.float32
-    )
+    cross_mine = jnp.dot(observed, smooth_all, preferred_element_type=jnp.float32)
     moment_mine = jnp.einsum("bw,wij->bij", mask_mine, all_moments, precision=HIGH)
     counts_mine = jnp.sum(mask_mine, axis=1)
     cross_blocks = cross_mine.reshape(blocks_share, BLOCK, factors)

time: 293 us -> 762 us (2.60); the launches traced: 292 us -> 749 us
  local copies, waits for them, and re-layouts: 6.35 us -> 384 us
  other arithmetic: 25.8 us -> 109 us
  blocking collectives: 58.9 us -> 0 us
  waiting for transfers between devices: 105 us -> 155 us
    slice x149 -> x150, local copies, waits for them, and re-layouts: 3.3 us -> 288 us  [the longest x75 155 us: per_device(): lax.associative_scan(compose, (jnp.flip(decay_all, 0), jnp.flip(est_all,...]
    all_to_all x1, waiting for transfers between devices: 0.01 us -> 144 us  [per_device(): obs_mine = lax.all_to_all(observations, 'tm', 0, 1, tiled=True)]
    pad x64 -> x44, local copies, waits for them, and re-layouts: 0.61 us -> 60.8 us  [the longest x22 36.5 us: per_device(): lax.associative_scan(compose, (jnp.flip(decay_all, 0), jnp.flip(est_all,...]
    all_gather x1 -> x0, blocking collectives: 58.9 us -> none  [per_device(): windows = lax.all_gather(summary, 'tm', axis=0, tiled=False)]
    psum x1 -> x0, waiting for transfers between devices: 56.3 us -> none  [per_device(): summed = lax.psum(jnp.concatenate([info_part, gram_part], 0), 'sens')]
    all_gather x1, waiting for transfers between devices: 48.2 us -> 0.01 us  [per_device(): lax.all_gather(jnp.concatenate([local_est, decay, covariance], 0), 'tm',...]
    mul x34 -> x22, other arithmetic: 0.36 us -> 37.5 us  [compose(): before_seg[0] * after_seg[0]]
    add x40 -> x26, other arithmetic: 0.28 us -> 16.8 us  [the longest x12 11.5 us: per_device(): lax.associative_scan(compose, (jnp.flip(decay_all, 0), jnp.flip(est_all,...]
  transfers between devices with their start and end apart: 3 -> 5, of which waited for: 2 -> 4; matrix products, arithmetic and copies ran while one was open for 4% -> 3% of each run, Pallas kernels for 19% -> 0%
where the time goes in v4:
time: 762 us; the launch traced here: 749 us
  local copies, waits for them, and re-layouts  384 us (50%)
  waiting for transfers between devices  155 us (20%)
  other arithmetic  109 us (14%)
  Pallas kernels  54.7 us (7%)
  matrix products  18.6 us (2%)
  between operations  15.2 us (2%)
  starting transfers between devices  13.3 us (2%)
    slice x75, local copies, waits for them, and re-layouts, per_device(): lax.associative_scan(compose, (jnp.flip(decay_all, 0), jnp.flip(est_all,...  155 us
    all_to_all x1, waiting for transfers between devices, per_device(): obs_mine = lax.all_to_all(observations, 'tm', 0, 1, tiled=True)  144 us
    slice x74, local copies, waits for them, and re-layouts, per_device(): forward = lax.associative_scan(compose, (decay_all, est_all), axis=0)[1]  129 us
    pallas_call x2, Pallas kernels, spd_inverse(): pl.pallas_call(_gauss_jordan, out_shape=jax.ShapeDtypeStruct(a.shape, jnp...  54.7 us
    mul x22, other arithmetic, compose(): before_seg[0] * after_seg[0]  37.5 us
    pad x22, local copies, waits for them, and re-layouts, per_device(): lax.associative_scan(compose, (jnp.flip(decay_all, 0), jnp.flip(est_all,...  36.5 us
    pad x22, local copies, waits for them, and re-layouts, per_device(): forward = lax.associative_scan(compose, (decay_all, est_all), axis=0)[1]  24.3 us
    rev x1, local copies, waits for them, and re-layouts, per_device(): jnp.flip(lax.associative_scan(compose, (jnp.flip(decay_all, 0), jnp.flip(...  16.5 us
  transfers between devices with their start and end apart: 5, of which 4 were waited for; matrix products, arithmetic and copies ran while one was open for 3% of the time, Pallas kernels for 0%

profile of v4, /device:TPU:0, one launch (start us, length us, event | category | flops | bytes accessed | tf_op | source)
XLA Modules:
  0.0 749.0 jit_solution(9377742120476324135)
XLA Ops:
  10.2 15.3 %subtract_convert_fusion = (bf16[16384,128]{1,0:T(8,128)(2,1)S(1)}, bf16[16384,128]{1,0:T(8,128)(2,1)S(1)}, bf16[16384,128]{1,0:T(8,128)(2,1)S(1)}, bf16[16384,128]{1,0:T(8,128)(2,1)S(1)}) fusion(f32[16384,128]{1,0:T(8,128)} %param.6, f32[16384]{0:T(1024)S(1)} %broadcast_bitcast_fusion, f32[16384]{0:T(1024)} %param.7), kind=kLoop, calls=%fused_computation.11 | loop fusion | flops 20971520 | bytes 25296896 | tf_op jit(solution)/shard_map/convert_element_type | solution.py:81
  28.0 3.3 convolution_bitcast_fusion
  34.7 5.2 collective-permute-done.1
  40.0 3.4 collective-permute-start.2
  43.4 4.3 collective-permute-done.2
  48.4 16.7 %shard_map.68 = f32[1,128,128]{2,1,0:T(8,128)} custom-call(f32[1,128,128]{2,1,0:T(8,128)} %fusion.28.a_ref), custom_call_target="tpu_custom_call" | custom-call | tf_op jit(solution)/shard_map/pallas_call | solution.py:41
  67.8 8.0 %all-to-all-start = ((bf16[16,1024,256]{2,1,0:T(8,128)(2,1)}), bf16[16,1024,256]{2,1,0:T(8,128)(2,1)}, u32[]{:S(2)}, u32[]{:S(2)}) async-start(bf16[16,1024,256]{2,1,0:T(8,128)(2,1)} %bitcast.56), calls=%async_computation | async-start | bytes 16777216 | tf_op jit(solution)/shard_map/all_to_all | solution.py:73
  77.2 143.8 %all-to-all-done = bf16[16,1024,256]{2,1,0:T(8,128)(2,1)} async-done(((bf16[16,1024,256]{2,1,0:T(8,128)(2,1)}), bf16[16,1024,256]{2,1,0:T(8,128)(2,1)}, u32[]{:S(2)}, u32[]{:S(2)}) %all-to-all-start) | async-done | bytes 8388640 | tf_op jit(solution)/shard_map/all_to_all | solution.py:73
  221.0 12.3 %copy.22 = bf16[1024,16,256]{0,2,1:T(8,128)(2,1)} copy(bf16[1024,16,256]{2,0,1:T(8,128)(2,1)} %bitcast.1) | data formatting | bytes 16777216 | tf_op jit(solution)/shard_map/all_to_all | solution.py:73
  233.3 6.3 multiply_reduce_fusion
  239.6 4.0 fusion.43
  244.5 3.5 slice.612
  248.0 6.2 slice.610
  254.3 6.2 slice.614
  260.5 3.4 fusion.45
  263.9 3.6 slice.617
  267.5 3.6 slice.618
  271.1 3.6 slice.616
  274.7 3.6 slice.620
  371.8 3.6 slice.615
  375.4 3.6 slice.696
  380.2 8.8 %slice.702 = f32[2048,128]{1,0:T(8,128)} reverse(f32[2048,128]{1,0:T(8,128)} %slice.614), dimensions={0} | reverse | bytes 2097152 | tf_op jit(solution)/shard_map/slice | solution.py:106
  389.0 8.8 %slice.703 = f32[2048,128]{1,0:T(8,128)} reverse(f32[2048,128]{1,0:T(8,128)} %slice.612), dimensions={0} | reverse | bytes 2097152 | tf_op jit(solution)/shard_map/slice | solution.py:106
  397.8 5.1 slice.704
  402.9 8.8 %slice.706 = f32[2048,128]{1,0:T(8,128)} reverse(f32[2048,128]{1,0:T(8,128)} %slice.610), dimensions={0} | reverse | bytes 2097152 | tf_op jit(solution)/shard_map/slice | solution.py:106
  411.7 3.4 fusion.46
  419.1 3.6 slice.708
  422.8 3.6 slice.712
  528.7 3.6 slice.707
  534.9 6.3 slice.700
  541.2 3.5 slice.790
  544.7 6.3 slice.609
  551.0 3.4 slice.698
  574.8 4.7 pad.167
  581.8 8.7 %pad.169 = f32[4096,128]{1,0:T(8,128)} pad(f32[2048,128]{1,0:T(8,128)} %add.393, f32[]{:T(128)} %constant.25.clone.1), padding=1_0_1x0_0_0 | pad | bytes 3145732 | tf_op jit(solution)/shard_map/pad | solution.py:104
  610.6 4.6 pad.190
  615.2 4.6 pad.191
  619.8 2.6 add.428
  622.4 8.5 %pad.193 = f32[4096,128]{1,0:T(8,128)} pad(f32[2048,128]{1,0:T(8,128)} %add.428, f32[]{:T(128)} %constant.25.clone.1), padding=1_0_1x0_0_0 | pad | bytes 3145732 | tf_op jit(solution)/shard_map/pad | solution.py:106
  630.9 9.0 %slice.701 = f32[2047,128]{1,0:T(8,128)} reverse(f32[2047,128]{1,0:T(8,128)} %slice.700), dimensions={0} | reverse | bytes 2096128 | tf_op jit(solution)/shard_map/slice | solution.py:106
  640.0 9.1 %slice.791 = f32[2047,128]{1,0:T(8,128)} reverse(f32[2047,128]{1,0:T(8,128)} %slice.790), dimensions={0} | reverse | bytes 2096128 | tf_op jit(solution)/shard_map/slice | solution.py:106
  653.6 8.5 %pad.192 = f32[4096,128]{1,0:T(8,128)} pad(f32[2048,128]{1,0:T(8,128)} %get-tuple-element.67, f32[]{:T(128)} %constant.25.clone.1), padding=0_1_1x0_0_0 | pad | bytes 3145732 | tf_op jit(solution)/shard_map/pad | solution.py:106
  662.2 3.7 add.430
  665.9 16.5 %rev.6 = f32[4096,128]{1,0:T(8,128)} reverse(f32[4096,128]{1,0:T(8,128)} %add.430), dimensions={0} | reverse | bytes 4194304 | tf_op jit(solution)/shard_map/jit(_flip)/rev | solution.py:105
  682.4 4.7 pad.168
  687.1 4.2 multiply_convert_fusion
  695.1 38.0 %shard_map.69 = f32[8,128,128]{2,1,0:T(8,128)} custom-call(f32[8,128,128]{2,1,0:T(8,128)} %copy.27.a_ref), custom_call_target="tpu_custom_call" | custom-call | tf_op jit(solution)/shard_map/pallas_call | solution.py:41
  734.3 5.7 fusion
  (377 shorter events, 271.7 us)
Async XLA Ops:
  7.2 232.4 %all-gather.3.cloned.1.call-start = ((), (), s32[]{:S(2)}) async-start(), calls=%async_computation.1 | async-start | bytes 5570560 | tf_op jit(solution)/shard_map/all_gather | solution.py:97
  10.1 66.4 %copy-start.14 = (f32[128,16]{0,1:T(8,128)}, f32[128,16]{0,1:T(8,128)S(1)}, u32[]{:S(2)}) copy-start(f32[128,16]{0,1:T(8,128)S(1)} %fusion.9) | copy-start | bytes 24580
  10.2 17.8 %slice-start = ((s8[8388608]{0:T(1024)(128)(4,1)}), s8[4194304]{0:T(1024)(128)(4,1)S(1)}, s32[]{:S(2)}) async-start(s8[8388608]{0:T(1024)(128)(4,1)} %bitcast.57), calls=%async_computation.2 | async-start | bytes 8388608
  25.5 2.5 slice-start.1
  28.0 38.2 %copy-start.8 = (f32[256,128]{1,0:T(8,128)S(1)}, f32[256,128]{1,0:T(8,128)}, u32[]{:S(2)}) copy-start(f32[256,128]{1,0:T(8,128)} %param.8) | copy-start | bytes 393220
  31.4 1.5 collective-permute-start
  32.9 7.0 collective-permute-start.1
  40.0 7.7 %collective-permute-start.2 = (f32[384,128]{1,0:T(8,128)S(1)}, f32[384,128]{1,0:T(8,128)S(1)}, u32[]{:S(2)}, u32[]{:S(2)}) collective-permute-start(f32[384,128]{1,0:T(8,128)S(1)} %add.357), channel_id=1, source_target_pairs={{0,64},{16,80},{32,96},{48,112},{64,0},{80,16},{96,32},{112,48},{1... | collective-permute-start | bytes 589832 | tf_op jit(solution)/shard_map/ppermute | solution.py:53
  67.8 153.2 %all-to-all-start = ((bf16[16,1024,256]{2,1,0:T(8,128)(2,1)}), bf16[16,1024,256]{2,1,0:T(8,128)(2,1)}, u32[]{:S(2)}, u32[]{:S(2)}) async-start(bf16[16,1024,256]{2,1,0:T(8,128)(2,1)} %bitcast.56), calls=%async_computation | async-start | bytes 16777216 | tf_op jit(solution)/shard_map/all_to_all | solution.py:73
  528.7 31.8 %copy-start.11 = (f32[31,128]{1,0:T(8,128)S(1)}, f32[31,128]{1,0:T(8,128)}, u32[]{:S(2)}) copy-start(f32[31,128]{1,0:T(8,128)} %slice.645) | copy-start | bytes 47620
  534.9 29.3 %copy-start.34 = (f32[1,128]{1,0:T(1,128)S(1)}, f32[1,128]{1,0:T(1,128)}, u32[]{:S(2)}) copy-start(f32[1,128]{1,0:T(1,128)} %slice.804) | copy-start | bytes 1540
  534.9 30.0 %copy-start.6 = (f32[255,128]{1,0:T(8,128)S(1)}, f32[255,128]{1,0:T(8,128)}, u32[]{:S(2)}) copy-start(f32[255,128]{1,0:T(8,128)} %slice.627) | copy-start | bytes 391684
  534.9 30.0 %copy-start.7 = (f32[255,128]{1,0:T(8,128)S(1)}, f32[255,128]{1,0:T(8,128)}, u32[]{:S(2)}) copy-start(f32[255,128]{1,0:T(8,128)} %slice.692) | copy-start | bytes 391684
  534.9 30.1 %copy-start.33 = (f32[1,128]{1,0:T(1,128)S(1)}, f32[1,128]{1,0:T(1,128)}, u32[]{:S(2)}) copy-start(f32[1,128]{1,0:T(1,128)} %slice.803) | copy-start | bytes 1540
  544.7 23.1 %copy-start.5 = (f32[511,128]{1,0:T(8,128)S(1)}, f32[511,128]{1,0:T(8,128)}, u32[]{:S(2)}) copy-start(f32[511,128]{1,0:T(8,128)} %slice.621) | copy-start | bytes 784900
  564.3 7.4 copy-start.32
  571.7 18.8 %copy-start.30 = (f32[1,128]{1,0:T(1,128)S(1)}, f32[1,128]{1,0:T(1,128)}, u32[]{:S(2)}) copy-start(f32[1,128]{1,0:T(1,128)} %get-tuple-element.54) | copy-start | bytes 1540
  571.7 18.8 %copy-start.31 = (f32[1,128]{1,0:T(1,128)S(1)}, f32[1,128]{1,0:T(1,128)}, u32[]{:S(2)}) copy-start(f32[1,128]{1,0:T(1,128)} %get-tuple-element.55) | copy-start | bytes 1540
  571.7 18.8 %copy-start.23 = (f32[4,128]{1,0:T(4,128)S(1)}, f32[4,128]{1,0:T(4,128)}, u32[]{:S(2)}) copy-start(f32[4,128]{1,0:T(4,128)} %pad.173) | copy-start | bytes 6148
  571.7 18.8 %copy-start.24 = (f32[3,128]{1,0:T(4,128)S(1)}, f32[3,128]{1,0:T(4,128)}, u32[]{:S(2)}) copy-start(f32[3,128]{1,0:T(4,128)} %slice.755) | copy-start | bytes 4612
  571.7 18.8 %copy-start.25 = (f32[3,128]{1,0:T(4,128)S(1)}, f32[3,128]{1,0:T(4,128)}, u32[]{:S(2)}) copy-start(f32[3,128]{1,0:T(4,128)} %slice.772) | copy-start | bytes 4612
  571.7 18.8 %copy-start.44 = (f32[1,128]{1,0:T(1,128)S(1)}, f32[1,128]{1,0:T(1,128)}, u32[]{:S(2)}) copy-start(f32[1,128]{1,0:T(1,128)} %slice.753) | copy-start | bytes 1540
  571.7 18.9 %copy-start.21 = (f32[7,128]{1,0:T(8,128)S(1)}, f32[7,128]{1,0:T(8,128)}, u32[]{:S(2)}) copy-start(f32[7,128]{1,0:T(8,128)} %slice.749) | copy-start | bytes 10756
  571.8 18.9 %copy-start.22 = (f32[7,128]{1,0:T(8,128)S(1)}, f32[7,128]{1,0:T(8,128)}, u32[]{:S(2)}) copy-start(f32[7,128]{1,0:T(8,128)} %slice.774) | copy-start | bytes 10756
  571.8 18.9 %copy-start.43 = (f32[1,128]{1,0:T(1,128)S(1)}, f32[1,128]{1,0:T(1,128)}, u32[]{:S(2)}) copy-start(f32[1,128]{1,0:T(1,128)} %slice.833) | copy-start | bytes 1540
  571.8 18.9 %copy-start.18 = (f32[15,128]{1,0:T(8,128)S(1)}, f32[15,128]{1,0:T(8,128)}, u32[]{:S(2)}) copy-start(f32[15,128]{1,0:T(8,128)} %slice.743) | copy-start | bytes 23044
  571.8 18.9 %copy-start.19 = (f32[15,128]{1,0:T(8,128)S(1)}, f32[15,128]{1,0:T(8,128)}, u32[]{:S(2)}) copy-start(f32[15,128]{1,0:T(8,128)} %slice.776) | copy-start | bytes 23044
  571.8 19.0 %copy-start.42 = (f32[1,128]{1,0:T(1,128)S(1)}, f32[1,128]{1,0:T(1,128)}, u32[]{:S(2)}) copy-start(f32[1,128]{1,0:T(1,128)} %slice.832) | copy-start | bytes 1540
  571.8 19.0 %copy-start.12 = (f32[31,128]{1,0:T(8,128)S(1)}, f32[31,128]{1,0:T(8,128)}, u32[]{:S(2)}) copy-start(f32[31,128]{1,0:T(8,128)} %slice.737) | copy-start | bytes 47620
  571.8 19.0 %copy-start.13 = (f32[31,128]{1,0:T(8,128)S(1)}, f32[31,128]{1,0:T(8,128)}, u32[]{:S(2)}) copy-start(f32[31,128]{1,0:T(8,128)} %slice.778) | copy-start | bytes 47620
  571.8 19.0 %copy-start.40 = (f32[1,128]{1,0:T(1,128)S(1)}, f32[1,128]{1,0:T(1,128)}, u32[]{:S(2)}) copy-start(f32[1,128]{1,0:T(1,128)} %slice.831) | copy-start | bytes 1540
  572.7 18.2 %copy-start.9 = (f32[63,128]{1,0:T(8,128)S(1)}, f32[63,128]{1,0:T(8,128)}, u32[]{:S(2)}) copy-start(f32[63,128]{1,0:T(8,128)} %slice.731) | copy-start | bytes 96772
  572.7 18.3 %copy-start.10 = (f32[63,128]{1,0:T(8,128)S(1)}, f32[63,128]{1,0:T(8,128)}, u32[]{:S(2)}) copy-start(f32[63,128]{1,0:T(8,128)} %slice.780) | copy-start | bytes 96772
  572.7 18.3 %copy-start.39 = (f32[1,128]{1,0:T(1,128)S(1)}, f32[1,128]{1,0:T(1,128)}, u32[]{:S(2)}) copy-start(f32[1,128]{1,0:T(1,128)} %slice.830) | copy-start | bytes 1540
  572.7 20.7 %copy-start.38 = (f32[1,128]{1,0:T(1,128)S(1)}, f32[1,128]{1,0:T(1,128)}, u32[]{:S(2)}) copy-start(f32[1,128]{1,0:T(1,128)} %slice.829) | copy-start | bytes 1540
  574.8 21.8 %copy-start.37 = (f32[1,128]{1,0:T(1,128)S(1)}, f32[1,128]{1,0:T(1,128)}, u32[]{:S(2)}) copy-start(f32[1,128]{1,0:T(1,128)} %slice.828) | copy-start | bytes 1540
  581.8 22.6 %copy-start.36 = (f32[1,128]{1,0:T(1,128)S(1)}, f32[1,128]{1,0:T(1,128)}, u32[]{:S(2)}) copy-start(f32[1,128]{1,0:T(1,128)} %slice.827) | copy-start | bytes 1540
  594.9 14.8 %copy-start.35 = (f32[1,128]{1,0:T(1,128)S(1)}, f32[1,128]{1,0:T(1,128)}, u32[]{:S(2)}) copy-start(f32[1,128]{1,0:T(1,128)} %slice.826) | copy-start | bytes 1540
  649.0 2.5 copy-start
  649.0 2.8 copy-start.1
  649.0 3.1 copy-start.2
  649.0 3.4 copy-start.28
  649.1 3.4 copy-start.29
  687.1 5.9 copy-start.15
  691.3 41.9 %copy-start.17 = (bf16[8,16]{0,1:T(8,128)(2,1)S(1)}, bf16[8,16]{0,1:T(8,128)(2,1)}, u32[]{:S(2)}) copy-start(bf16[8,16]{0,1:T(8,128)(2,1)} %copy-done.16) | copy-start | bytes 772
  734.3 5.8 copy-start.4
  734.3 7.2 copy-start.20
  734.3 7.2 copy-start.41
  (4 other events, 2.7 us)
Sparse Core Ops, SparseCore 0:
  67.9 151.3 all-gather.2

commit v5 on v3

--- a/solution.py
+++ b/solution.py
@@ -46,6 +46,30 @@
     )(a)
 
 
+def butterfly_sum(part, axis, count):
+    distance = 1
+    while distance < count:
+        pairs = [(i, i ^ distance) for i in range(count)]
+        part = part + lax.ppermute(part, axis, pairs)
+        distance *= 2
+    return part
+
+
+def butterfly_gather(part, axis, count):
+    place = lax.axis_index(axis)
+    held = part[None]
+    distance = 1
+    while distance < count:
+        pairs = [(i, i ^ distance) for i in range(count)]
+        other = lax.ppermute(held, axis, pairs)
+        upper = (place // distance) % 2 == 1
+        held = jnp.where(
+            upper, jnp.concatenate([other, held], 0), jnp.concatenate([held, other], 0)
+        )
+        distance *= 2
+    return held
+
+
 def entering(gains, values, position):
     inclusive = lax.associative_scan(compose, (gains, values), axis=0)
     shifted_value = jnp.concatenate([jnp.zeros_like(values[:1]), inclusive[1][:-1]], 0)
@@ -85,7 +109,7 @@
     gram_part = (
         split[:factors, :factors] + split[:factors, factors:] + split[factors:, :factors]
     )
-    summed = lax.psum(jnp.concatenate([info_part, gram_part], 0), "sens")
+    summed = butterfly_sum(jnp.concatenate([info_part, gram_part], 0), "sens", sens_count)
     info_vec = summed[:window_len]
     information = summed[window_len:]
     identity = jnp.eye(factors, dtype=jnp.float32)
@@ -98,7 +122,7 @@
     summary = jnp.concatenate(
         [fwd_gain[-1:], fwd_local[-1:], back_gain[-1:], back_local[-1:]], 0
     )
-    windows = lax.all_gather(summary, "tm", axis=0, tiled=False)
+    windows = butterfly_gather(summary, "tm", time_count)
     enter_fwd = entering(windows[:, 0], windows[:, 1], time_index)
     enter_back = entering(
         jnp.flip(windows[:, 2], 0), jnp.flip(windows[:, 3], 0), time_count - 1 - time_index

time: 293 us -> 278 us (0.949)
  blocking collectives: 58.9 us -> 0 us
  waiting for transfers between devices: 105 us -> 136 us
  starting transfers between devices: 8.26 us -> 21.1 us
    all_gather x1, waiting for transfers between devices: 48.2 us -> 119 us  [per_device(): lax.all_gather(jnp.concatenate([smoothed.astype(jnp.float32), moment], 0)...]
    all_gather x1 -> x0, blocking collectives: 58.9 us -> none  [per_device(): windows = lax.all_gather(summary, 'tm', axis=0, tiled=False)]
    psum x1 -> x0, waiting for transfers between devices: 56.3 us -> none  [per_device(): summed = lax.psum(jnp.concatenate([info_part, gram_part], 0), 'sens')]
    ppermute x0 -> x7, waiting for transfers between devices: none -> 16.6 us  [the longest x3 10.9 us: butterfly_sum(): part = part + lax.ppermute(part, axis, pairs)]
    ppermute x0 -> x7, starting transfers between devices: none -> 16 us  [the longest x4 10.6 us: butterfly_gather(): other = lax.ppermute(held, axis, pairs)]
    all_to_all x1, starting transfers between devices: 8.18 us -> 5.04 us  [per_device(): obs_mine = lax.all_to_all(observations, 'tm', 0, 1, tiled=True)]
  transfers between devices with their start and end apart: 3 -> 9, of which waited for: 2 -> 7; matrix products, arithmetic and copies ran while one was open for 4% -> 2% of each run, Pallas kernels for 19% -> 14%
where the time goes in v5:
time: 278 us; the launch traced here: 276 us
  waiting for transfers between devices  136 us (49%)
  Pallas kernels  54.7 us (20%)
  other arithmetic  24.3 us (9%)
  starting transfers between devices  21.1 us (8%)
  matrix products  17.8 us (6%)
  between operations  15.9 us (6%)
  local copies, waits for them, and re-layouts  6.35 us (2%)
    all_gather x1, waiting for transfers between devices, per_device(): lax.all_gather(jnp.concatenate([smoothed.astype(jnp.float32), moment], 0)...  119 us
    pallas_call x2, Pallas kernels, spd_inverse(): pl.pallas_call(_gauss_jordan, out_shape=jax.ShapeDtypeStruct(a.shape, jnp...  54.7 us
    convert_element_type x1, other arithmetic, per_device(): (loadings - loadings_hi.astype(jnp.float32)).astype(jnp.bfloat16)  15.1 us
    ppermute x3, waiting for transfers between devices, butterfly_sum(): part = part + lax.ppermute(part, axis, pairs)  10.9 us
    ppermute x4, starting transfers between devices, butterfly_gather(): other = lax.ppermute(held, axis, pairs)  10.6 us
    dot_general x1, matrix products, per_device(): jnp.dot(observed, smooth_all.astype(jnp.bfloat16), preferred_element_type...  6.44 us
    ppermute x4, waiting for transfers between devices, butterfly_gather(): other = lax.ppermute(held, axis, pairs)  5.77 us
    reduce_sum x1, other arithmetic, per_device(): sq_mine = jnp.sum(jnp.square(observed.astype(jnp.float32)), axis=1)  5.68 us
  transfers between devices with their start and end apart: 9, of which 7 were waited for; matrix products, arithmetic and copies ran while one was open for 2% of the time, Pallas kernels for 14%

profile of v5, /device:TPU:0, one launch (start us, length us, event | category | flops | bytes accessed | tf_op | source)
XLA Modules:
  0.0 276.2 jit_solution(11916530441102861089)
XLA Ops:
  7.2 1.1 fusion.42
  8.2 1.8 fusion.8
  10.1 0.1 broadcast_bitcast_fusion
  10.1 0.0 slice-start
  10.1 15.1 %subtract_convert_fusion = (bf16[16384,128]{1,0:T(8,128)(2,1)S(1)}, bf16[16384,128]{1,0:T(8,128)(2,1)S(1)}, bf16[16384,128]{1,0:T(8,128)(2,1)S(1)}, bf16[16384,128]{1,0:T(8,128)(2,1)S(1)}) fusion(f32[16384,128]{1,0:T(8,128)} %param.6, f32[16384]{0:T(1024)S(1)} %broadcast_bitcast_fusion, f32[16384]{0:T(1024)} %param.7), kind=kLoop, calls=%fused_computation.9 | loop fusion | flops 20971520 | bytes 25296896 | tf_op jit(solution)/shard_map/convert_element_type | solution.py:102
  25.3 0.0 slice-start.1
  25.3 2.4 fusion
  27.7 0.0 copy-start.2
  27.8 3.4 %convolution_bitcast_fusion = f32[256,128]{1,0:T(8,128)S(1)} fusion(bf16[16384,128]{1,0:T(8,128)(2,1)S(1)} %get-tuple-element.9, bf16[16384,256]{1,0:T(8,128)(2,1)S(1)} %bitcast.68), kind=kOutput, calls=%fused_computation.19 | convolution fusion | flops 1073741824 | bytes 12713984 | tf_op jit(solution)/shard_map/dot_general | solution.py:97
  31.2 0.1 collective-permute-start
  31.3 1.4 collective-permute-done
  32.7 1.8 collective-permute-start.1
  34.7 5.1 %collective-permute-done.1 = f32[384,128]{1,0:T(8,128)S(1)} collective-permute-done((f32[384,128]{1,0:T(8,128)S(1)}, f32[384,128]{1,0:T(8,128)S(1)}, u32[]{:S(2)}, u32[]{:S(2)}) %collective-permute-start.1) | collective-permute-done | bytes 196640 | tf_op jit(solution)/shard_map/ppermute | solution.py:53
  39.8 3.6 %collective-permute-start.2 = (f32[384,128]{1,0:T(8,128)S(1)}, f32[384,128]{1,0:T(8,128)S(1)}, u32[]{:S(2)}, u32[]{:S(2)}) collective-permute-start(f32[384,128]{1,0:T(8,128)S(1)} %add.497), channel_id=1, source_target_pairs={{0,64},{16,80},{32,96},{48,112},{64,0},{80,16},{96,32},{112,48},{1... | collective-permute-start | bytes 589832 | tf_op jit(solution)/shard_map/ppermute | solution.py:53
  43.4 4.3 %collective-permute-done.2 = f32[384,128]{1,0:T(8,128)S(1)} collective-permute-done((f32[384,128]{1,0:T(8,128)S(1)}, f32[384,128]{1,0:T(8,128)S(1)}, u32[]{:S(2)}, u32[]{:S(2)}) %collective-permute-start.2) | collective-permute-done | bytes 196640 | tf_op jit(solution)/shard_map/ppermute | solution.py:53
  47.7 0.6 fusion.21.a_ref
  48.4 16.7 %shard_map.68 = f32[1,128,128]{2,1,0:T(8,128)} custom-call(f32[1,128,128]{2,1,0:T(8,128)} %fusion.21.a_ref), custom_call_target="tpu_custom_call" | custom-call | tf_op jit(solution)/shard_map/pallas_call | solution.py:41
  65.1 1.1 fusion.17
  69.9 1.6 collective-permute-start.3
  71.5 2.0 collective-permute-done.3
  73.5 3.1 %collective-permute-start.4 = (f32[2,4,128]{2,1,0:T(4,128)S(1)}, f32[2,4,128]{2,1,0:T(4,128)S(1)}, u32[]{:S(2)}, u32[]{:S(2)}) collective-permute-start(f32[2,4,128]{2,1,0:T(4,128)S(1)} %maximum_select_fusion.3), channel_id=1, source_target_pairs={{0,2},{1,3},{2,0},{3,1},{4,6},{5,7},{6,4},{7,5},{8,10},{9,11},{10,... | collective-permute-start | bytes 12296 | tf_op jit(solution)/shard_map/ppermute | solution.py:64
  76.6 2.0 collective-permute-done.4
  78.7 2.0 collective-permute-start.5
  80.6 1.7 collective-permute-done.5
  82.3 3.9 %collective-permute-start.6 = (f32[8,4,128]{2,1,0:T(4,128)S(1)}, f32[8,4,128]{2,1,0:T(4,128)S(1)}, u32[]{:S(2)}, u32[]{:S(2)}) collective-permute-start(f32[8,4,128]{2,1,0:T(4,128)S(1)} %maximum_select_fusion.1), channel_id=1, source_target_pairs={{0,8},{1,9},{2,10},{3,11},{4,12},{5,13},{6,14},{7,15},{8,0},{9,1},... | collective-permute-start | bytes 49160 | tf_op jit(solution)/shard_map/ppermute | solution.py:64
  86.3 5.0 %all-to-all-start = ((bf16[16,1024,256]{2,1,0:T(8,128)(2,1)}), bf16[16,1024,256]{2,1,0:T(8,128)(2,1)}, u32[]{:S(2)}, u32[]{:S(2)}) async-start(bf16[16,1024,256]{2,1,0:T(8,128)(2,1)} %bitcast.66), calls=%async_computation | async-start | bytes 16777216 | tf_op jit(solution)/shard_map/all_to_all | solution.py:94
  91.3 0.0 all-gather.3.cloned.1.call-start
  91.4 0.1 rev.13
  91.5 0.1 rev.12
  92.9 0.1 fusion.38
  93.0 0.2 convolution_add_fusion
  93.2 0.7 pad_maximum_fusion.1
  93.9 0.0 all-gather.3.cloned.1.call-update
  93.9 0.1 dynamic-slice_convert_fusion
  94.0 0.1 broadcast_in_dim.23
  94.1 0.1 dynamic-slice_reduce_fusion
  94.2 119.5 %all-gather.3.cloned.1.call-done = f32[6144,128]{1,0:T(8,128)} async-done(((f32[384,128]{1,0:T(8,128)}), f32[6144,128]{1,0:T(8,128)}) %all-gather.3.cloned.1.call-update) | async-done | bytes 3145744 | tf_op jit(solution)/shard_map/all_gather | solution.py:142
  213.7 1.3 slice.1032
  215.0 1.2 fusion.13
  216.2 0.9 copy.15.a_ref
  217.1 38.0 %shard_map.69 = f32[8,128,128]{2,1,0:T(8,128)} custom-call(f32[8,128,128]{2,1,0:T(8,128)} %copy.15.a_ref), custom_call_target="tpu_custom_call" | custom-call | tf_op jit(solution)/shard_map/pallas_call | solution.py:41
  255.1 0.0 all-to-all-done
  255.1 6.4 %fusion.7 = f32[1024,128,1]{1,0,2:T(8,128)S(1)} fusion(bf16[16,1024,256]{2,1,0:T(8,128)(2,1)} %all-to-all-done, bf16[1024,16]{0,1:T(8,128)(2,1)S(1)} %bitcast.73, f32[16,384,128]{2,1,0:T(8,128)} %bitcast.72), kind=kOutput, calls=%fused_computation.12 | convolution fusion | flops 1077936128 | bytes 9994240 | tf_op jit(solution)/shard_map/dot_general | solution.py:152
  261.6 1.2 fusion.68
  262.8 0.0 copy-start
  262.8 0.2 fusion.15
  263.0 5.7 %multiply_reduce_fusion = f32[1024]{0:T(1024)S(1)} fusion(bf16[16,1024,256]{2,1,0:T(8,128)(2,1)} %all-to-all-done, bf16[1024,16]{0,1:T(8,128)(2,1)S(1)} %bitcast.74), kind=kLoop, calls=%fused_computation | loop fusion | flops 16776192 | bytes 8425472 | tf_op jit(solution)/shard_map/reduce_sum | solution.py:151
  268.7 0.7 bitcast_divide_fusion
  (358 shorter events, 3.8 us)
Async XLA Ops:
  10.1 17.6 %slice-start = ((s8[8388608]{0:T(1024)(128)(4,1)}), s8[4194304]{0:T(1024)(128)(4,1)S(1)}, s32[]{:S(2)}) async-start(s8[8388608]{0:T(1024)(128)(4,1)} %bitcast.67), calls=%async_computation.2 | async-start | bytes 8388608
  25.3 2.5 slice-start.1
  27.7 6.8 %copy-start.2 = (f32[256,128]{1,0:T(8,128)S(1)}, f32[256,128]{1,0:T(8,128)}, u32[]{:S(2)}) copy-start(f32[256,128]{1,0:T(8,128)} %param.8) | copy-start | bytes 393220
  31.2 1.5 collective-permute-start
  32.7 7.0 %collective-permute-start.1 = (f32[384,128]{1,0:T(8,128)S(1)}, f32[384,128]{1,0:T(8,128)S(1)}, u32[]{:S(2)}, u32[]{:S(2)}) collective-permute-start(f32[384,128]{1,0:T(8,128)S(1)} %fusion.36), channel_id=1, source_target_pairs={{0,32},{16,48},{32,0},{48,16},{64,96},{80,112},{96,64},{112,80},{1... | collective-permute-start | bytes 589832 | tf_op jit(solution)/shard_map/ppermute | solution.py:53
  39.8 7.9 %collective-permute-start.2 = (f32[384,128]{1,0:T(8,128)S(1)}, f32[384,128]{1,0:T(8,128)S(1)}, u32[]{:S(2)}, u32[]{:S(2)}) collective-permute-start(f32[384,128]{1,0:T(8,128)S(1)} %add.497), channel_id=1, source_target_pairs={{0,64},{16,80},{32,96},{48,112},{64,0},{80,16},{96,32},{112,48},{1... | collective-permute-start | bytes 589832 | tf_op jit(solution)/shard_map/ppermute | solution.py:53
  69.9 3.7 %collective-permute-start.3 = (f32[1,4,128]{2,1,0:T(4,128)S(1)}, f32[1,4,128]{2,1,0:T(4,128)S(1)}, u32[]{:S(2)}, u32[]{:S(2)}) collective-permute-start(f32[1,4,128]{2,1,0:T(4,128)S(1)} %maximum_bitcast_fusion), channel_id=1, source_target_pairs={{0,1},{1,0},{2,3},{3,2},{4,5},{5,4},{6,7},{7,6},{8,9},{9,8},{10,11... | collective-permute-start | bytes 6152 | tf_op jit(solution)/shard_map/ppermute | solution.py:64
  73.5 5.1 %collective-permute-start.4 = (f32[2,4,128]{2,1,0:T(4,128)S(1)}, f32[2,4,128]{2,1,0:T(4,128)S(1)}, u32[]{:S(2)}, u32[]{:S(2)}) collective-permute-start(f32[2,4,128]{2,1,0:T(4,128)S(1)} %maximum_select_fusion.3), channel_id=1, source_target_pairs={{0,2},{1,3},{2,0},{3,1},{4,6},{5,7},{6,4},{7,5},{8,10},{9,11},{10,... | collective-permute-start | bytes 12296 | tf_op jit(solution)/shard_map/ppermute | solution.py:64
  78.7 3.7 %collective-permute-start.5 = (f32[4,4,128]{2,1,0:T(4,128)S(1)}, f32[4,4,128]{2,1,0:T(4,128)S(1)}, u32[]{:S(2)}, u32[]{:S(2)}) collective-permute-start(f32[4,4,128]{2,1,0:T(4,128)S(1)} %maximum_select_fusion.2), channel_id=1, source_target_pairs={{0,4},{1,5},{2,6},{3,7},{4,0},{5,1},{6,2},{7,3},{8,12},{9,13},{10,... | collective-permute-start | bytes 24584 | tf_op jit(solution)/shard_map/ppermute | solution.py:64
  82.3 9.3 %collective-permute-start.6 = (f32[8,4,128]{2,1,0:T(4,128)S(1)}, f32[8,4,128]{2,1,0:T(4,128)S(1)}, u32[]{:S(2)}, u32[]{:S(2)}) collective-permute-start(f32[8,4,128]{2,1,0:T(4,128)S(1)} %maximum_select_fusion.1), channel_id=1, source_target_pairs={{0,8},{1,9},{2,10},{3,11},{4,12},{5,13},{6,14},{7,15},{8,0},{9,1},... | collective-permute-start | bytes 49160 | tf_op jit(solution)/shard_map/ppermute | solution.py:64
  86.2 6.7 %copy-start.3 = (f32[1,128,128]{2,1,0:T(8,128)S(1)}, f32[1,128,128]{2,1,0:T(8,128)}, u32[]{:S(2)}) copy-start(f32[1,128,128]{2,1,0:T(8,128)} %shard_map.68) | copy-start | bytes 196612
  86.3 168.9 %all-to-all-start = ((bf16[16,1024,256]{2,1,0:T(8,128)(2,1)}), bf16[16,1024,256]{2,1,0:T(8,128)(2,1)}, u32[]{:S(2)}, u32[]{:S(2)}) async-start(bf16[16,1024,256]{2,1,0:T(8,128)(2,1)} %bitcast.66), calls=%async_computation | async-start | bytes 16777216 | tf_op jit(solution)/shard_map/all_to_all | solution.py:94
  91.3 122.4 %all-gather.3.cloned.1.call-start = ((), (), s32[]{:S(2)}) async-start(), calls=%async_computation.1 | async-start | bytes 3342336 | tf_op jit(solution)/shard_map/all_gather | solution.py:142
  255.1 6.5 %copy-start.1 = (f32[8,128,128]{2,1,0:T(8,128)S(1)}, f32[8,128,128]{2,1,0:T(8,128)}, u32[]{:S(2)}) copy-start(f32[8,128,128]{2,1,0:T(8,128)} %shard_map.69) | copy-start | bytes 1572868
  262.8 6.6 %copy-start = (f32[8,128,128]{2,1,0:T(8,128)}, f32[8,128,128]{2,1,0:T(8,128)S(1)}, u32[]{:S(2)}) copy-start(f32[8,128,128]{2,1,0:T(8,128)S(1)} %fusion.68) | copy-start | bytes 1572868
Sparse Core Ops, SparseCore 0:
  94.8 118.7 all-gather.2

commit v6 on v5

--- a/solution.py
+++ b/solution.py
@@ -114,6 +114,7 @@
     information = summed[window_len:]
     identity = jnp.eye(factors, dtype=jnp.float32)
     covariance = spd_inverse((identity + information)[None])[0]
+    cov_all = lax.all_gather(covariance, "tm", axis=0, tiled=False)
     local_est = jnp.dot(info_vec, covariance, precision=HIGH)
     fwd_gain, fwd_local = lax.associative_scan(compose, (decay, local_est), axis=0)
     back_gain, back_local = lax.associative_scan(
@@ -135,23 +136,18 @@
         jnp.bfloat16
     )
     mask_mine = lax.dynamic_slice_in_dim(tile_mask, time_index * blocks_share, blocks_share, 0)
-    squares = lax.dot_general(
-        smoothed, smoothed, (((0,), (0,)), ((), ())), preferred_element_type=jnp.float32
+    smooth_win = lax.all_gather(smoothed, "tm", axis=0, tiled=False)
+    smooth_all = smooth_win.reshape(time_count * window_len, factors)
+    all_moments = (
+        jnp.einsum("wtk,wtj->wkj", smooth_win, smooth_win, preferred_element_type=jnp.float32)
+        + window_len * cov_all
     )
-    moment = squares + window_len * covariance
-    gathered = lax.all_gather(
-        jnp.concatenate([smoothed.astype(jnp.float32), moment], 0), "tm", axis=0, tiled=False
-    )
-    smooth_all = gathered[:, :window_len].reshape(time_count * window_len, factors)
-    all_moments = gathered[:, window_len:]
     mask_full = jnp.broadcast_to(
         mask_mine[:, None, :, None], (blocks_share, BLOCK, time_count, window_len)
     ).reshape(blocks_share * BLOCK, time_count * window_len)
     observed = obs_mine * mask_full.astype(jnp.bfloat16)
     sq_mine = jnp.sum(jnp.square(observed.astype(jnp.float32)), axis=1)
-    cross_mine = jnp.dot(
-        observed, smooth_all.astype(jnp.bfloat16), preferred_element_type=jnp.float32
-    )
+    cross_mine = jnp.dot(observed, smooth_all, preferred_element_type=jnp.float32)
     moment_mine = jnp.einsum("bw,wij->bij", mask_mine, all_moments, precision=HIGH)
     counts_mine = jnp.sum(mask_mine, axis=1)
     cross_blocks = cross_mine.reshape(blocks_share, BLOCK, factors)

time: 278 us -> 318 us (1.14)
  waiting for transfers between devices: 136 us -> 177 us
    all_gather x1 -> x2, waiting for transfers between devices: 119 us -> 159 us  [the longest x1 115 us: per_device(): cov_all = lax.all_gather(covariance, 'tm', axis=0, tiled=False)]
  transfers between devices with their start and end apart: 9 -> 10, of which waited for: 7 -> 8; matrix products, arithmetic and copies ran while one was open for 2% -> 2% of each run, Pallas kernels for 14% -> 12%
where the time goes in v6:
time: 318 us; the launch traced here: 317 us
  waiting for transfers between devices  177 us (56%)
  Pallas kernels  54.7 us (17%)
  other arithmetic  24.3 us (8%)
  starting transfers between devices  21 us (7%)
  matrix products  19.6 us (6%)
  between operations  15.9 us (5%)
  local copies, waits for them, and re-layouts  5.02 us (2%)
    all_gather x1, waiting for transfers between devices, per_device(): cov_all = lax.all_gather(covariance, 'tm', axis=0, tiled=False)  115 us
    pallas_call x2, Pallas kernels, spd_inverse(): pl.pallas_call(_gauss_jordan, out_shape=jax.ShapeDtypeStruct(a.shape, jnp...  54.7 us
    all_gather x1, waiting for transfers between devices, per_device(): smooth_win = lax.all_gather(smoothed, 'tm', axis=0, tiled=False)  44.3 us
    convert_element_type x1, other arithmetic, per_device(): (loadings - loadings_hi.astype(jnp.float32)).astype(jnp.bfloat16)  15.1 us
    ppermute x3, waiting for transfers between devices, butterfly_sum(): part = part + lax.ppermute(part, axis, pairs)  10.9 us
    ppermute x4, starting transfers between devices, butterfly_gather(): other = lax.ppermute(held, axis, pairs)  10.6 us
  transfers between devices with their start and end apart: 10, of which 8 were waited for; matrix products, arithmetic and copies ran while one was open for 2% of the time, Pallas kernels for 12%

profile of v6, /device:TPU:0, one launch (start us, length us, event | category | flops | bytes accessed | tf_op | source)
XLA Modules:
  0.0 317.2 jit_solution(18288571378562702974)
XLA Ops:
  7.2 1.1 fusion.41
  8.2 1.8 fusion.8
  10.1 0.1 broadcast_bitcast_fusion
  10.1 0.0 slice-start
  10.1 15.1 %subtract_convert_fusion = (bf16[16384,128]{1,0:T(8,128)(2,1)S(1)}, bf16[16384,128]{1,0:T(8,128)(2,1)S(1)}, bf16[16384,128]{1,0:T(8,128)(2,1)S(1)}, bf16[16384,128]{1,0:T(8,128)(2,1)S(1)}) fusion(f32[16384,128]{1,0:T(8,128)} %param.6, f32[16384]{0:T(1024)S(1)} %broadcast_bitcast_fusion, f32[16384]{0:T(1024)} %param.7), kind=kLoop, calls=%fused_computation.9 | loop fusion | flops 20971520 | bytes 25296896 | tf_op jit(solution)/shard_map/convert_element_type | solution.py:102
  25.3 0.0 slice-start.1
  25.3 2.4 fusion
  27.7 0.0 copy-start.2
  27.8 3.4 %convolution_bitcast_fusion = f32[256,128]{1,0:T(8,128)S(1)} fusion(bf16[16384,128]{1,0:T(8,128)(2,1)S(1)} %get-tuple-element.7, bf16[16384,256]{1,0:T(8,128)(2,1)S(1)} %bitcast.66), kind=kOutput, calls=%fused_computation.19 | convolution fusion | flops 1073741824 | bytes 12713984 | tf_op jit(solution)/shard_map/dot_general | solution.py:97
  31.2 0.1 collective-permute-start
  31.3 1.4 collective-permute-done
  32.7 1.8 collective-permute-start.1
  34.7 5.1 %collective-permute-done.1 = f32[384,128]{1,0:T(8,128)S(1)} collective-permute-done((f32[384,128]{1,0:T(8,128)S(1)}, f32[384,128]{1,0:T(8,128)S(1)}, u32[]{:S(2)}, u32[]{:S(2)}) %collective-permute-start.1) | collective-permute-done | bytes 196640 | tf_op jit(solution)/shard_map/ppermute | solution.py:53
  39.8 3.6 %collective-permute-start.2 = (f32[384,128]{1,0:T(8,128)S(1)}, f32[384,128]{1,0:T(8,128)S(1)}, u32[]{:S(2)}, u32[]{:S(2)}) collective-permute-start(f32[384,128]{1,0:T(8,128)S(1)} %add.497), channel_id=1, source_target_pairs={{0,64},{16,80},{32,96},{48,112},{64,0},{80,16},{96,32},{112,48},{1... | collective-permute-start | bytes 589832 | tf_op jit(solution)/shard_map/ppermute | solution.py:53
  43.4 4.3 %collective-permute-done.2 = f32[384,128]{1,0:T(8,128)S(1)} collective-permute-done((f32[384,128]{1,0:T(8,128)S(1)}, f32[384,128]{1,0:T(8,128)S(1)}, u32[]{:S(2)}, u32[]{:S(2)}) %collective-permute-start.2) | collective-permute-done | bytes 196640 | tf_op jit(solution)/shard_map/ppermute | solution.py:53
  47.7 0.6 fusion.21.a_ref
  48.4 16.7 %shard_map.68 = f32[1,128,128]{2,1,0:T(8,128)} custom-call(f32[1,128,128]{2,1,0:T(8,128)} %fusion.21.a_ref), custom_call_target="tpu_custom_call" | custom-call | tf_op jit(solution)/shard_map/pallas_call | solution.py:41
  65.0 1.1 fusion.17
  69.9 1.6 collective-permute-start.3
  71.5 2.1 collective-permute-done.3
  73.5 3.1 collective-permute-start.4
  76.6 2.1 collective-permute-done.4
  78.7 2.0 collective-permute-start.5
  80.6 1.7 collective-permute-done.5
  82.3 3.9 %collective-permute-start.6 = (f32[8,4,128]{2,1,0:T(4,128)S(1)}, f32[8,4,128]{2,1,0:T(4,128)S(1)}, u32[]{:S(2)}, u32[]{:S(2)}) collective-permute-start(f32[8,4,128]{2,1,0:T(4,128)S(1)} %maximum_select_fusion.1), channel_id=1, source_target_pairs={{0,8},{1,9},{2,10},{3,11},{4,12},{5,13},{6,14},{7,15},{8,0},{9,1},... | collective-permute-start | bytes 49160 | tf_op jit(solution)/shard_map/ppermute | solution.py:64
  86.2 4.9 %all-to-all-start = ((bf16[16,1024,256]{2,1,0:T(8,128)(2,1)}), bf16[16,1024,256]{2,1,0:T(8,128)(2,1)}, u32[]{:S(2)}, u32[]{:S(2)}) async-start(bf16[16,1024,256]{2,1,0:T(8,128)(2,1)} %bitcast.64), calls=%async_computation | async-start | bytes 16777216 | tf_op jit(solution)/shard_map/all_to_all | solution.py:94
  91.2 0.0 all-gather.4.cloned.1.call-start
  91.3 0.6 all-gather.4.cloned.1.call-update
  91.9 0.0 all-gather.6.cloned.1.call-start
  91.9 0.1 rev.13
  92.0 0.1 rev.12
  92.1 0.0 collective-permute-done.6
  93.4 0.7 multiply_convert_fusion
  94.1 0.0 all-gather.6.cloned.1.call-update
  94.1 0.1 dynamic-slice_convert_fusion
  94.2 0.1 broadcast_in_dim.23
  94.3 0.1 dynamic-slice_reduce_fusion
  94.4 115.2 %all-gather.4.cloned.1.call-done = f32[16,128,128]{2,1,0:T(8,128)} async-done(((f32[1,128,128]{2,1,0:T(8,128)}), f32[16,128,128]{2,1,0:T(8,128)}) %all-gather.4.cloned.1.call-update) | async-done | bytes 1048592 | tf_op jit(solution)/shard_map/all_gather | solution.py:117
  209.7 44.3 %all-gather.6.cloned.1.call-done = bf16[4096,128]{1,0:T(8,128)(2,1)} async-done(((bf16[256,128]{1,0:T(8,128)(2,1)}), bf16[4096,128]{1,0:T(8,128)(2,1)}) %all-gather.6.cloned.1.call-update) | async-done | bytes 1048592 | tf_op jit(solution)/shard_map/all_gather | solution.py:139
  253.9 2.3 convolution_add_fusion
  256.3 1.2 fusion.13
  257.5 0.9 copy.19.a_ref
  258.4 38.0 %shard_map.69 = f32[8,128,128]{2,1,0:T(8,128)} custom-call(f32[8,128,128]{2,1,0:T(8,128)} %copy.19.a_ref), custom_call_target="tpu_custom_call" | custom-call | tf_op jit(solution)/shard_map/pallas_call | solution.py:41
  296.4 6.1 %fusion.7 = f32[1024,128,1]{1,0,2:T(8,128)S(1)} fusion(bf16[16,256,128]{2,1,0:T(8,128)(2,1)} %bitcast.68, bf16[16,1024,256]{2,1,0:T(8,128)(2,1)} %all-to-all-done, bf16[1024,16]{0,1:T(8,128)(2,1)S(1)} %bitcast.71), kind=kOutput, calls=%fused_computation.12 | convolution fusion | flops 1077936128 | bytes 9994240 | tf_op jit(solution)/shard_map/dot_general | solution.py:150
  302.5 1.2 fusion.60
  303.7 0.2 fusion.15
  304.0 5.7 %multiply_reduce_fusion = f32[1024]{0:T(1024)S(1)} fusion(bf16[16,1024,256]{2,1,0:T(8,128)(2,1)} %all-to-all-done, bf16[1024,16]{0,1:T(8,128)(2,1)S(1)} %bitcast.72), kind=kLoop, calls=%fused_computation | loop fusion | flops 16776192 | bytes 8425472 | tf_op jit(solution)/shard_map/reduce_sum | solution.py:149
  309.6 0.7 bitcast_divide_fusion
  (357 shorter events, 3.8 us)
Async XLA Ops:
  10.1 17.6 %slice-start = ((s8[8388608]{0:T(1024)(128)(4,1)}), s8[4194304]{0:T(1024)(128)(4,1)S(1)}, s32[]{:S(2)}) async-start(s8[8388608]{0:T(1024)(128)(4,1)} %bitcast.65), calls=%async_computation.3 | async-start | bytes 8388608
  25.3 2.5 slice-start.1
  27.7 6.8 %copy-start.2 = (f32[256,128]{1,0:T(8,128)S(1)}, f32[256,128]{1,0:T(8,128)}, u32[]{:S(2)}) copy-start(f32[256,128]{1,0:T(8,128)} %param.8) | copy-start | bytes 393220
  31.2 1.5 collective-permute-start
  32.7 7.0 %collective-permute-start.1 = (f32[384,128]{1,0:T(8,128)S(1)}, f32[384,128]{1,0:T(8,128)S(1)}, u32[]{:S(2)}, u32[]{:S(2)}) collective-permute-start(f32[384,128]{1,0:T(8,128)S(1)} %fusion.36), channel_id=1, source_target_pairs={{0,32},{16,48},{32,0},{48,16},{64,96},{80,112},{96,64},{112,80},{1... | collective-permute-start | bytes 589832 | tf_op jit(solution)/shard_map/ppermute | solution.py:53
  39.8 7.9 %collective-permute-start.2 = (f32[384,128]{1,0:T(8,128)S(1)}, f32[384,128]{1,0:T(8,128)S(1)}, u32[]{:S(2)}, u32[]{:S(2)}) collective-permute-start(f32[384,128]{1,0:T(8,128)S(1)} %add.497), channel_id=1, source_target_pairs={{0,64},{16,80},{32,96},{48,112},{64,0},{80,16},{96,32},{112,48},{1... | collective-permute-start | bytes 589832 | tf_op jit(solution)/shard_map/ppermute | solution.py:53
  69.9 3.7 %collective-permute-start.3 = (f32[1,4,128]{2,1,0:T(4,128)S(1)}, f32[1,4,128]{2,1,0:T(4,128)S(1)}, u32[]{:S(2)}, u32[]{:S(2)}) collective-permute-start(f32[1,4,128]{2,1,0:T(4,128)S(1)} %maximum_bitcast_fusion), channel_id=1, source_target_pairs={{0,1},{1,0},{2,3},{3,2},{4,5},{5,4},{6,7},{7,6},{8,9},{9,8},{10,11... | collective-permute-start | bytes 6152 | tf_op jit(solution)/shard_map/ppermute | solution.py:64
  73.5 5.1 %collective-permute-start.4 = (f32[2,4,128]{2,1,0:T(4,128)S(1)}, f32[2,4,128]{2,1,0:T(4,128)S(1)}, u32[]{:S(2)}, u32[]{:S(2)}) collective-permute-start(f32[2,4,128]{2,1,0:T(4,128)S(1)} %maximum_select_fusion.3), channel_id=1, source_target_pairs={{0,2},{1,3},{2,0},{3,1},{4,6},{5,7},{6,4},{7,5},{8,10},{9,11},{10,... | collective-permute-start | bytes 12296 | tf_op jit(solution)/shard_map/ppermute | solution.py:64
  78.7 3.7 %collective-permute-start.5 = (f32[4,4,128]{2,1,0:T(4,128)S(1)}, f32[4,4,128]{2,1,0:T(4,128)S(1)}, u32[]{:S(2)}, u32[]{:S(2)}) collective-permute-start(f32[4,4,128]{2,1,0:T(4,128)S(1)} %maximum_select_fusion.2), channel_id=1, source_target_pairs={{0,4},{1,5},{2,6},{3,7},{4,0},{5,1},{6,2},{7,3},{8,12},{9,13},{10,... | collective-permute-start | bytes 24584 | tf_op jit(solution)/shard_map/ppermute | solution.py:64
  82.3 9.8 %collective-permute-start.6 = (f32[8,4,128]{2,1,0:T(4,128)S(1)}, f32[8,4,128]{2,1,0:T(4,128)S(1)}, u32[]{:S(2)}, u32[]{:S(2)}) collective-permute-start(f32[8,4,128]{2,1,0:T(4,128)S(1)} %maximum_select_fusion.1), channel_id=1, source_target_pairs={{0,8},{1,9},{2,10},{3,11},{4,12},{5,13},{6,14},{7,15},{8,0},{9,1},... | collective-permute-start | bytes 49160 | tf_op jit(solution)/shard_map/ppermute | solution.py:64
  86.2 210.2 %all-to-all-start = ((bf16[16,1024,256]{2,1,0:T(8,128)(2,1)}), bf16[16,1024,256]{2,1,0:T(8,128)(2,1)}, u32[]{:S(2)}, u32[]{:S(2)}) async-start(bf16[16,1024,256]{2,1,0:T(8,128)(2,1)} %bitcast.64), calls=%async_computation | async-start | bytes 16777216 | tf_op jit(solution)/shard_map/all_to_all | solution.py:94
  91.2 118.5 %all-gather.4.cloned.1.call-start = ((), (), s32[]{:S(2)}) async-start(), calls=%async_computation.1 | async-start | bytes 1114112 | tf_op jit(solution)/shard_map/all_gather | solution.py:117
  91.9 162.0 %all-gather.6.cloned.1.call-start = ((), (), s32[]{:S(2)}) async-start(), calls=%async_computation.2 | async-start | bytes 1114112 | tf_op jit(solution)/shard_map/all_gather | solution.py:139
  296.4 6.1 %copy-start.1 = (f32[8,128,128]{2,1,0:T(8,128)S(1)}, f32[8,128,128]{2,1,0:T(8,128)}, u32[]{:S(2)}) copy-start(f32[8,128,128]{2,1,0:T(8,128)} %shard_map.69) | copy-start | bytes 1572868
  303.7 6.6 %copy-start = (f32[8,128,128]{2,1,0:T(8,128)}, f32[8,128,128]{2,1,0:T(8,128)S(1)}, u32[]{:S(2)}) copy-start(f32[8,128,128]{2,1,0:T(8,128)S(1)} %fusion.60) | copy-start | bytes 1572868
Sparse Core Ops, SparseCore 0:
  94.1 115.5 all-gather.3
  212.4 41.5 all-gather.5

commit v7 on v5

--- a/solution.py
+++ b/solution.py
@@ -38,11 +38,15 @@
 
 
 def spd_inverse(a):
+    batch, n, _ = a.shape
     return pl.pallas_call(
         _gauss_jordan,
         out_shape=jax.ShapeDtypeStruct(a.shape, jnp.float32),
         in_specs=[pl.BlockSpec(memory_space=pltpu.VMEM)],
         out_specs=pl.BlockSpec(memory_space=pltpu.VMEM),
+        cost_estimate=pl.CostEstimate(
+            flops=8 * batch * n * n * n, transcendentals=0, bytes_accessed=8 * batch * n * n
+        ),
     )(a)
 
 
@@ -92,11 +96,8 @@
     present = lax.dynamic_index_in_dim(tile_mask, time_index, 1, keepdims=False)
     sensor_mask = jnp.repeat(present, BLOCK)
     obs_mine = lax.all_to_all(observations, "tm", 0, 1, tiled=True)
-    weighted = loadings / noise_var[:, None] * sensor_mask[:, None]
+    weighted = loadings * (1.0 / noise_var)[:, None] * sensor_mask[:, None]
     scaled = weighted.astype(jnp.bfloat16)
-    info_part = lax.dot_general(
-        observations, scaled, (((0,), (0,)), ((), ())), preferred_element_type=jnp.float32
-    )
     weighted_lo = (weighted - scaled.astype(jnp.float32)).astype(jnp.bfloat16)
     loadings_hi = loadings.astype(jnp.bfloat16)
     loadings_lo = (loadings - loadings_hi.astype(jnp.float32)).astype(jnp.bfloat16)
@@ -109,9 +110,11 @@
     gram_part = (
         split[:factors, :factors] + split[:factors, factors:] + split[factors:, :factors]
     )
-    summed = butterfly_sum(jnp.concatenate([info_part, gram_part], 0), "sens", sens_count)
-    info_vec = summed[:window_len]
-    information = summed[window_len:]
+    information = butterfly_sum(gram_part, "sens", sens_count)
+    info_part = lax.dot_general(
+        observations, scaled, (((0,), (0,)), ((), ())), preferred_element_type=jnp.float32
+    )
+    info_vec = butterfly_sum(info_part, "sens", sens_count)
     identity = jnp.eye(factors, dtype=jnp.float32)
     covariance = spd_inverse((identity + information)[None])[0]
     local_est = jnp.dot(info_vec, covariance, precision=HIGH)

time: 278 us -> 272 us (0.978)
  waiting for transfers between devices: 136 us -> 133 us
    ppermute x3 -> x6, waiting for transfers between devices: 10.9 us -> 6.72 us  [butterfly_sum(): part = part + lax.ppermute(part, axis, pairs)]
    convert_element_type x1, other arithmetic: 15.1 us -> 11.5 us  [per_device(): (loadings - loadings_hi.astype(jnp.float32)).astype(jnp.bfloat16)]
    ppermute x3 -> x6, starting transfers between devices: 5.42 us -> 7.74 us  [butterfly_sum(): part = part + lax.ppermute(part, axis, pairs)]
  transfers between devices with their start and end apart: 9 -> 12, of which waited for: 7 -> 6; matrix products, arithmetic and copies ran while one was open for 2% -> 3% of each run, Pallas kernels for 14% -> 20%
where the time goes in v7:
time: 272 us; the launch traced here: 271 us
  waiting for transfers between devices  133 us (49%)
  Pallas kernels  54.7 us (20%)
  starting transfers between devices  23.2 us (9%)
  other arithmetic  21.6 us (8%)
  matrix products  16 us (6%)
  between operations  15.9 us (6%)
  local copies, waits for them, and re-layouts  6.34 us (2%)
    all_gather x1, waiting for transfers between devices, per_device(): lax.all_gather(jnp.concatenate([smoothed.astype(jnp.float32), moment], 0)...  120 us
    pallas_call x2, Pallas kernels, spd_inverse(): pl.pallas_call(_gauss_jordan, out_shape=jax.ShapeDtypeStruct(a.shape, jnp...  54.7 us
    convert_element_type x1, other arithmetic, per_device(): (loadings - loadings_hi.astype(jnp.float32)).astype(jnp.bfloat16)  11.5 us
    ppermute x4, starting transfers between devices, butterfly_gather(): other = lax.ppermute(held, axis, pairs)  10.4 us
    ppermute x6, starting transfers between devices, butterfly_sum(): part = part + lax.ppermute(part, axis, pairs)  7.74 us
    ppermute x6, waiting for transfers between devices, butterfly_sum(): part = part + lax.ppermute(part, axis, pairs)  6.72 us
    dot_general x1, matrix products, per_device(): jnp.dot(observed, smooth_all.astype(jnp.bfloat16), preferred_element_type...  6.44 us
    ppermute x4, waiting for transfers between devices, butterfly_gather(): other = lax.ppermute(held, axis, pairs)  5.92 us
  transfers between devices with their start and end apart: 12, of which 6 were waited for; matrix products, arithmetic and copies ran while one was open for 3% of the time, Pallas kernels for 20%

profile of v7, /device:TPU:0, one launch (start us, length us, event | category | flops | bytes accessed | tf_op | source)
XLA Modules:
  0.0 270.5 jit_solution(13003493997881359888)
XLA Ops:
  7.2 1.1 fusion.40
  8.2 1.8 fusion.9
  10.1 0.1 broadcast_bitcast_fusion
  10.1 0.9 broadcast_divide_fusion
  11.0 0.0 slice-start
  11.0 11.5 %subtract_convert_fusion = (bf16[16384,128]{1,0:T(8,128)(2,1)S(1)}, bf16[16384,128]{1,0:T(8,128)(2,1)S(1)}, bf16[16384,128]{1,0:T(8,128)(2,1)S(1)}, bf16[16384,128]{1,0:T(8,128)(2,1)S(1)}) fusion(f32[16384,128]{1,0:T(8,128)} %param.6, f32[16384]{0:T(1024)S(1)} %broadcast_bitcast_fusion, f32[16384]{0:T(1024)S(1)} %broadcast_divide_fusion), kind=kLoop, calls=%fused_computation.9 | loop fusion | flops 20971520 | bytes 25296896 | tf_op jit(solution)/shard_map/convert_element_type | solution.py:103
  22.5 0.0 slice-start.1
  22.5 2.4 fusion
  24.9 0.1 collective-permute-start.3
  25.1 1.5 convolution_bitcast_fusion
  26.6 0.6 collective-permute-start
  27.2 1.8 collective-permute-start.4
  28.9 2.6 collective-permute-done.4
  31.5 3.4 %collective-permute-start.5 = (f32[128,128]{1,0:T(8,128)S(1)}, f32[128,128]{1,0:T(8,128)S(1)}, u32[]{:S(2)}, u32[]{:S(2)}) collective-permute-start(f32[128,128]{1,0:T(8,128)S(1)} %add.509), channel_id=1, source_target_pairs={{0,64},{16,80},{32,96},{48,112},{64,0},{80,16},{96,32},{112,48},{1... | collective-permute-start | bytes 196616 | tf_op jit(solution)/shard_map/ppermute | solution.py:57
  34.9 0.8 collective-permute-start.1
  35.9 4.1 %collective-permute-done.1 = f32[256,128]{0,1:T(8,128)S(1)} collective-permute-done((f32[256,128]{0,1:T(8,128)S(1)}, f32[256,128]{0,1:T(8,128)S(1)}, u32[]{:S(2)}, u32[]{:S(2)}) %collective-permute-start.1) | collective-permute-done | bytes 131104 | tf_op jit(solution)/shard_map/ppermute | solution.py:57
  40.0 1.2 collective-permute-start.2
  41.2 0.6 add_bitcast_fusion.a_ref
  41.8 16.7 %shard_map.68 = f32[1,128,128]{2,1,0:T(8,128)} custom-call(f32[1,128,128]{2,1,0:T(8,128)} %add_bitcast_fusion.a_ref), custom_call_target="tpu_custom_call" | custom-call | flops 16777216 | bytes 131072 | tf_op jit(solution)/shard_map/pallas_call | solution.py:42
  58.5 1.2 fusion.18
  63.5 1.6 collective-permute-start.6
  65.1 2.1 collective-permute-done.6
  67.2 3.0 %collective-permute-start.7 = (f32[2,4,128]{2,1,0:T(4,128)S(1)}, f32[2,4,128]{2,1,0:T(4,128)S(1)}, u32[]{:S(2)}, u32[]{:S(2)}) collective-permute-start(f32[2,4,128]{2,1,0:T(4,128)S(1)} %maximum_select_fusion.3), channel_id=1, source_target_pairs={{0,2},{1,3},{2,0},{3,1},{4,6},{5,7},{6,4},{7,5},{8,10},{9,11},{10,... | collective-permute-start | bytes 12296 | tf_op jit(solution)/shard_map/ppermute | solution.py:68
  70.2 2.1 collective-permute-done.7
  72.3 1.9 collective-permute-start.8
  74.2 1.7 collective-permute-done.8
  75.9 3.9 %collective-permute-start.9 = (f32[8,4,128]{2,1,0:T(4,128)S(1)}, f32[8,4,128]{2,1,0:T(4,128)S(1)}, u32[]{:S(2)}, u32[]{:S(2)}) collective-permute-start(f32[8,4,128]{2,1,0:T(4,128)S(1)} %maximum_select_fusion.1), channel_id=1, source_target_pairs={{0,8},{1,9},{2,10},{3,11},{4,12},{5,13},{6,14},{7,15},{8,0},{9,1},... | collective-permute-start | bytes 49160 | tf_op jit(solution)/shard_map/ppermute | solution.py:68
  79.8 5.0 %all-to-all-start = ((bf16[16,1024,256]{2,1,0:T(8,128)(2,1)}), bf16[16,1024,256]{2,1,0:T(8,128)(2,1)}, u32[]{:S(2)}, u32[]{:S(2)}) async-start(bf16[16,1024,256]{2,1,0:T(8,128)(2,1)} %bitcast.66), calls=%async_computation | async-start | bytes 16777216 | tf_op jit(solution)/shard_map/all_to_all | solution.py:98
  84.9 0.0 all-gather.3.cloned.1.call-start
  85.0 0.1 rev.13
  85.1 0.1 rev.12
  86.5 0.1 fusion.36
  86.5 0.2 convolution_add_fusion
  86.7 0.7 pad_maximum_fusion
  87.4 0.0 all-gather.3.cloned.1.call-update
  87.5 0.1 dynamic-slice_convert_fusion
  87.5 0.1 broadcast_in_dim.23
  87.6 0.1 dynamic-slice_reduce_fusion
  87.8 120.2 %all-gather.3.cloned.1.call-done = f32[6144,128]{1,0:T(8,128)} async-done(((f32[384,128]{1,0:T(8,128)}), f32[6144,128]{1,0:T(8,128)}) %all-gather.3.cloned.1.call-update) | async-done | bytes 3145744 | tf_op jit(solution)/shard_map/all_gather | solution.py:145
  208.0 1.3 slice.1022
  209.3 1.2 fusion.14
  210.5 0.9 copy.12.a_ref
  211.4 38.0 %shard_map.69 = f32[8,128,128]{2,1,0:T(8,128)} custom-call(f32[8,128,128]{2,1,0:T(8,128)} %copy.12.a_ref), custom_call_target="tpu_custom_call" | custom-call | flops 134217728 | bytes 1048576 | tf_op jit(solution)/shard_map/pallas_call | solution.py:42
  249.4 6.4 %fusion.8 = f32[1024,128,1]{1,0,2:T(8,128)S(1)} fusion(bf16[16,1024,256]{2,1,0:T(8,128)(2,1)} %all-to-all-done, bf16[1024,16]{0,1:T(8,128)(2,1)S(1)} %bitcast.73, f32[16,384,128]{2,1,0:T(8,128)} %bitcast.72), kind=kOutput, calls=%fused_computation.13 | convolution fusion | flops 1077936128 | bytes 9994240 | tf_op jit(solution)/shard_map/dot_general | solution.py:155
  255.9 1.2 fusion.66
  257.1 0.2 fusion.16
  257.3 5.7 %multiply_reduce_fusion = f32[1024]{0:T(1024)S(1)} fusion(bf16[16,1024,256]{2,1,0:T(8,128)(2,1)} %all-to-all-done, bf16[1024,16]{0,1:T(8,128)(2,1)S(1)} %bitcast.74), kind=kLoop, calls=%fused_computation | loop fusion | flops 16776192 | bytes 8425472 | tf_op jit(solution)/shard_map/reduce_sum | solution.py:154
  263.0 0.7 bitcast_divide_fusion
  (365 shorter events, 3.8 us)
Async XLA Ops:
  11.0 14.0 %slice-start = ((s8[8388608]{0:T(1024)(128)(4,1)}), s8[4194304]{0:T(1024)(128)(4,1)S(1)}, s32[]{:S(2)}) async-start(s8[8388608]{0:T(1024)(128)(4,1)} %bitcast.67), calls=%async_computation.2 | async-start | bytes 8388608
  22.5 2.5 slice-start.1
  24.9 10.8 %copy-start.2 = (f32[256,128]{1,0:T(8,128)S(1)}, f32[256,128]{1,0:T(8,128)}, u32[]{:S(2)}) copy-start(f32[256,128]{1,0:T(8,128)} %param.8) | copy-start | bytes 393220
  24.9 2.2 collective-permute-start.3
  26.6 8.3 %collective-permute-start = (f32[256,128]{0,1:T(8,128)S(1)}, f32[256,128]{0,1:T(8,128)S(1)}, u32[]{:S(2)}, u32[]{:S(2)}) collective-permute-start(f32[256,128]{0,1:T(8,128)S(1)} %convolution_bitcast_fusion), channel_id=1, source_target_pairs={{0,16},{16,0},{32,48},{48,32},{64,80},{80,64},{96,112},{112,96},{1... | collective-permute-start | bytes 393224 | tf_op jit(solution)/shard_map/ppermute | solution.py:57
  27.2 4.3 %collective-permute-start.4 = (f32[128,128]{1,0:T(8,128)S(1)}, f32[128,128]{1,0:T(8,128)S(1)}, u32[]{:S(2)}, u32[]{:S(2)}) collective-permute-start(f32[128,128]{1,0:T(8,128)S(1)} %fusion.73), channel_id=1, source_target_pairs={{0,32},{16,48},{32,0},{48,16},{64,96},{80,112},{96,64},{112,80},{1... | collective-permute-start | bytes 196616 | tf_op jit(solution)/shard_map/ppermute | solution.py:57
  31.5 9.7 %collective-permute-start.5 = (f32[128,128]{1,0:T(8,128)S(1)}, f32[128,128]{1,0:T(8,128)S(1)}, u32[]{:S(2)}, u32[]{:S(2)}) collective-permute-start(f32[128,128]{1,0:T(8,128)S(1)} %add.509), channel_id=1, source_target_pairs={{0,64},{16,80},{32,96},{48,112},{64,0},{80,16},{96,32},{112,48},{1... | collective-permute-start | bytes 196616 | tf_op jit(solution)/shard_map/ppermute | solution.py:57
  34.9 5.0 %collective-permute-start.1 = (f32[256,128]{0,1:T(8,128)S(1)}, f32[256,128]{0,1:T(8,128)S(1)}, u32[]{:S(2)}, u32[]{:S(2)}) collective-permute-start(f32[256,128]{0,1:T(8,128)S(1)} %add.503), channel_id=1, source_target_pairs={{0,32},{16,48},{32,0},{48,16},{64,96},{80,112},{96,64},{112,80},{1... | collective-permute-start | bytes 393224 | tf_op jit(solution)/shard_map/ppermute | solution.py:57
  40.0 18.5 %collective-permute-start.2 = (f32[256,128]{0,1:T(8,128)S(1)}, f32[256,128]{0,1:T(8,128)S(1)}, u32[]{:S(2)}, u32[]{:S(2)}) collective-permute-start(f32[256,128]{0,1:T(8,128)S(1)} %add.504), channel_id=1, source_target_pairs={{0,64},{16,80},{32,96},{48,112},{64,0},{80,16},{96,32},{112,48},{1... | collective-permute-start | bytes 393224 | tf_op jit(solution)/shard_map/ppermute | solution.py:57
  63.5 3.7 %collective-permute-start.6 = (f32[1,4,128]{2,1,0:T(4,128)S(1)}, f32[1,4,128]{2,1,0:T(4,128)S(1)}, u32[]{:S(2)}, u32[]{:S(2)}) collective-permute-start(f32[1,4,128]{2,1,0:T(4,128)S(1)} %maximum_bitcast_fusion), channel_id=1, source_target_pairs={{0,1},{1,0},{2,3},{3,2},{4,5},{5,4},{6,7},{7,6},{8,9},{9,8},{10,11... | collective-permute-start | bytes 6152 | tf_op jit(solution)/shard_map/ppermute | solution.py:68
  67.2 5.1 %collective-permute-start.7 = (f32[2,4,128]{2,1,0:T(4,128)S(1)}, f32[2,4,128]{2,1,0:T(4,128)S(1)}, u32[]{:S(2)}, u32[]{:S(2)}) collective-permute-start(f32[2,4,128]{2,1,0:T(4,128)S(1)} %maximum_select_fusion.3), channel_id=1, source_target_pairs={{0,2},{1,3},{2,0},{3,1},{4,6},{5,7},{6,4},{7,5},{8,10},{9,11},{10,... | collective-permute-start | bytes 12296 | tf_op jit(solution)/shard_map/ppermute | solution.py:68
  72.3 3.7 %collective-permute-start.8 = (f32[4,4,128]{2,1,0:T(4,128)S(1)}, f32[4,4,128]{2,1,0:T(4,128)S(1)}, u32[]{:S(2)}, u32[]{:S(2)}) collective-permute-start(f32[4,4,128]{2,1,0:T(4,128)S(1)} %maximum_select_fusion.2), channel_id=1, source_target_pairs={{0,4},{1,5},{2,6},{3,7},{4,0},{5,1},{6,2},{7,3},{8,12},{9,13},{10,... | collective-permute-start | bytes 24584 | tf_op jit(solution)/shard_map/ppermute | solution.py:68
  75.9 9.2 %collective-permute-start.9 = (f32[8,4,128]{2,1,0:T(4,128)S(1)}, f32[8,4,128]{2,1,0:T(4,128)S(1)}, u32[]{:S(2)}, u32[]{:S(2)}) collective-permute-start(f32[8,4,128]{2,1,0:T(4,128)S(1)} %maximum_select_fusion.1), channel_id=1, source_target_pairs={{0,8},{1,9},{2,10},{3,11},{4,12},{5,13},{6,14},{7,15},{8,0},{9,1},... | collective-permute-start | bytes 49160 | tf_op jit(solution)/shard_map/ppermute | solution.py:68
  79.8 6.7 %copy-start.3 = (f32[1,128,128]{2,1,0:T(8,128)S(1)}, f32[1,128,128]{2,1,0:T(8,128)}, u32[]{:S(2)}) copy-start(f32[1,128,128]{2,1,0:T(8,128)} %shard_map.68) | copy-start | bytes 196612
  79.8 169.6 %all-to-all-start = ((bf16[16,1024,256]{2,1,0:T(8,128)(2,1)}), bf16[16,1024,256]{2,1,0:T(8,128)(2,1)}, u32[]{:S(2)}, u32[]{:S(2)}) async-start(bf16[16,1024,256]{2,1,0:T(8,128)(2,1)} %bitcast.66), calls=%async_computation | async-start | bytes 16777216 | tf_op jit(solution)/shard_map/all_to_all | solution.py:98
  84.9 123.1 %all-gather.3.cloned.1.call-start = ((), (), s32[]{:S(2)}) async-start(), calls=%async_computation.1 | async-start | bytes 3342336 | tf_op jit(solution)/shard_map/all_gather | solution.py:145
  249.4 6.5 %copy-start.1 = (f32[8,128,128]{2,1,0:T(8,128)S(1)}, f32[8,128,128]{2,1,0:T(8,128)}, u32[]{:S(2)}) copy-start(f32[8,128,128]{2,1,0:T(8,128)} %shard_map.69) | copy-start | bytes 1572868
  257.1 6.6 %copy-start = (f32[8,128,128]{2,1,0:T(8,128)}, f32[8,128,128]{2,1,0:T(8,128)S(1)}, u32[]{:S(2)}) copy-start(f32[8,128,128]{2,1,0:T(8,128)S(1)} %fusion.66) | copy-start | bytes 1572868
Sparse Core Ops, SparseCore 0:
  88.4 119.5 all-gather.2

commit v8 on v7

--- a/solution.py
+++ b/solution.py
@@ -16,13 +16,11 @@
 
 
 def _gauss_jordan(a_ref, o_ref):
-    n = a_ref.shape[-1]
-    o_ref[...] = a_ref[...]
+    batch, n, _ = a_ref.shape
     lane = lax.broadcasted_iota(jnp.int32, (1, 1, n), 2)
     sub = lax.broadcasted_iota(jnp.int32, (1, n, 1), 1)
 
-    def step(k, carry):
-        a = o_ref[...]
+    def update(k, a):
         colmask = lane == k
         rowmask = sub == k
         c = jnp.sum(jnp.where(colmask, a, 0.0), axis=2, keepdims=True)
@@ -31,10 +29,18 @@
         inv_p = 1.0 / p
         rs = jnp.where(colmask, inv_p, r * inv_p)
         out = jnp.where(colmask, -c * inv_p, a - c * rs)
-        o_ref[...] = jnp.where(rowmask, rs, out)
-        return carry
+        return jnp.where(rowmask, rs, out)
 
-    lax.fori_loop(0, n, step, 0)
+    if batch == 1:
+        o_ref[...] = lax.fori_loop(0, n, update, a_ref[...], unroll=4)
+    else:
+        o_ref[...] = a_ref[...]
+
+        def step(k, carry):
+            o_ref[...] = update(k, o_ref[...])
+            return carry
+
+        lax.fori_loop(0, n, step, 0, unroll=2)
 
 
 def spd_inverse(a):

time: 272 us -> 270 us (level)
  no operation moved by 1% of the time
where the time goes in v8:
time: 270 us; the launch traced here: 269 us
  waiting for transfers between devices  133 us (49%)
  Pallas kernels  52.9 us (20%)
  starting transfers between devices  23.2 us (9%)
  other arithmetic  21.6 us (8%)
  matrix products  16 us (6%)
  between operations  15.9 us (6%)
  local copies, waits for them, and re-layouts  6.34 us (2%)
    all_gather x1, waiting for transfers between devices, per_device(): lax.all_gather(jnp.concatenate([smoothed.astype(jnp.float32), moment], 0)...  120 us
    pallas_call x2, Pallas kernels, spd_inverse(): pl.pallas_call(_gauss_jordan, out_shape=jax.ShapeDtypeStruct(a.shape, jnp...  52.9 us
    convert_element_type x1, other arithmetic, per_device(): (loadings - loadings_hi.astype(jnp.float32)).astype(jnp.bfloat16)  11.5 us
    ppermute x4, starting transfers between devices, butterfly_gather(): other = lax.ppermute(held, axis, pairs)  10.4 us
    ppermute x6, starting transfers between devices, butterfly_sum(): part = part + lax.ppermute(part, axis, pairs)  7.74 us
    ppermute x6, waiting for transfers between devices, butterfly_sum(): part = part + lax.ppermute(part, axis, pairs)  6.72 us
    dot_general x1, matrix products, per_device(): jnp.dot(observed, smooth_all.astype(jnp.bfloat16), preferred_element_type...  6.44 us
    ppermute x4, waiting for transfers between devices, butterfly_gather(): other = lax.ppermute(held, axis, pairs)  5.92 us
  transfers between devices with their start and end apart: 12, of which 6 were waited for; matrix products, arithmetic and copies ran while one was open for 3% of the time, Pallas kernels for 20%

profile of v8, /device:TPU:0, one launch (start us, length us, event | category | flops | bytes accessed | tf_op | source)
XLA Modules:
  0.0 268.8 jit_solution(437672613773693094)
XLA Ops:
  7.2 1.1 fusion.40
  8.2 1.8 fusion.9
  10.1 0.1 broadcast_bitcast_fusion
  10.1 0.9 broadcast_divide_fusion
  11.0 0.0 slice-start
  11.0 11.5 %subtract_convert_fusion = (bf16[16384,128]{1,0:T(8,128)(2,1)S(1)}, bf16[16384,128]{1,0:T(8,128)(2,1)S(1)}, bf16[16384,128]{1,0:T(8,128)(2,1)S(1)}, bf16[16384,128]{1,0:T(8,128)(2,1)S(1)}) fusion(f32[16384,128]{1,0:T(8,128)} %param.6, f32[16384]{0:T(1024)S(1)} %broadcast_bitcast_fusion, f32[16384]{0:T(1024)S(1)} %broadcast_divide_fusion), kind=kLoop, calls=%fused_computation.9 | loop fusion | flops 20971520 | bytes 25296896 | tf_op jit(solution)/shard_map/convert_element_type | solution.py:109
  22.5 0.0 slice-start.1
  22.5 2.4 fusion
  24.9 0.1 collective-permute-start.3
  25.1 1.5 convolution_bitcast_fusion
  26.6 0.6 collective-permute-start
  27.2 1.8 collective-permute-start.4
  28.9 2.6 collective-permute-done.4
  31.5 3.4 %collective-permute-start.5 = (f32[128,128]{1,0:T(8,128)S(1)}, f32[128,128]{1,0:T(8,128)S(1)}, u32[]{:S(2)}, u32[]{:S(2)}) collective-permute-start(f32[128,128]{1,0:T(8,128)S(1)} %add.509), channel_id=1, source_target_pairs={{0,64},{16,80},{32,96},{48,112},{64,0},{80,16},{96,32},{112,48},{1... | collective-permute-start | bytes 196616 | tf_op jit(solution)/shard_map/ppermute | solution.py:63
  34.9 0.8 collective-permute-start.1
  35.9 4.1 %collective-permute-done.1 = f32[256,128]{0,1:T(8,128)S(1)} collective-permute-done((f32[256,128]{0,1:T(8,128)S(1)}, f32[256,128]{0,1:T(8,128)S(1)}, u32[]{:S(2)}, u32[]{:S(2)}) %collective-permute-start.1) | collective-permute-done | bytes 131104 | tf_op jit(solution)/shard_map/ppermute | solution.py:63
  40.0 1.2 collective-permute-start.2
  41.2 0.6 add_bitcast_fusion.a_ref
  41.8 16.1 %shard_map.68 = f32[1,128,128]{2,1,0:T(8,128)} custom-call(f32[1,128,128]{2,1,0:T(8,128)} %add_bitcast_fusion.a_ref), custom_call_target="tpu_custom_call" | custom-call | flops 16777216 | bytes 131072 | tf_op jit(solution)/shard_map/pallas_call | solution.py:48
  58.0 1.2 fusion.18
  62.9 1.6 collective-permute-start.6
  64.5 2.1 collective-permute-done.6
  66.6 3.0 %collective-permute-start.7 = (f32[2,4,128]{2,1,0:T(4,128)S(1)}, f32[2,4,128]{2,1,0:T(4,128)S(1)}, u32[]{:S(2)}, u32[]{:S(2)}) collective-permute-start(f32[2,4,128]{2,1,0:T(4,128)S(1)} %maximum_select_fusion.3), channel_id=1, source_target_pairs={{0,2},{1,3},{2,0},{3,1},{4,6},{5,7},{6,4},{7,5},{8,10},{9,11},{10,... | collective-permute-start | bytes 12296 | tf_op jit(solution)/shard_map/ppermute | solution.py:74
  69.6 2.1 collective-permute-done.7
  71.7 1.9 collective-permute-start.8
  73.6 1.7 collective-permute-done.8
  75.4 3.9 %collective-permute-start.9 = (f32[8,4,128]{2,1,0:T(4,128)S(1)}, f32[8,4,128]{2,1,0:T(4,128)S(1)}, u32[]{:S(2)}, u32[]{:S(2)}) collective-permute-start(f32[8,4,128]{2,1,0:T(4,128)S(1)} %maximum_select_fusion.1), channel_id=1, source_target_pairs={{0,8},{1,9},{2,10},{3,11},{4,12},{5,13},{6,14},{7,15},{8,0},{9,1},... | collective-permute-start | bytes 49160 | tf_op jit(solution)/shard_map/ppermute | solution.py:74
  79.2 5.0 %all-to-all-start = ((bf16[16,1024,256]{2,1,0:T(8,128)(2,1)}), bf16[16,1024,256]{2,1,0:T(8,128)(2,1)}, u32[]{:S(2)}, u32[]{:S(2)}) async-start(bf16[16,1024,256]{2,1,0:T(8,128)(2,1)} %bitcast.66), calls=%async_computation | async-start | bytes 16777216 | tf_op jit(solution)/shard_map/all_to_all | solution.py:104
  84.3 0.0 all-gather.3.cloned.1.call-start
  84.4 0.1 rev.13
  84.5 0.1 rev.12
  85.9 0.1 fusion.36
  86.0 0.2 convolution_add_fusion
  86.2 0.7 pad_maximum_fusion
  86.9 0.0 all-gather.3.cloned.1.call-update
  86.9 0.1 dynamic-slice_convert_fusion
  87.0 0.1 broadcast_in_dim.23
  87.1 0.1 dynamic-slice_reduce_fusion
  87.2 120.2 %all-gather.3.cloned.1.call-done = f32[6144,128]{1,0:T(8,128)} async-done(((f32[384,128]{1,0:T(8,128)}), f32[6144,128]{1,0:T(8,128)}) %all-gather.3.cloned.1.call-update) | async-done | bytes 3145744 | tf_op jit(solution)/shard_map/all_gather | solution.py:151
  207.4 1.3 slice.1022
  208.7 1.2 fusion.14
  210.0 0.9 copy.12.a_ref
  210.9 36.8 %shard_map.69 = f32[8,128,128]{2,1,0:T(8,128)} custom-call(f32[8,128,128]{2,1,0:T(8,128)} %copy.12.a_ref), custom_call_target="tpu_custom_call" | custom-call | flops 134217728 | bytes 1048576 | tf_op jit(solution)/shard_map/pallas_call | solution.py:48
  247.7 6.4 %fusion.8 = f32[1024,128,1]{1,0,2:T(8,128)S(1)} fusion(bf16[16,1024,256]{2,1,0:T(8,128)(2,1)} %all-to-all-done, bf16[1024,16]{0,1:T(8,128)(2,1)S(1)} %bitcast.73, f32[16,384,128]{2,1,0:T(8,128)} %bitcast.72), kind=kOutput, calls=%fused_computation.13 | convolution fusion | flops 1077936128 | bytes 9994240 | tf_op jit(solution)/shard_map/dot_general | solution.py:161
  254.2 1.2 fusion.66
  255.4 0.2 fusion.16
  255.6 5.7 %multiply_reduce_fusion = f32[1024]{0:T(1024)S(1)} fusion(bf16[16,1024,256]{2,1,0:T(8,128)(2,1)} %all-to-all-done, bf16[1024,16]{0,1:T(8,128)(2,1)S(1)} %bitcast.74), kind=kLoop, calls=%fused_computation | loop fusion | flops 16776192 | bytes 8425472 | tf_op jit(solution)/shard_map/reduce_sum | solution.py:160
  261.3 0.7 bitcast_divide_fusion
  (365 shorter events, 3.8 us)
Async XLA Ops:
  11.0 14.0 %slice-start = ((s8[8388608]{0:T(1024)(128)(4,1)}), s8[4194304]{0:T(1024)(128)(4,1)S(1)}, s32[]{:S(2)}) async-start(s8[8388608]{0:T(1024)(128)(4,1)} %bitcast.67), calls=%async_computation.2 | async-start | bytes 8388608
  22.5 2.5 slice-start.1
  24.9 10.8 %copy-start.2 = (f32[256,128]{1,0:T(8,128)S(1)}, f32[256,128]{1,0:T(8,128)}, u32[]{:S(2)}) copy-start(f32[256,128]{1,0:T(8,128)} %param.8) | copy-start | bytes 393220
  24.9 2.2 collective-permute-start.3
  26.6 8.3 %collective-permute-start = (f32[256,128]{0,1:T(8,128)S(1)}, f32[256,128]{0,1:T(8,128)S(1)}, u32[]{:S(2)}, u32[]{:S(2)}) collective-permute-start(f32[256,128]{0,1:T(8,128)S(1)} %convolution_bitcast_fusion), channel_id=1, source_target_pairs={{0,16},{16,0},{32,48},{48,32},{64,80},{80,64},{96,112},{112,96},{1... | collective-permute-start | bytes 393224 | tf_op jit(solution)/shard_map/ppermute | solution.py:63
  27.2 4.3 %collective-permute-start.4 = (f32[128,128]{1,0:T(8,128)S(1)}, f32[128,128]{1,0:T(8,128)S(1)}, u32[]{:S(2)}, u32[]{:S(2)}) collective-permute-start(f32[128,128]{1,0:T(8,128)S(1)} %fusion.73), channel_id=1, source_target_pairs={{0,32},{16,48},{32,0},{48,16},{64,96},{80,112},{96,64},{112,80},{1... | collective-permute-start | bytes 196616 | tf_op jit(solution)/shard_map/ppermute | solution.py:63
  31.5 9.7 %collective-permute-start.5 = (f32[128,128]{1,0:T(8,128)S(1)}, f32[128,128]{1,0:T(8,128)S(1)}, u32[]{:S(2)}, u32[]{:S(2)}) collective-permute-start(f32[128,128]{1,0:T(8,128)S(1)} %add.509), channel_id=1, source_target_pairs={{0,64},{16,80},{32,96},{48,112},{64,0},{80,16},{96,32},{112,48},{1... | collective-permute-start | bytes 196616 | tf_op jit(solution)/shard_map/ppermute | solution.py:63
  34.9 5.0 %collective-permute-start.1 = (f32[256,128]{0,1:T(8,128)S(1)}, f32[256,128]{0,1:T(8,128)S(1)}, u32[]{:S(2)}, u32[]{:S(2)}) collective-permute-start(f32[256,128]{0,1:T(8,128)S(1)} %add.503), channel_id=1, source_target_pairs={{0,32},{16,48},{32,0},{48,16},{64,96},{80,112},{96,64},{112,80},{1... | collective-permute-start | bytes 393224 | tf_op jit(solution)/shard_map/ppermute | solution.py:63
  40.0 18.0 %collective-permute-start.2 = (f32[256,128]{0,1:T(8,128)S(1)}, f32[256,128]{0,1:T(8,128)S(1)}, u32[]{:S(2)}, u32[]{:S(2)}) collective-permute-start(f32[256,128]{0,1:T(8,128)S(1)} %add.504), channel_id=1, source_target_pairs={{0,64},{16,80},{32,96},{48,112},{64,0},{80,16},{96,32},{112,48},{1... | collective-permute-start | bytes 393224 | tf_op jit(solution)/shard_map/ppermute | solution.py:63
  62.9 3.7 %collective-permute-start.6 = (f32[1,4,128]{2,1,0:T(4,128)S(1)}, f32[1,4,128]{2,1,0:T(4,128)S(1)}, u32[]{:S(2)}, u32[]{:S(2)}) collective-permute-start(f32[1,4,128]{2,1,0:T(4,128)S(1)} %maximum_bitcast_fusion), channel_id=1, source_target_pairs={{0,1},{1,0},{2,3},{3,2},{4,5},{5,4},{6,7},{7,6},{8,9},{9,8},{10,11... | collective-permute-start | bytes 6152 | tf_op jit(solution)/shard_map/ppermute | solution.py:74
  66.6 5.1 %collective-permute-start.7 = (f32[2,4,128]{2,1,0:T(4,128)S(1)}, f32[2,4,128]{2,1,0:T(4,128)S(1)}, u32[]{:S(2)}, u32[]{:S(2)}) collective-permute-start(f32[2,4,128]{2,1,0:T(4,128)S(1)} %maximum_select_fusion.3), channel_id=1, source_target_pairs={{0,2},{1,3},{2,0},{3,1},{4,6},{5,7},{6,4},{7,5},{8,10},{9,11},{10,... | collective-permute-start | bytes 12296 | tf_op jit(solution)/shard_map/ppermute | solution.py:74
  71.7 3.7 %collective-permute-start.8 = (f32[4,4,128]{2,1,0:T(4,128)S(1)}, f32[4,4,128]{2,1,0:T(4,128)S(1)}, u32[]{:S(2)}, u32[]{:S(2)}) collective-permute-start(f32[4,4,128]{2,1,0:T(4,128)S(1)} %maximum_select_fusion.2), channel_id=1, source_target_pairs={{0,4},{1,5},{2,6},{3,7},{4,0},{5,1},{6,2},{7,3},{8,12},{9,13},{10,... | collective-permute-start | bytes 24584 | tf_op jit(solution)/shard_map/ppermute | solution.py:74
  75.4 9.2 %collective-permute-start.9 = (f32[8,4,128]{2,1,0:T(4,128)S(1)}, f32[8,4,128]{2,1,0:T(4,128)S(1)}, u32[]{:S(2)}, u32[]{:S(2)}) collective-permute-start(f32[8,4,128]{2,1,0:T(4,128)S(1)} %maximum_select_fusion.1), channel_id=1, source_target_pairs={{0,8},{1,9},{2,10},{3,11},{4,12},{5,13},{6,14},{7,15},{8,0},{9,1},... | collective-permute-start | bytes 49160 | tf_op jit(solution)/shard_map/ppermute | solution.py:74
  79.2 6.7 %copy-start.3 = (f32[1,128,128]{2,1,0:T(8,128)S(1)}, f32[1,128,128]{2,1,0:T(8,128)}, u32[]{:S(2)}) copy-start(f32[1,128,128]{2,1,0:T(8,128)} %shard_map.68) | copy-start | bytes 196612
  79.2 168.5 %all-to-all-start = ((bf16[16,1024,256]{2,1,0:T(8,128)(2,1)}), bf16[16,1024,256]{2,1,0:T(8,128)(2,1)}, u32[]{:S(2)}, u32[]{:S(2)}) async-start(bf16[16,1024,256]{2,1,0:T(8,128)(2,1)} %bitcast.66), calls=%async_computation | async-start | bytes 16777216 | tf_op jit(solution)/shard_map/all_to_all | solution.py:104
  84.3 123.1 %all-gather.3.cloned.1.call-start = ((), (), s32[]{:S(2)}) async-start(), calls=%async_computation.1 | async-start | bytes 3342336 | tf_op jit(solution)/shard_map/all_gather | solution.py:151
  247.7 6.5 %copy-start.1 = (f32[8,128,128]{2,1,0:T(8,128)S(1)}, f32[8,128,128]{2,1,0:T(8,128)}, u32[]{:S(2)}) copy-start(f32[8,128,128]{2,1,0:T(8,128)} %shard_map.69) | copy-start | bytes 1572868
  255.4 6.6 %copy-start = (f32[8,128,128]{2,1,0:T(8,128)}, f32[8,128,128]{2,1,0:T(8,128)S(1)}, u32[]{:S(2)}) copy-start(f32[8,128,128]{2,1,0:T(8,128)S(1)} %fusion.66) | copy-start | bytes 1572868
Sparse Core Ops, SparseCore 0:
  87.8 119.5 all-gather.2

commit v9 on v8

--- a/solution.py
+++ b/solution.py
@@ -35,9 +35,22 @@
         o_ref[...] = lax.fori_loop(0, n, update, a_ref[...], unroll=4)
     else:
         o_ref[...] = a_ref[...]
+        pad = jnp.zeros((n - batch, n), jnp.float32)
 
         def step(k, carry):
-            o_ref[...] = update(k, o_ref[...])
+            a = o_ref[...]
+            colmask = lane == k
+            rowmask = sub == k
+            r = jnp.sum(jnp.where(rowmask, a, 0.0), axis=1)
+            turned = jnp.transpose(jnp.concatenate([r, pad], 0))
+            sign = jnp.where(sub < k, -1.0, 1.0)
+            c = jnp.stack([turned[:, b : b + 1] for b in range(batch)], 0) * sign
+            r = r[:, None, :]
+            p = jnp.sum(jnp.where(colmask, r, 0.0), axis=2, keepdims=True)
+            inv_p = 1.0 / p
+            rs = jnp.where(colmask, inv_p, r * inv_p)
+            out = jnp.where(colmask, -c * inv_p, a - c * rs)
+            o_ref[...] = jnp.where(rowmask, rs, out)
             return carry
 
         lax.fori_loop(0, n, step, 0, unroll=2)

time: 270 us -> 318 us (1.18)
  Pallas kernels: 52.9 us -> 101 us
    pallas_call x2, Pallas kernels: 52.9 us -> 101 us  [spd_inverse(): pl.pallas_call(_gauss_jordan, out_shape=jax.ShapeDtypeStruct(a.shape, jnp...]
  transfers between devices with their start and end apart: 12 -> 12, of which waited for: 6 -> 6; matrix products, arithmetic and copies ran while one was open for 3% -> 3% of each run, Pallas kernels for 20% -> 32%
where the time goes in v9:
time: 318 us; the launch traced here: 317 us
  waiting for transfers between devices  133 us (42%)
  Pallas kernels  101 us (32%)
  starting transfers between devices  23.2 us (7%)
  other arithmetic  21.6 us (7%)
  matrix products  16 us (5%)
  between operations  15.9 us (5%)
  local copies, waits for them, and re-layouts  6.34 us (2%)
    all_gather x1, waiting for transfers between devices, per_device(): lax.all_gather(jnp.concatenate([smoothed.astype(jnp.float32), moment], 0)...  120 us
    pallas_call x2, Pallas kernels, spd_inverse(): pl.pallas_call(_gauss_jordan, out_shape=jax.ShapeDtypeStruct(a.shape, jnp...  101 us
    convert_element_type x1, other arithmetic, per_device(): (loadings - loadings_hi.astype(jnp.float32)).astype(jnp.bfloat16)  11.5 us
    ppermute x4, starting transfers between devices, butterfly_gather(): other = lax.ppermute(held, axis, pairs)  10.4 us
    ppermute x6, starting transfers between devices, butterfly_sum(): part = part + lax.ppermute(part, axis, pairs)  7.74 us
    ppermute x6, waiting for transfers between devices, butterfly_sum(): part = part + lax.ppermute(part, axis, pairs)  6.72 us
    dot_general x1, matrix products, per_device(): jnp.dot(observed, smooth_all.astype(jnp.bfloat16), preferred_element_type...  6.44 us
  transfers between devices with their start and end apart: 12, of which 6 were waited for; matrix products, arithmetic and copies ran while one was open for 3% of the time, Pallas kernels for 32%

profile of v9, /device:TPU:0, one launch (start us, length us, event | category | flops | bytes accessed | tf_op | source)
XLA Modules:
  0.0 317.3 jit_solution(3793325221831090990)
XLA Ops:
  7.2 1.1 fusion.40
  8.2 1.8 fusion.9
  10.1 0.1 broadcast_bitcast_fusion
  10.1 0.9 broadcast_divide_fusion
  11.0 0.0 slice-start
  11.0 11.5 %subtract_convert_fusion = (bf16[16384,128]{1,0:T(8,128)(2,1)S(1)}, bf16[16384,128]{1,0:T(8,128)(2,1)S(1)}, bf16[16384,128]{1,0:T(8,128)(2,1)S(1)}, bf16[16384,128]{1,0:T(8,128)(2,1)S(1)}) fusion(f32[16384,128]{1,0:T(8,128)} %param.6, f32[16384]{0:T(1024)S(1)} %broadcast_bitcast_fusion, f32[16384]{0:T(1024)S(1)} %broadcast_divide_fusion), kind=kLoop, calls=%fused_computation.9 | loop fusion | flops 20971520 | bytes 25296896 | tf_op jit(solution)/shard_map/convert_element_type | solution.py:122
  22.5 0.0 slice-start.1
  22.5 2.4 fusion
  24.9 0.1 collective-permute-start.3
  25.1 1.5 convolution_bitcast_fusion
  26.6 0.6 collective-permute-start
  27.2 1.8 collective-permute-start.4
  28.9 2.6 collective-permute-done.4
  31.5 3.4 %collective-permute-start.5 = (f32[128,128]{1,0:T(8,128)S(1)}, f32[128,128]{1,0:T(8,128)S(1)}, u32[]{:S(2)}, u32[]{:S(2)}) collective-permute-start(f32[128,128]{1,0:T(8,128)S(1)} %add.509), channel_id=1, source_target_pairs={{0,64},{16,80},{32,96},{48,112},{64,0},{80,16},{96,32},{112,48},{1... | collective-permute-start | bytes 196616 | tf_op jit(solution)/shard_map/ppermute | solution.py:76
  34.9 0.8 collective-permute-start.1
  35.9 4.1 %collective-permute-done.1 = f32[256,128]{0,1:T(8,128)S(1)} collective-permute-done((f32[256,128]{0,1:T(8,128)S(1)}, f32[256,128]{0,1:T(8,128)S(1)}, u32[]{:S(2)}, u32[]{:S(2)}) %collective-permute-start.1) | collective-permute-done | bytes 131104 | tf_op jit(solution)/shard_map/ppermute | solution.py:76
  40.0 1.2 collective-permute-start.2
  41.2 0.6 add_bitcast_fusion.a_ref
  41.8 16.1 %shard_map.68 = f32[1,128,128]{2,1,0:T(8,128)} custom-call(f32[1,128,128]{2,1,0:T(8,128)} %add_bitcast_fusion.a_ref), custom_call_target="tpu_custom_call" | custom-call | flops 16777216 | bytes 131072 | tf_op jit(solution)/shard_map/pallas_call | solution.py:61
  58.0 1.2 fusion.18
  62.9 1.6 collective-permute-start.6
  64.5 2.1 collective-permute-done.6
  66.6 3.0 collective-permute-start.7
  69.6 2.1 collective-permute-done.7
  71.7 1.9 collective-permute-start.8
  73.6 1.7 collective-permute-done.8
  75.4 3.9 %collective-permute-start.9 = (f32[8,4,128]{2,1,0:T(4,128)S(1)}, f32[8,4,128]{2,1,0:T(4,128)S(1)}, u32[]{:S(2)}, u32[]{:S(2)}) collective-permute-start(f32[8,4,128]{2,1,0:T(4,128)S(1)} %maximum_select_fusion.1), channel_id=1, source_target_pairs={{0,8},{1,9},{2,10},{3,11},{4,12},{5,13},{6,14},{7,15},{8,0},{9,1},... | collective-permute-start | bytes 49160 | tf_op jit(solution)/shard_map/ppermute | solution.py:87
  79.2 5.0 %all-to-all-start = ((bf16[16,1024,256]{2,1,0:T(8,128)(2,1)}), bf16[16,1024,256]{2,1,0:T(8,128)(2,1)}, u32[]{:S(2)}, u32[]{:S(2)}) async-start(bf16[16,1024,256]{2,1,0:T(8,128)(2,1)} %bitcast.66), calls=%async_computation | async-start | bytes 16777216 | tf_op jit(solution)/shard_map/all_to_all | solution.py:117
  84.3 0.0 all-gather.3.cloned.1.call-start
  84.4 0.1 rev.13
  84.5 0.1 rev.12
  85.9 0.1 fusion.36
  86.0 0.2 convolution_add_fusion
  86.2 0.7 pad_maximum_fusion
  86.9 0.0 all-gather.3.cloned.1.call-update
  86.9 0.1 dynamic-slice_convert_fusion
  87.0 0.1 broadcast_in_dim.23
  87.1 0.1 dynamic-slice_reduce_fusion
  87.2 120.2 %all-gather.3.cloned.1.call-done = f32[6144,128]{1,0:T(8,128)} async-done(((f32[384,128]{1,0:T(8,128)}), f32[6144,128]{1,0:T(8,128)}) %all-gather.3.cloned.1.call-update) | async-done | bytes 3145744 | tf_op jit(solution)/shard_map/all_gather | solution.py:164
  207.4 1.3 slice.1022
  208.7 1.2 fusion.14
  210.0 0.9 copy.12.a_ref
  210.9 85.3 %shard_map.69 = f32[8,128,128]{2,1,0:T(8,128)} custom-call(f32[8,128,128]{2,1,0:T(8,128)} %copy.12.a_ref), custom_call_target="tpu_custom_call" | custom-call | flops 134217728 | bytes 1048576 | tf_op jit(solution)/shard_map/pallas_call | solution.py:61
  296.2 6.4 %fusion.8 = f32[1024,128,1]{1,0,2:T(8,128)S(1)} fusion(bf16[16,1024,256]{2,1,0:T(8,128)(2,1)} %all-to-all-done, bf16[1024,16]{0,1:T(8,128)(2,1)S(1)} %bitcast.73, f32[16,384,128]{2,1,0:T(8,128)} %bitcast.72), kind=kOutput, calls=%fused_computation.13 | convolution fusion | flops 1077936128 | bytes 9994240 | tf_op jit(solution)/shard_map/dot_general | solution.py:174
  302.7 1.2 fusion.66
  303.9 0.2 fusion.16
  304.1 5.7 %multiply_reduce_fusion = f32[1024]{0:T(1024)S(1)} fusion(bf16[16,1024,256]{2,1,0:T(8,128)(2,1)} %all-to-all-done, bf16[1024,16]{0,1:T(8,128)(2,1)S(1)} %bitcast.74), kind=kLoop, calls=%fused_computation | loop fusion | flops 16776192 | bytes 8425472 | tf_op jit(solution)/shard_map/reduce_sum | solution.py:173
  309.8 0.7 bitcast_divide_fusion
  (365 shorter events, 3.8 us)
Async XLA Ops:
  11.0 14.0 %slice-start = ((s8[8388608]{0:T(1024)(128)(4,1)}), s8[4194304]{0:T(1024)(128)(4,1)S(1)}, s32[]{:S(2)}) async-start(s8[8388608]{0:T(1024)(128)(4,1)} %bitcast.67), calls=%async_computation.2 | async-start | bytes 8388608
  22.5 2.5 slice-start.1
  24.9 10.8 %copy-start.2 = (f32[256,128]{1,0:T(8,128)S(1)}, f32[256,128]{1,0:T(8,128)}, u32[]{:S(2)}) copy-start(f32[256,128]{1,0:T(8,128)} %param.8) | copy-start | bytes 393220
  24.9 2.2 collective-permute-start.3
  26.6 8.3 %collective-permute-start = (f32[256,128]{0,1:T(8,128)S(1)}, f32[256,128]{0,1:T(8,128)S(1)}, u32[]{:S(2)}, u32[]{:S(2)}) collective-permute-start(f32[256,128]{0,1:T(8,128)S(1)} %convolution_bitcast_fusion), channel_id=1, source_target_pairs={{0,16},{16,0},{32,48},{48,32},{64,80},{80,64},{96,112},{112,96},{1... | collective-permute-start | bytes 393224 | tf_op jit(solution)/shard_map/ppermute | solution.py:76
  27.2 4.3 %collective-permute-start.4 = (f32[128,128]{1,0:T(8,128)S(1)}, f32[128,128]{1,0:T(8,128)S(1)}, u32[]{:S(2)}, u32[]{:S(2)}) collective-permute-start(f32[128,128]{1,0:T(8,128)S(1)} %fusion.73), channel_id=1, source_target_pairs={{0,32},{16,48},{32,0},{48,16},{64,96},{80,112},{96,64},{112,80},{1... | collective-permute-start | bytes 196616 | tf_op jit(solution)/shard_map/ppermute | solution.py:76
  31.5 9.7 %collective-permute-start.5 = (f32[128,128]{1,0:T(8,128)S(1)}, f32[128,128]{1,0:T(8,128)S(1)}, u32[]{:S(2)}, u32[]{:S(2)}) collective-permute-start(f32[128,128]{1,0:T(8,128)S(1)} %add.509), channel_id=1, source_target_pairs={{0,64},{16,80},{32,96},{48,112},{64,0},{80,16},{96,32},{112,48},{1... | collective-permute-start | bytes 196616 | tf_op jit(solution)/shard_map/ppermute | solution.py:76
  34.9 5.0 %collective-permute-start.1 = (f32[256,128]{0,1:T(8,128)S(1)}, f32[256,128]{0,1:T(8,128)S(1)}, u32[]{:S(2)}, u32[]{:S(2)}) collective-permute-start(f32[256,128]{0,1:T(8,128)S(1)} %add.503), channel_id=1, source_target_pairs={{0,32},{16,48},{32,0},{48,16},{64,96},{80,112},{96,64},{112,80},{1... | collective-permute-start | bytes 393224 | tf_op jit(solution)/shard_map/ppermute | solution.py:76
  40.0 18.0 %collective-permute-start.2 = (f32[256,128]{0,1:T(8,128)S(1)}, f32[256,128]{0,1:T(8,128)S(1)}, u32[]{:S(2)}, u32[]{:S(2)}) collective-permute-start(f32[256,128]{0,1:T(8,128)S(1)} %add.504), channel_id=1, source_target_pairs={{0,64},{16,80},{32,96},{48,112},{64,0},{80,16},{96,32},{112,48},{1... | collective-permute-start | bytes 393224 | tf_op jit(solution)/shard_map/ppermute | solution.py:76
  62.9 3.7 %collective-permute-start.6 = (f32[1,4,128]{2,1,0:T(4,128)S(1)}, f32[1,4,128]{2,1,0:T(4,128)S(1)}, u32[]{:S(2)}, u32[]{:S(2)}) collective-permute-start(f32[1,4,128]{2,1,0:T(4,128)S(1)} %maximum_bitcast_fusion), channel_id=1, source_target_pairs={{0,1},{1,0},{2,3},{3,2},{4,5},{5,4},{6,7},{7,6},{8,9},{9,8},{10,11... | collective-permute-start | bytes 6152 | tf_op jit(solution)/shard_map/ppermute | solution.py:87
  66.6 5.1 %collective-permute-start.7 = (f32[2,4,128]{2,1,0:T(4,128)S(1)}, f32[2,4,128]{2,1,0:T(4,128)S(1)}, u32[]{:S(2)}, u32[]{:S(2)}) collective-permute-start(f32[2,4,128]{2,1,0:T(4,128)S(1)} %maximum_select_fusion.3), channel_id=1, source_target_pairs={{0,2},{1,3},{2,0},{3,1},{4,6},{5,7},{6,4},{7,5},{8,10},{9,11},{10,... | collective-permute-start | bytes 12296 | tf_op jit(solution)/shard_map/ppermute | solution.py:87
  71.7 3.7 %collective-permute-start.8 = (f32[4,4,128]{2,1,0:T(4,128)S(1)}, f32[4,4,128]{2,1,0:T(4,128)S(1)}, u32[]{:S(2)}, u32[]{:S(2)}) collective-permute-start(f32[4,4,128]{2,1,0:T(4,128)S(1)} %maximum_select_fusion.2), channel_id=1, source_target_pairs={{0,4},{1,5},{2,6},{3,7},{4,0},{5,1},{6,2},{7,3},{8,12},{9,13},{10,... | collective-permute-start | bytes 24584 | tf_op jit(solution)/shard_map/ppermute | solution.py:87
  75.4 9.2 %collective-permute-start.9 = (f32[8,4,128]{2,1,0:T(4,128)S(1)}, f32[8,4,128]{2,1,0:T(4,128)S(1)}, u32[]{:S(2)}, u32[]{:S(2)}) collective-permute-start(f32[8,4,128]{2,1,0:T(4,128)S(1)} %maximum_select_fusion.1), channel_id=1, source_target_pairs={{0,8},{1,9},{2,10},{3,11},{4,12},{5,13},{6,14},{7,15},{8,0},{9,1},... | collective-permute-start | bytes 49160 | tf_op jit(solution)/shard_map/ppermute | solution.py:87
  79.2 6.7 %copy-start.3 = (f32[1,128,128]{2,1,0:T(8,128)S(1)}, f32[1,128,128]{2,1,0:T(8,128)}, u32[]{:S(2)}) copy-start(f32[1,128,128]{2,1,0:T(8,128)} %shard_map.68) | copy-start | bytes 196612
  79.2 217.0 %all-to-all-start = ((bf16[16,1024,256]{2,1,0:T(8,128)(2,1)}), bf16[16,1024,256]{2,1,0:T(8,128)(2,1)}, u32[]{:S(2)}, u32[]{:S(2)}) async-start(bf16[16,1024,256]{2,1,0:T(8,128)(2,1)} %bitcast.66), calls=%async_computation | async-start | bytes 16777216 | tf_op jit(solution)/shard_map/all_to_all | solution.py:117
  84.3 123.1 %all-gather.3.cloned.1.call-start = ((), (), s32[]{:S(2)}) async-start(), calls=%async_computation.1 | async-start | bytes 3342336 | tf_op jit(solution)/shard_map/all_gather | solution.py:164
  296.2 6.5 %copy-start.1 = (f32[8,128,128]{2,1,0:T(8,128)S(1)}, f32[8,128,128]{2,1,0:T(8,128)}, u32[]{:S(2)}) copy-start(f32[8,128,128]{2,1,0:T(8,128)} %shard_map.69) | copy-start | bytes 1572868
  303.9 6.6 %copy-start = (f32[8,128,128]{2,1,0:T(8,128)}, f32[8,128,128]{2,1,0:T(8,128)S(1)}, u32[]{:S(2)}) copy-start(f32[8,128,128]{2,1,0:T(8,128)S(1)} %fusion.66) | copy-start | bytes 1572868
Sparse Core Ops, SparseCore 0:
  87.8 119.5 all-gather.2

commit v10 on v8

--- a/solution.py
+++ b/solution.py
@@ -32,7 +32,7 @@
         return jnp.where(rowmask, rs, out)
 
     if batch == 1:
-        o_ref[...] = lax.fori_loop(0, n, update, a_ref[...], unroll=4)
+        o_ref[...] = lax.fori_loop(0, n, update, a_ref[...], unroll=8)
     else:
         o_ref[...] = a_ref[...]
 
@@ -40,7 +40,7 @@
             o_ref[...] = update(k, o_ref[...])
             return carry
 
-        lax.fori_loop(0, n, step, 0, unroll=2)
+        lax.fori_loop(0, n, step, 0, unroll=4)
 
 
 def spd_inverse(a):

time: 270 us -> 269 us (level)
  no operation moved by 1% of the time
where the time goes in v10:
time: 269 us; the launch traced here: 268 us
  waiting for transfers between devices  133 us (49%)
  Pallas kernels  52.4 us (19%)
  starting transfers between devices  23.2 us (9%)
  other arithmetic  21.6 us (8%)
  matrix products  16 us (6%)
  between operations  15.9 us (6%)
  local copies, waits for them, and re-layouts  6.34 us (2%)
    all_gather x1, waiting for transfers between devices, per_device(): lax.all_gather(jnp.concatenate([smoothed.astype(jnp.float32), moment], 0)...  120 us
    pallas_call x2, Pallas kernels, spd_inverse(): pl.pallas_call(_gauss_jordan, out_shape=jax.ShapeDtypeStruct(a.shape, jnp...  52.4 us
    convert_element_type x1, other arithmetic, per_device(): (loadings - loadings_hi.astype(jnp.float32)).astype(jnp.bfloat16)  11.5 us
    ppermute x4, starting transfers between devices, butterfly_gather(): other = lax.ppermute(held, axis, pairs)  10.4 us
    ppermute x6, starting transfers between devices, butterfly_sum(): part = part + lax.ppermute(part, axis, pairs)  7.74 us
    ppermute x6, waiting for transfers between devices, butterfly_sum(): part = part + lax.ppermute(part, axis, pairs)  6.72 us
    dot_general x1, matrix products, per_device(): jnp.dot(observed, smooth_all.astype(jnp.bfloat16), preferred_element_type...  6.44 us
    ppermute x4, waiting for transfers between devices, butterfly_gather(): other = lax.ppermute(held, axis, pairs)  5.92 us
  transfers between devices with their start and end apart: 12, of which 6 were waited for; matrix products, arithmetic and copies ran while one was open for 3% of the time, Pallas kernels for 20%

profile of v10, /device:TPU:0, one launch (start us, length us, event | category | flops | bytes accessed | tf_op | source)
XLA Modules:
  0.0 268.3 jit_solution(356736588593739814)
XLA Ops:
  7.2 1.1 fusion.40
  8.2 1.8 fusion.9
  10.1 0.1 broadcast_bitcast_fusion
  10.1 0.9 broadcast_divide_fusion
  11.0 0.0 slice-start
  11.0 11.5 %subtract_convert_fusion = (bf16[16384,128]{1,0:T(8,128)(2,1)S(1)}, bf16[16384,128]{1,0:T(8,128)(2,1)S(1)}, bf16[16384,128]{1,0:T(8,128)(2,1)S(1)}, bf16[16384,128]{1,0:T(8,128)(2,1)S(1)}) fusion(f32[16384,128]{1,0:T(8,128)} %param.6, f32[16384]{0:T(1024)S(1)} %broadcast_bitcast_fusion, f32[16384]{0:T(1024)S(1)} %broadcast_divide_fusion), kind=kLoop, calls=%fused_computation.9 | loop fusion | flops 20971520 | bytes 25296896 | tf_op jit(solution)/shard_map/convert_element_type | solution.py:109
  22.5 0.0 slice-start.1
  22.5 2.4 fusion
  24.9 0.1 collective-permute-start.3
  25.1 1.5 convolution_bitcast_fusion
  26.6 0.6 collective-permute-start
  27.2 1.8 collective-permute-start.4
  28.9 2.6 collective-permute-done.4
  31.5 3.4 %collective-permute-start.5 = (f32[128,128]{1,0:T(8,128)S(1)}, f32[128,128]{1,0:T(8,128)S(1)}, u32[]{:S(2)}, u32[]{:S(2)}) collective-permute-start(f32[128,128]{1,0:T(8,128)S(1)} %add.509), channel_id=1, source_target_pairs={{0,64},{16,80},{32,96},{48,112},{64,0},{80,16},{96,32},{112,48},{1... | collective-permute-start | bytes 196616 | tf_op jit(solution)/shard_map/ppermute | solution.py:63
  34.9 0.8 collective-permute-start.1
  35.9 4.1 %collective-permute-done.1 = f32[256,128]{0,1:T(8,128)S(1)} collective-permute-done((f32[256,128]{0,1:T(8,128)S(1)}, f32[256,128]{0,1:T(8,128)S(1)}, u32[]{:S(2)}, u32[]{:S(2)}) %collective-permute-start.1) | collective-permute-done | bytes 131104 | tf_op jit(solution)/shard_map/ppermute | solution.py:63
  40.0 1.2 collective-permute-start.2
  41.2 0.6 add_bitcast_fusion.a_ref
  41.8 16.0 %shard_map.68 = f32[1,128,128]{2,1,0:T(8,128)} custom-call(f32[1,128,128]{2,1,0:T(8,128)} %add_bitcast_fusion.a_ref), custom_call_target="tpu_custom_call" | custom-call | flops 16777216 | bytes 131072 | tf_op jit(solution)/shard_map/pallas_call | solution.py:48
  57.9 1.2 fusion.18
  62.8 1.6 collective-permute-start.6
  64.4 2.1 collective-permute-done.6
  66.5 3.0 %collective-permute-start.7 = (f32[2,4,128]{2,1,0:T(4,128)S(1)}, f32[2,4,128]{2,1,0:T(4,128)S(1)}, u32[]{:S(2)}, u32[]{:S(2)}) collective-permute-start(f32[2,4,128]{2,1,0:T(4,128)S(1)} %maximum_select_fusion.3), channel_id=1, source_target_pairs={{0,2},{1,3},{2,0},{3,1},{4,6},{5,7},{6,4},{7,5},{8,10},{9,11},{10,... | collective-permute-start | bytes 12296 | tf_op jit(solution)/shard_map/ppermute | solution.py:74
  69.5 2.1 collective-permute-done.7
  71.6 1.9 collective-permute-start.8
  73.5 1.7 collective-permute-done.8
  75.3 3.9 %collective-permute-start.9 = (f32[8,4,128]{2,1,0:T(4,128)S(1)}, f32[8,4,128]{2,1,0:T(4,128)S(1)}, u32[]{:S(2)}, u32[]{:S(2)}) collective-permute-start(f32[8,4,128]{2,1,0:T(4,128)S(1)} %maximum_select_fusion.1), channel_id=1, source_target_pairs={{0,8},{1,9},{2,10},{3,11},{4,12},{5,13},{6,14},{7,15},{8,0},{9,1},... | collective-permute-start | bytes 49160 | tf_op jit(solution)/shard_map/ppermute | solution.py:74
  79.2 5.0 %all-to-all-start = ((bf16[16,1024,256]{2,1,0:T(8,128)(2,1)}), bf16[16,1024,256]{2,1,0:T(8,128)(2,1)}, u32[]{:S(2)}, u32[]{:S(2)}) async-start(bf16[16,1024,256]{2,1,0:T(8,128)(2,1)} %bitcast.66), calls=%async_computation | async-start | bytes 16777216 | tf_op jit(solution)/shard_map/all_to_all | solution.py:104
  84.2 0.0 all-gather.3.cloned.1.call-start
  84.3 0.1 rev.13
  84.4 0.1 rev.12
  85.8 0.1 fusion.36
  85.9 0.2 convolution_add_fusion
  86.1 0.7 pad_maximum_fusion
  86.8 0.0 all-gather.3.cloned.1.call-update
  86.8 0.1 dynamic-slice_convert_fusion
  86.9 0.1 broadcast_in_dim.23
  87.0 0.1 dynamic-slice_reduce_fusion
  87.1 120.2 %all-gather.3.cloned.1.call-done = f32[6144,128]{1,0:T(8,128)} async-done(((f32[384,128]{1,0:T(8,128)}), f32[6144,128]{1,0:T(8,128)}) %all-gather.3.cloned.1.call-update) | async-done | bytes 3145744 | tf_op jit(solution)/shard_map/all_gather | solution.py:151
  207.3 1.3 slice.1022
  208.6 1.2 fusion.14
  209.9 0.9 copy.12.a_ref
  210.8 36.4 %shard_map.69 = f32[8,128,128]{2,1,0:T(8,128)} custom-call(f32[8,128,128]{2,1,0:T(8,128)} %copy.12.a_ref), custom_call_target="tpu_custom_call" | custom-call | flops 134217728 | bytes 1048576 | tf_op jit(solution)/shard_map/pallas_call | solution.py:48
  247.2 6.4 %fusion.8 = f32[1024,128,1]{1,0,2:T(8,128)S(1)} fusion(bf16[16,1024,256]{2,1,0:T(8,128)(2,1)} %all-to-all-done, bf16[1024,16]{0,1:T(8,128)(2,1)S(1)} %bitcast.73, f32[16,384,128]{2,1,0:T(8,128)} %bitcast.72), kind=kOutput, calls=%fused_computation.13 | convolution fusion | flops 1077936128 | bytes 9994240 | tf_op jit(solution)/shard_map/dot_general | solution.py:161
  253.7 1.2 fusion.66
  254.9 0.2 fusion.16
  255.1 5.7 %multiply_reduce_fusion = f32[1024]{0:T(1024)S(1)} fusion(bf16[16,1024,256]{2,1,0:T(8,128)(2,1)} %all-to-all-done, bf16[1024,16]{0,1:T(8,128)(2,1)S(1)} %bitcast.74), kind=kLoop, calls=%fused_computation | loop fusion | flops 16776192 | bytes 8425472 | tf_op jit(solution)/shard_map/reduce_sum | solution.py:160
  260.8 0.7 bitcast_divide_fusion
  (365 shorter events, 3.8 us)
Async XLA Ops:
  11.0 14.0 %slice-start = ((s8[8388608]{0:T(1024)(128)(4,1)}), s8[4194304]{0:T(1024)(128)(4,1)S(1)}, s32[]{:S(2)}) async-start(s8[8388608]{0:T(1024)(128)(4,1)} %bitcast.67), calls=%async_computation.2 | async-start | bytes 8388608
  22.5 2.5 slice-start.1
  24.9 10.8 %copy-start.2 = (f32[256,128]{1,0:T(8,128)S(1)}, f32[256,128]{1,0:T(8,128)}, u32[]{:S(2)}) copy-start(f32[256,128]{1,0:T(8,128)} %param.8) | copy-start | bytes 393220
  24.9 2.2 collective-permute-start.3
  26.6 8.3 %collective-permute-start = (f32[256,128]{0,1:T(8,128)S(1)}, f32[256,128]{0,1:T(8,128)S(1)}, u32[]{:S(2)}, u32[]{:S(2)}) collective-permute-start(f32[256,128]{0,1:T(8,128)S(1)} %convolution_bitcast_fusion), channel_id=1, source_target_pairs={{0,16},{16,0},{32,48},{48,32},{64,80},{80,64},{96,112},{112,96},{1... | collective-permute-start | bytes 393224 | tf_op jit(solution)/shard_map/ppermute | solution.py:63
  27.2 4.3 %collective-permute-start.4 = (f32[128,128]{1,0:T(8,128)S(1)}, f32[128,128]{1,0:T(8,128)S(1)}, u32[]{:S(2)}, u32[]{:S(2)}) collective-permute-start(f32[128,128]{1,0:T(8,128)S(1)} %fusion.73), channel_id=1, source_target_pairs={{0,32},{16,48},{32,0},{48,16},{64,96},{80,112},{96,64},{112,80},{1... | collective-permute-start | bytes 196616 | tf_op jit(solution)/shard_map/ppermute | solution.py:63
  31.5 9.7 %collective-permute-start.5 = (f32[128,128]{1,0:T(8,128)S(1)}, f32[128,128]{1,0:T(8,128)S(1)}, u32[]{:S(2)}, u32[]{:S(2)}) collective-permute-start(f32[128,128]{1,0:T(8,128)S(1)} %add.509), channel_id=1, source_target_pairs={{0,64},{16,80},{32,96},{48,112},{64,0},{80,16},{96,32},{112,48},{1... | collective-permute-start | bytes 196616 | tf_op jit(solution)/shard_map/ppermute | solution.py:63
  34.9 5.0 %collective-permute-start.1 = (f32[256,128]{0,1:T(8,128)S(1)}, f32[256,128]{0,1:T(8,128)S(1)}, u32[]{:S(2)}, u32[]{:S(2)}) collective-permute-start(f32[256,128]{0,1:T(8,128)S(1)} %add.503), channel_id=1, source_target_pairs={{0,32},{16,48},{32,0},{48,16},{64,96},{80,112},{96,64},{112,80},{1... | collective-permute-start | bytes 393224 | tf_op jit(solution)/shard_map/ppermute | solution.py:63
  40.0 17.9 %collective-permute-start.2 = (f32[256,128]{0,1:T(8,128)S(1)}, f32[256,128]{0,1:T(8,128)S(1)}, u32[]{:S(2)}, u32[]{:S(2)}) collective-permute-start(f32[256,128]{0,1:T(8,128)S(1)} %add.504), channel_id=1, source_target_pairs={{0,64},{16,80},{32,96},{48,112},{64,0},{80,16},{96,32},{112,48},{1... | collective-permute-start | bytes 393224 | tf_op jit(solution)/shard_map/ppermute | solution.py:63
  62.8 3.7 %collective-permute-start.6 = (f32[1,4,128]{2,1,0:T(4,128)S(1)}, f32[1,4,128]{2,1,0:T(4,128)S(1)}, u32[]{:S(2)}, u32[]{:S(2)}) collective-permute-start(f32[1,4,128]{2,1,0:T(4,128)S(1)} %maximum_bitcast_fusion), channel_id=1, source_target_pairs={{0,1},{1,0},{2,3},{3,2},{4,5},{5,4},{6,7},{7,6},{8,9},{9,8},{10,11... | collective-permute-start | bytes 6152 | tf_op jit(solution)/shard_map/ppermute | solution.py:74
  66.5 5.1 %collective-permute-start.7 = (f32[2,4,128]{2,1,0:T(4,128)S(1)}, f32[2,4,128]{2,1,0:T(4,128)S(1)}, u32[]{:S(2)}, u32[]{:S(2)}) collective-permute-start(f32[2,4,128]{2,1,0:T(4,128)S(1)} %maximum_select_fusion.3), channel_id=1, source_target_pairs={{0,2},{1,3},{2,0},{3,1},{4,6},{5,7},{6,4},{7,5},{8,10},{9,11},{10,... | collective-permute-start | bytes 12296 | tf_op jit(solution)/shard_map/ppermute | solution.py:74
  71.6 3.7 %collective-permute-start.8 = (f32[4,4,128]{2,1,0:T(4,128)S(1)}, f32[4,4,128]{2,1,0:T(4,128)S(1)}, u32[]{:S(2)}, u32[]{:S(2)}) collective-permute-start(f32[4,4,128]{2,1,0:T(4,128)S(1)} %maximum_select_fusion.2), channel_id=1, source_target_pairs={{0,4},{1,5},{2,6},{3,7},{4,0},{5,1},{6,2},{7,3},{8,12},{9,13},{10,... | collective-permute-start | bytes 24584 | tf_op jit(solution)/shard_map/ppermute | solution.py:74
  75.3 9.2 %collective-permute-start.9 = (f32[8,4,128]{2,1,0:T(4,128)S(1)}, f32[8,4,128]{2,1,0:T(4,128)S(1)}, u32[]{:S(2)}, u32[]{:S(2)}) collective-permute-start(f32[8,4,128]{2,1,0:T(4,128)S(1)} %maximum_select_fusion.1), channel_id=1, source_target_pairs={{0,8},{1,9},{2,10},{3,11},{4,12},{5,13},{6,14},{7,15},{8,0},{9,1},... | collective-permute-start | bytes 49160 | tf_op jit(solution)/shard_map/ppermute | solution.py:74
  79.2 6.7 %copy-start.3 = (f32[1,128,128]{2,1,0:T(8,128)S(1)}, f32[1,128,128]{2,1,0:T(8,128)}, u32[]{:S(2)}) copy-start(f32[1,128,128]{2,1,0:T(8,128)} %shard_map.68) | copy-start | bytes 196612
  79.2 168.0 %all-to-all-start = ((bf16[16,1024,256]{2,1,0:T(8,128)(2,1)}), bf16[16,1024,256]{2,1,0:T(8,128)(2,1)}, u32[]{:S(2)}, u32[]{:S(2)}) async-start(bf16[16,1024,256]{2,1,0:T(8,128)(2,1)} %bitcast.66), calls=%async_computation | async-start | bytes 16777216 | tf_op jit(solution)/shard_map/all_to_all | solution.py:104
  84.2 123.1 %all-gather.3.cloned.1.call-start = ((), (), s32[]{:S(2)}) async-start(), calls=%async_computation.1 | async-start | bytes 3342336 | tf_op jit(solution)/shard_map/all_gather | solution.py:151
  247.2 6.5 %copy-start.1 = (f32[8,128,128]{2,1,0:T(8,128)S(1)}, f32[8,128,128]{2,1,0:T(8,128)}, u32[]{:S(2)}) copy-start(f32[8,128,128]{2,1,0:T(8,128)} %shard_map.69) | copy-start | bytes 1572868
  254.9 6.6 %copy-start = (f32[8,128,128]{2,1,0:T(8,128)}, f32[8,128,128]{2,1,0:T(8,128)S(1)}, u32[]{:S(2)}) copy-start(f32[8,128,128]{2,1,0:T(8,128)S(1)} %fusion.66) | copy-start | bytes 1572868
Sparse Core Ops, SparseCore 0:
  87.7 119.5 all-gather.2
